TPU v7x, 512 devices: a whole 4x4x16 slice. The times are simulated.
512 devices in a mesh: segment: 8 (over y_hi, x), dp: 64 (over y_lo, z, core).
Axes of the slice: x: 4, y: 4 (y_hi: 2, y_lo: 2; y = y_hi * 2 + y_lo), z: 16, core: 2. Of those that a mesh axis runs over, the one named last changes fastest.
Arguments:
- acts: bfloat16 [8, 128, 4, 8, 8, 128], P('segment', 'dp'), may hold values from -6 to 6
- weights: bfloat16 [8, 3456, 128], P('segment', 'dp'), may hold values from -0.109375 to 0.109375
- pos_weight: float32 [8, 3, 128], P('segment'), may hold values from -4 to 4
- anchors: int32 [128, 3], P('dp'), may hold values from 0 to 1983
- top_grad: bfloat16 [128, 4, 8, 8, 128], P('dp'), may hold values from -6 to 6
Outputs:
- section_grads: bfloat16 [8, 128, 4, 8, 8, 128], P('segment', 'dp')
- weight_grad: float32 [8, 3456, 128], P('segment', 'dp')
Inputs may be any that keep to these rules, and one draw needn't show every extreme that they name: `anchors`: mesh coordinates of each crop's corner.
All inputs are finite; a program needn't handle non-finite values.
Results may differ from a plain program's by a relative error of at most 0.015.
Values may be sent and summed in bfloat16 or wider, within the bound.
No kernel may reach another device: no remote copies, remote signals or barrier semaphores. Data moves between devices by JAX's collectives and lax.ppermute only.
A program may use at most 64 MiB of HBM per device.

v0:
```python
import math

import jax
import jax.numpy as jnp
from jax import lax
from jax.sharding import PartitionSpec as P

STRIDE = 2
WAVE = 64


def passed_along(array, axis, by):
    length = lax.axis_size(axis)
    pairs = [(i, i + by) for i in range(length) if 0 <= i + by < length]
    return lax.ppermute(array, axis, pairs)


def apply_taps(field, kernel_taps):
    size_x, size_y, size_z, channels = field.shape
    padded = jnp.pad(field, ((1, 1), (1, 1), (1, 1), (0, 0)))
    summed = jnp.zeros((size_x * size_y * size_z, kernel_taps.shape[2]), jnp.float32)
    tap_index = 0
    for first in range(3):
        for second in range(3):
            for third in range(3):
                window_rows = padded[
                    first : first + size_x, second : second + size_y, third : third + size_z
                ].reshape(size_x * size_y * size_z, channels)
                summed = summed + jnp.dot(
                    window_rows, kernel_taps[tap_index], preferred_element_type=jnp.float32
                )
                tap_index += 1
    return summed


def tap_grads(field, slope):
    size_x, size_y, size_z, channels = field.shape
    padded = jnp.pad(field, ((1, 1), (1, 1), (1, 1), (0, 0)))
    blocks = []
    for first in range(3):
        for second in range(3):
            for third in range(3):
                window_rows = padded[
                    first : first + size_x, second : second + size_y, third : third + size_z
                ].reshape(size_x * size_y * size_z, channels)
                blocks.append(jnp.dot(window_rows.T, slope, preferred_element_type=jnp.float32))
    return jnp.concatenate(blocks, axis=0)


def position_term(anchor, pos_gain, size_x, size_y, size_z):
    phases = []
    for axis_num, axis_len in enumerate((size_x, size_y, size_z)):
        coords = anchor[axis_num] + STRIDE * jnp.arange(axis_len, dtype=jnp.int32)
        phase_val = (coords % WAVE).astype(jnp.float32)
        phases.append(jnp.sin(phase_val * (2.0 * math.pi / WAVE)))
    position_sum = (
        phases[0][:, None, None, None] * pos_gain[0]
        + phases[1][None, :, None, None] * pos_gain[1]
        + phases[2][None, None, :, None] * pos_gain[2]
    )
    return position_sum.reshape(size_x * size_y * size_z, pos_gain.shape[1])


def layer_slope(incoming_rows, pre_act):
    sigmoid_h = jax.nn.sigmoid(pre_act)
    silu_slope = sigmoid_h * (1.0 + pre_act * (1.0 - sigmoid_h))
    return (incoming_rows * silu_slope).astype(jnp.bfloat16)


def local(acts, weights, pos_weight, anchors, top_grad):
    segments = lax.axis_size("segment")
    dp_count = lax.axis_size("dp")
    segment_index = lax.axis_index("segment")
    gathered = lax.all_gather(weights[0], "dp", axis=0, tiled=True)
    channels = gathered.shape[1]
    kernel_taps = gathered.reshape(-1, channels, channels)
    flipped = jnp.transpose(jnp.flip(kernel_taps, 0), (0, 2, 1))
    inputs_local = acts[0]
    micro_count = inputs_local.shape[0]
    size_x, size_y, size_z = (inputs_local.shape[1], inputs_local.shape[2], inputs_local.shape[3])
    cell_count = size_x * size_y * size_z
    rows_local = weights.shape[1]
    pos_gain = pos_weight[0]
    position_all = jnp.stack(
        [
            position_term(anchors[micro], pos_gain, size_x, size_y, size_z)
            for micro in range(micro_count)
        ]
    )
    tick_count = segments + micro_count - 1
    scale_factor = 1.0 / math.sqrt(dp_count * micro_count * cell_count)

    def tick_step(step_num, carry):
        incoming, grads_held, slopes_held, accumulated = carry
        micro_index = step_num - (segments - 1 - segment_index)
        active = (micro_index >= 0) & (micro_index < micro_count)
        slot_index = jnp.clip(micro_index, 0, micro_count - 1)

        def busy_work(operands):
            incoming_in, grads_in, slopes_in = operands
            top_slice = lax.dynamic_index_in_dim(top_grad, slot_index, 0, keepdims=False)
            cotangent = jnp.where(segment_index == segments - 1, top_slice, incoming_in)
            field = lax.dynamic_index_in_dim(inputs_local, slot_index, 0, keepdims=False)
            pre_act = apply_taps(field, kernel_taps) + lax.dynamic_index_in_dim(
                position_all, slot_index, 0, keepdims=False
            )
            incoming_rows = cotangent.reshape(cell_count, channels).astype(jnp.float32)
            slope = layer_slope(incoming_rows, pre_act)
            down_grad = (
                incoming_rows + apply_taps(slope.reshape(size_x, size_y, size_z, channels), flipped)
            ).astype(jnp.bfloat16)
            down_grad = down_grad.reshape(size_x, size_y, size_z, channels)
            grads_out = lax.dynamic_update_index_in_dim(grads_in, down_grad, slot_index, 0)
            slopes_out = lax.dynamic_update_index_in_dim(slopes_in, slope, slot_index, 0)
            grad_term = jnp.zeros((1, channels), jnp.float32)
            return (down_grad, grads_out, slopes_out, grad_term)

        def quiet_work(operands):
            incoming_in, grads_in, slopes_in = operands
            grad_term = jnp.zeros((1, channels), jnp.float32)
            return (jnp.zeros_like(incoming_in), grads_in, slopes_in, grad_term)

        down_grad, grads_held, slopes_held, grad_term = lax.cond(
            active, busy_work, quiet_work, (incoming, grads_held, slopes_held)
        )
        incoming = passed_along(down_grad, "segment", -1)
        return (incoming, grads_held, slopes_held, accumulated)

    start_carry = (
        jnp.zeros((size_x, size_y, size_z, channels), jnp.bfloat16),
        jnp.zeros(inputs_local.shape, jnp.bfloat16),
        jnp.zeros((micro_count, cell_count, channels), jnp.bfloat16),
        jnp.zeros((rows_local, channels), jnp.float32),
    )
    incoming, grads_held, slopes_held, accumulated = lax.fori_loop(
        0, tick_count, tick_step, start_carry
    )
    grad_term = tap_grads(inputs_local[0], slopes_held[0])
    micro = 1
    grad_term = grad_term + tap_grads(inputs_local[micro], slopes_held[micro])
    reduced = lax.psum_scatter(grad_term, "dp", scatter_dimension=0, tiled=True)
    return (grads_held[None], (reduced * scale_factor)[None])


def solution(mesh):
    return jax.shard_map(
        local,
        mesh=mesh,
        in_specs=(
            P("segment", "dp", None, None, None, None),
            P("segment", "dp", None),
            P("segment", None, None),
            P("dp", None),
            P("dp", None, None, None, None),
        ),
        out_specs=(P("segment", "dp", None, None, None, None), P("segment", "dp", None)),
        check_vma=False,
    )
```

profile of v0, /device:TPU:1, one launch (start us, length us, event | category | flops | bytes accessed | tf_op | source)
XLA Modules:
  0.0 428.4 jit_solution(7778404728182434695)
XLA Ops:
  0.6 1.6 fusion.250
  5.3 75.9 %all-gather = bf16[1,3456,128]{2,0,1:T(2,128)(2,1)S(1)} all-gather(bf16[1,54,128]{2,0,1:T(2,128)(2,1)S(1)} %copy.12), channel_id=2, replica_groups=mesh['segment'=8,'dp'=64] {'dp'}, dimensions={1}, use_global_device_ids=true | all-gather | bytes 898560 | tf_op jit(solution)/shard_map/all_gather | solution.py:74
  89.9 157.1 %while.18 = (s32[]{:T(128)}, bf16[4,8,8,128]{3,2,1,0:T(8,128)(2,1)S(1)}, bf16[2,4,8,8,128]{4,3,2,1,0:T(8,128)(2,1)}, bf16[2,256,128]{2,1,0:T(8,128)(2,1)S(1)}, s...) while((s32[]{:T(128)}, ...), condition=%wide.region_3.4_spmd, body=%wide.region_0.3_spmd.sunk | while | flops 455180288 | bytes 23921024 | solution.py:135
  91.9 4.3 %collective-permute-done = bf16[4,8,8,128]{3,2,1,0:T(8,128)(2,1)S(1)} collective-permute-done((bf16[4,8,8,128]{3,2,1,0:T(8,128)(2,1)}, bf16[4,8,8,128]{3,2,1,0:T(8,128)(2,1)S(1)}, u32[]{:S(2)}, u32[]{:S(2)}) %collective-permute-start) | collective-permute-done | bytes 65568 | tf_op jit(solution)/shard_map/while/body/eval_jaxpr/ppermute | solution.py:15
  98.2 3.9 collective-permute-done
  104.1 3.9 collective-permute-done
  109.9 6.5 %collective-permute-done = bf16[4,8,8,128]{3,2,1,0:T(8,128)(2,1)S(1)} collective-permute-done((bf16[4,8,8,128]{3,2,1,0:T(8,128)(2,1)}, bf16[4,8,8,128]{3,2,1,0:T(8,128)(2,1)S(1)}, u32[]{:S(2)}, u32[]{:S(2)}) %collective-permute-start) | collective-permute-done | bytes 65568 | tf_op jit(solution)/shard_map/while/body/eval_jaxpr/ppermute | solution.py:15
  118.4 7.5 %collective-permute-done = bf16[4,8,8,128]{3,2,1,0:T(8,128)(2,1)S(1)} collective-permute-done((bf16[4,8,8,128]{3,2,1,0:T(8,128)(2,1)}, bf16[4,8,8,128]{3,2,1,0:T(8,128)(2,1)S(1)}, u32[]{:S(2)}, u32[]{:S(2)}) %collective-permute-start) | collective-permute-done | bytes 65568 | tf_op jit(solution)/shard_map/while/body/eval_jaxpr/ppermute | solution.py:15
  127.8 7.5 %collective-permute-done = bf16[4,8,8,128]{3,2,1,0:T(8,128)(2,1)S(1)} collective-permute-done((bf16[4,8,8,128]{3,2,1,0:T(8,128)(2,1)}, bf16[4,8,8,128]{3,2,1,0:T(8,128)(2,1)S(1)}, u32[]{:S(2)}, u32[]{:S(2)}) %collective-permute-start) | collective-permute-done | bytes 65568 | tf_op jit(solution)/shard_map/while/body/eval_jaxpr/ppermute | solution.py:15
  137.3 71.9 %collective-permute-done = bf16[4,8,8,128]{3,2,1,0:T(8,128)(2,1)S(1)} collective-permute-done((bf16[4,8,8,128]{3,2,1,0:T(8,128)(2,1)}, bf16[4,8,8,128]{3,2,1,0:T(8,128)(2,1)S(1)}, u32[]{:S(2)}, u32[]{:S(2)}) %collective-permute-start) | collective-permute-done | bytes 65568 | tf_op jit(solution)/shard_map/while/body/eval_jaxpr/ppermute | solution.py:15
  209.2 11.9 %conditional.2 = (bf16[4,8,8,128]{3,2,1,0:T(8,128)(2,1)}, bf16[2,4,8,8,128]{4,3,2,1,0:T(8,128)(2,1)}, bf16[2,256,128]{2,1,0:T(8,128)(2,1)S(1)}) conditional(s32[]{:T(128)} %convert_element_type.107, (bf16[2,4,8,8,128]{4,3,2,1,0:T(8,128)(2,1)}, bf16[2,256,128]{2,1,0:T(8,128)(2,1)S(1)}) %tuple.170, (s32[]{:T(128)}, s32[]{:T(128)}, ...), branch_computations={%region_1.1_spmd, %region_2.2_spmd} | conditional | flops 455180288 | bytes 23658574 | solution.py:123
  219.6 1.5 constant_dynamic-update-slice_fusion
  222.4 7.5 %collective-permute-done = bf16[4,8,8,128]{3,2,1,0:T(8,128)(2,1)S(1)} collective-permute-done((bf16[4,8,8,128]{3,2,1,0:T(8,128)(2,1)}, bf16[4,8,8,128]{3,2,1,0:T(8,128)(2,1)S(1)}, u32[]{:S(2)}, u32[]{:S(2)}) %collective-permute-start) | collective-permute-done | bytes 65568 | tf_op jit(solution)/shard_map/while/body/eval_jaxpr/ppermute | solution.py:15
  229.9 11.9 %conditional.2 = (bf16[4,8,8,128]{3,2,1,0:T(8,128)(2,1)}, bf16[2,4,8,8,128]{4,3,2,1,0:T(8,128)(2,1)}, bf16[2,256,128]{2,1,0:T(8,128)(2,1)S(1)}) conditional(s32[]{:T(128)} %convert_element_type.107, (bf16[2,4,8,8,128]{4,3,2,1,0:T(8,128)(2,1)}, bf16[2,256,128]{2,1,0:T(8,128)(2,1)S(1)}) %tuple.170, (s32[]{:T(128)}, s32[]{:T(128)}, ...), branch_computations={%region_1.1_spmd, %region_2.2_spmd} | conditional | flops 455180288 | bytes 23658574 | solution.py:123
  243.2 3.9 collective-permute-done
  258.7 122.4 %fusion = f32[64,128]{1,0:T(8,128)S(1)} fusion(f32[3456,128]{1,0:T(8,128)S(1)} %add.436), kind=kCustom, calls=%all-reduce-scatter | all-reduce-scatter fusion | flops 524289 | bytes 1804288
  385.0 11.3 %collective-permute-start.6 = (f32[64,128]{1,0:T(8,128)S(1)}, f32[64,128]{1,0:T(8,128)S(1)}, u32[]{:S(2)}, u32[]{:S(2)}) collective-permute-start(f32[64,128]{1,0:T(8,128)S(1)} %fusion), channel_id=1, source_target_pairs={{0,6},{1,7},{2,8},{3,9},{4,10},{5,11},{6,12},{7,13},{8,14},{9,15},... | collective-permute-start | bytes 98312
  396.3 6.0 %collective-permute-start.10 = (f32[54,128]{1,0:T(8,128)S(1)}, f32[54,128]{1,0:T(8,128)S(1)}, u32[]{:S(2)}, u32[]{:S(2)}) collective-permute-start(f32[54,128]{1,0:T(8,128)S(1)} %slice.604), channel_id=1, source_target_pairs={{0,10},{1,11},{2,12},{3,13},{4,14},{5,15},{6,16},{7,17},{8,18},{9,... | collective-permute-start | bytes 82952
  402.2 1.7 collective-permute-done.10
  404.0 2.0 collective-permute-start.5
  406.0 9.6 %collective-permute-start.4 = (f32[64,128]{1,0:T(8,128)S(1)}, f32[64,128]{1,0:T(8,128)S(1)}, u32[]{:S(2)}, u32[]{:S(2)}) collective-permute-start(f32[64,128]{1,0:T(8,128)S(1)} %fusion), channel_id=1, source_target_pairs={{0,4},{1,5},{2,6},{3,7},{4,8},{5,9},{6,10},{7,11},{8,12},{9,13},{1... | collective-permute-start | bytes 98312
  416.9 3.1 collective-permute-start.2
  420.1 4.0 collective-permute-start.1
  426.1 1.7 concatenate.8
  (346 shorter events, 72.0 us)
Async XLA Ops:
  89.9 158.1 %copy-start.42 = (bf16[4,8,8,128]{3,2,1,0:T(8,128)(2,1)S(1)}, bf16[4,8,8,128]{3,2,1,0:T(8,128)(2,1)}, u32[]{:S(2)}) copy-start(bf16[4,8,8,128]{3,2,1,0:T(8,128)(2,1)} %get-tuple-element.394) | copy-start | bytes 196612
  89.9 158.3 %copy-start.41 = (bf16[4,8,8,128]{3,2,1,0:T(8,128)(2,1)S(1)}, bf16[4,8,8,128]{3,2,1,0:T(8,128)(2,1)}, u32[]{:S(2)}) copy-start(bf16[4,8,8,128]{3,2,1,0:T(8,128)(2,1)} %get-tuple-element.395) | copy-start | bytes 196612
  89.9 158.5 %copy-start.40 = (bf16[4,8,8,128]{3,2,1,0:T(8,128)(2,1)S(1)}, bf16[4,8,8,128]{3,2,1,0:T(8,128)(2,1)}, u32[]{:S(2)}) copy-start(bf16[4,8,8,128]{3,2,1,0:T(8,128)(2,1)} %get-tuple-element.396) | copy-start | bytes 196612
  89.9 158.7 %copy-start.39 = (bf16[4,8,8,128]{3,2,1,0:T(8,128)(2,1)S(1)}, bf16[4,8,8,128]{3,2,1,0:T(8,128)(2,1)}, u32[]{:S(2)}) copy-start(bf16[4,8,8,128]{3,2,1,0:T(8,128)(2,1)} %get-tuple-element.397) | copy-start | bytes 196612
  89.9 158.9 %copy-start.38 = (bf16[4,8,8,128]{3,2,1,0:T(8,128)(2,1)S(1)}, bf16[4,8,8,128]{3,2,1,0:T(8,128)(2,1)}, u32[]{:S(2)}) copy-start(bf16[4,8,8,128]{3,2,1,0:T(8,128)(2,1)} %get-tuple-element.398) | copy-start | bytes 196612
  90.6 5.6 %collective-permute-start = (bf16[4,8,8,128]{3,2,1,0:T(8,128)(2,1)}, bf16[4,8,8,128]{3,2,1,0:T(8,128)(2,1)S(1)}, u32[]{:S(2)}, u32[]{:S(2)}) collective-permute-start(bf16[4,8,8,128]{3,2,1,0:T(8,128)(2,1)} %get-tuple-element.513), channel_id=1, source_target_pairs={{64,0},{128,64},{192,128},{256,192},{320,256},{384,320},{448,384},... | collective-permute-start | bytes 196616 | tf_op jit(solution)/shard_map/while/body/eval_jaxpr/ppermute | solution.py:15
  96.9 5.2 %collective-permute-start = (bf16[4,8,8,128]{3,2,1,0:T(8,128)(2,1)}, bf16[4,8,8,128]{3,2,1,0:T(8,128)(2,1)S(1)}, u32[]{:S(2)}, u32[]{:S(2)}) collective-permute-start(bf16[4,8,8,128]{3,2,1,0:T(8,128)(2,1)} %get-tuple-element.513), channel_id=1, source_target_pairs={{64,0},{128,64},{192,128},{256,192},{320,256},{384,320},{448,384},... | collective-permute-start | bytes 196616 | tf_op jit(solution)/shard_map/while/body/eval_jaxpr/ppermute | solution.py:15
  102.8 5.2 %collective-permute-start = (bf16[4,8,8,128]{3,2,1,0:T(8,128)(2,1)}, bf16[4,8,8,128]{3,2,1,0:T(8,128)(2,1)S(1)}, u32[]{:S(2)}, u32[]{:S(2)}) collective-permute-start(bf16[4,8,8,128]{3,2,1,0:T(8,128)(2,1)} %get-tuple-element.513), channel_id=1, source_target_pairs={{64,0},{128,64},{192,128},{256,192},{320,256},{384,320},{448,384},... | collective-permute-start | bytes 196616 | tf_op jit(solution)/shard_map/while/body/eval_jaxpr/ppermute | solution.py:15
  108.6 7.8 %collective-permute-start = (bf16[4,8,8,128]{3,2,1,0:T(8,128)(2,1)}, bf16[4,8,8,128]{3,2,1,0:T(8,128)(2,1)S(1)}, u32[]{:S(2)}, u32[]{:S(2)}) collective-permute-start(bf16[4,8,8,128]{3,2,1,0:T(8,128)(2,1)} %get-tuple-element.513), channel_id=1, source_target_pairs={{64,0},{128,64},{192,128},{256,192},{320,256},{384,320},{448,384},... | collective-permute-start | bytes 196616 | tf_op jit(solution)/shard_map/while/body/eval_jaxpr/ppermute | solution.py:15
  117.1 8.8 %collective-permute-start = (bf16[4,8,8,128]{3,2,1,0:T(8,128)(2,1)}, bf16[4,8,8,128]{3,2,1,0:T(8,128)(2,1)S(1)}, u32[]{:S(2)}, u32[]{:S(2)}) collective-permute-start(bf16[4,8,8,128]{3,2,1,0:T(8,128)(2,1)} %get-tuple-element.513), channel_id=1, source_target_pairs={{64,0},{128,64},{192,128},{256,192},{320,256},{384,320},{448,384},... | collective-permute-start | bytes 196616 | tf_op jit(solution)/shard_map/while/body/eval_jaxpr/ppermute | solution.py:15
  126.5 8.8 %collective-permute-start = (bf16[4,8,8,128]{3,2,1,0:T(8,128)(2,1)}, bf16[4,8,8,128]{3,2,1,0:T(8,128)(2,1)S(1)}, u32[]{:S(2)}, u32[]{:S(2)}) collective-permute-start(bf16[4,8,8,128]{3,2,1,0:T(8,128)(2,1)} %get-tuple-element.513), channel_id=1, source_target_pairs={{64,0},{128,64},{192,128},{256,192},{320,256},{384,320},{448,384},... | collective-permute-start | bytes 196616 | tf_op jit(solution)/shard_map/while/body/eval_jaxpr/ppermute | solution.py:15
  136.0 73.2 %collective-permute-start = (bf16[4,8,8,128]{3,2,1,0:T(8,128)(2,1)}, bf16[4,8,8,128]{3,2,1,0:T(8,128)(2,1)S(1)}, u32[]{:S(2)}, u32[]{:S(2)}) collective-permute-start(bf16[4,8,8,128]{3,2,1,0:T(8,128)(2,1)} %get-tuple-element.513), channel_id=1, source_target_pairs={{64,0},{128,64},{192,128},{256,192},{320,256},{384,320},{448,384},... | collective-permute-start | bytes 196616 | tf_op jit(solution)/shard_map/while/body/eval_jaxpr/ppermute | solution.py:15
  221.1 8.8 %collective-permute-start = (bf16[4,8,8,128]{3,2,1,0:T(8,128)(2,1)}, bf16[4,8,8,128]{3,2,1,0:T(8,128)(2,1)S(1)}, u32[]{:S(2)}, u32[]{:S(2)}) collective-permute-start(bf16[4,8,8,128]{3,2,1,0:T(8,128)(2,1)} %get-tuple-element.513), channel_id=1, source_target_pairs={{64,0},{128,64},{192,128},{256,192},{320,256},{384,320},{448,384},... | collective-permute-start | bytes 196616 | tf_op jit(solution)/shard_map/while/body/eval_jaxpr/ppermute | solution.py:15
  241.9 5.2 %collective-permute-start = (bf16[4,8,8,128]{3,2,1,0:T(8,128)(2,1)}, bf16[4,8,8,128]{3,2,1,0:T(8,128)(2,1)S(1)}, u32[]{:S(2)}, u32[]{:S(2)}) collective-permute-start(bf16[4,8,8,128]{3,2,1,0:T(8,128)(2,1)} %get-tuple-element.513), channel_id=1, source_target_pairs={{64,0},{128,64},{192,128},{256,192},{320,256},{384,320},{448,384},... | collective-permute-start | bytes 196616 | tf_op jit(solution)/shard_map/while/body/eval_jaxpr/ppermute | solution.py:15
  381.1 24.9 %collective-permute-start.9 = (f32[64,128]{1,0:T(8,128)S(1)}, f32[64,128]{1,0:T(8,128)S(1)}, u32[]{:S(2)}, u32[]{:S(2)}) collective-permute-start(f32[64,128]{1,0:T(8,128)S(1)} %fusion), channel_id=1, source_target_pairs={{0,9},{1,10},{2,11},{3,12},{4,13},{5,14},{6,15},{7,16},{8,17},{9,1... | collective-permute-start | bytes 98312
  382.4 33.2 %collective-permute-start.8 = (f32[64,128]{1,0:T(8,128)S(1)}, f32[64,128]{1,0:T(8,128)S(1)}, u32[]{:S(2)}, u32[]{:S(2)}) collective-permute-start(f32[64,128]{1,0:T(8,128)S(1)} %fusion), channel_id=1, source_target_pairs={{0,8},{1,9},{2,10},{3,11},{4,12},{5,13},{6,14},{7,15},{8,16},{9,17... | collective-permute-start | bytes 98312
  383.7 33.3 %collective-permute-start.7 = (f32[64,128]{1,0:T(8,128)S(1)}, f32[64,128]{1,0:T(8,128)S(1)}, u32[]{:S(2)}, u32[]{:S(2)}) collective-permute-start(f32[64,128]{1,0:T(8,128)S(1)} %fusion), channel_id=1, source_target_pairs={{0,7},{1,8},{2,9},{3,10},{4,11},{5,12},{6,13},{7,14},{8,15},{9,16}... | collective-permute-start | bytes 98312
  385.0 35.1 %collective-permute-start.6 = (f32[64,128]{1,0:T(8,128)S(1)}, f32[64,128]{1,0:T(8,128)S(1)}, u32[]{:S(2)}, u32[]{:S(2)}) collective-permute-start(f32[64,128]{1,0:T(8,128)S(1)} %fusion), channel_id=1, source_target_pairs={{0,6},{1,7},{2,8},{3,9},{4,10},{5,11},{6,12},{7,13},{8,14},{9,15},... | collective-permute-start | bytes 98312
  396.3 7.7 %collective-permute-start.10 = (f32[54,128]{1,0:T(8,128)S(1)}, f32[54,128]{1,0:T(8,128)S(1)}, u32[]{:S(2)}, u32[]{:S(2)}) collective-permute-start(f32[54,128]{1,0:T(8,128)S(1)} %slice.604), channel_id=1, source_target_pairs={{0,10},{1,11},{2,12},{3,13},{4,14},{5,15},{6,16},{7,17},{8,18},{9,... | collective-permute-start | bytes 82952
  404.0 22.1 %collective-permute-start.5 = (f32[64,128]{1,0:T(8,128)S(1)}, f32[64,128]{1,0:T(8,128)S(1)}, u32[]{:S(2)}, u32[]{:S(2)}) collective-permute-start(f32[64,128]{1,0:T(8,128)S(1)} %fusion), channel_id=1, source_target_pairs={{0,5},{1,6},{2,7},{3,8},{4,9},{5,10},{6,11},{7,12},{8,13},{9,14},{... | collective-permute-start | bytes 98312
  406.0 20.1 %collective-permute-start.4 = (f32[64,128]{1,0:T(8,128)S(1)}, f32[64,128]{1,0:T(8,128)S(1)}, u32[]{:S(2)}, u32[]{:S(2)}) collective-permute-start(f32[64,128]{1,0:T(8,128)S(1)} %fusion), channel_id=1, source_target_pairs={{0,4},{1,5},{2,6},{3,7},{4,8},{5,9},{6,10},{7,11},{8,12},{9,13},{1... | collective-permute-start | bytes 98312
  415.6 10.4 %collective-permute-start.3 = (f32[64,128]{1,0:T(8,128)S(1)}, f32[64,128]{1,0:T(8,128)S(1)}, u32[]{:S(2)}, u32[]{:S(2)}) collective-permute-start(f32[64,128]{1,0:T(8,128)S(1)} %fusion), channel_id=1, source_target_pairs={{0,3},{1,4},{2,5},{3,6},{4,7},{5,8},{6,9},{7,10},{8,11},{9,12},{10... | collective-permute-start | bytes 98312
  416.9 9.1 %collective-permute-start.2 = (f32[64,128]{1,0:T(8,128)S(1)}, f32[64,128]{1,0:T(8,128)S(1)}, u32[]{:S(2)}, u32[]{:S(2)}) collective-permute-start(f32[64,128]{1,0:T(8,128)S(1)} %fusion), channel_id=1, source_target_pairs={{0,2},{1,3},{2,4},{3,5},{4,6},{5,7},{6,8},{7,9},{8,10},{9,11},{10,... | collective-permute-start | bytes 98312
  420.1 6.0 %collective-permute-start.1 = (f32[64,128]{1,0:T(8,128)S(1)}, f32[64,128]{1,0:T(8,128)S(1)}, u32[]{:S(2)}, u32[]{:S(2)}) collective-permute-start(f32[64,128]{1,0:T(8,128)S(1)} %fusion), channel_id=1, source_target_pairs={{0,1},{1,2},{2,3},{3,4},{4,5},{5,6},{6,7},{7,8},{8,9},{9,10},{10,1... | collective-permute-start | bytes 98312
  (47 other events, 780.0 us)
where the time goes:
time: 429 us; the launch traced here: 428 us
  blocking collectives  198 us (46%)
  waiting for transfers between devices  119 us (28%)
  starting transfers between devices  52.7 us (12%)
  matrix products  29.6 us (7%)
  local copies, waits for them, and re-layouts  20.6 us (5%)
  other arithmetic  5.32 us (1%)
    unnamed x1, blocking collectives  122 us
    ppermute x9, waiting for transfers between devices, passed_along(): return lax.ppermute(array, axis, pairs)  117 us
    all_gather x1, blocking collectives, local(): gathered = lax.all_gather(weights[0], 'dp', axis=0, tiled=True)  75.9 us
    unnamed x10, starting transfers between devices  41.2 us
    dot_general x108, matrix products, apply_taps(): jnp.dot(window_rows, kernel_taps[tap_index], preferred_element_type=jnp.f...  19.1 us
    ppermute x9, starting transfers between devices, passed_along(): return lax.ppermute(array, axis, pairs)  11.5 us
    dot_general x54, matrix products, tap_grads(): jnp.dot(window_rows.T, slope, preferred_element_type=jnp.float32)  10.4 us
  transfers between devices with their start and end apart: 19, of which 10 were waited for; matrix products, arithmetic and copies ran while one was open for 0% of the time, Pallas kernels for 0%

commit v1 on v0

v1 whole, which is shorter than its diff:
```python
import math

import jax
import jax.numpy as jnp
from jax import lax
from jax.sharding import PartitionSpec as P

STRIDE = 2
WAVE = 64


def passed_along(array, axis, by):
    length = lax.axis_size(axis)
    pairs = [(i, i + by) for i in range(length) if 0 <= i + by < length]
    return lax.ppermute(array, axis, pairs)


def conv_forward(field, kernel):
    return lax.conv_general_dilated(
        field, kernel, (1, 1, 1), [(1, 1)] * 3,
        dimension_numbers=("NDHWC", "DHWIO", "NDHWC"),
        preferred_element_type=jnp.float32,
    )


def conv_transposed(slope, kernel):
    flipped = jnp.flip(kernel, (0, 1, 2))
    return lax.conv_general_dilated(
        slope, flipped, (1, 1, 1), [(1, 1)] * 3,
        dimension_numbers=("NDHWC", "DHWOI", "NDHWC"),
        preferred_element_type=jnp.float32,
    )


def conv_kernel_grad(field, slope):
    return lax.conv_general_dilated(
        field, slope, (1, 1, 1), [(1, 1)] * 3,
        dimension_numbers=("CDHWN", "IDHWO", "DHWNC"),
        preferred_element_type=jnp.float32,
    )


def position_term(anchor, pos_gain, size_x, size_y, size_z):
    phases = []
    for axis_num, axis_len in enumerate((size_x, size_y, size_z)):
        coords = anchor[axis_num] + STRIDE * jnp.arange(axis_len, dtype=jnp.int32)
        phase_val = (coords % WAVE).astype(jnp.float32)
        phases.append(jnp.sin(phase_val * (2.0 * math.pi / WAVE)))
    return (
        phases[0][:, None, None, None] * pos_gain[0]
        + phases[1][None, :, None, None] * pos_gain[1]
        + phases[2][None, None, :, None] * pos_gain[2]
    )


def local(acts, weights, pos_weight, anchors, top_grad):
    segments = lax.axis_size("segment")
    dp_count = lax.axis_size("dp")
    segment_index = lax.axis_index("segment")
    channels = weights.shape[2]
    gathered = lax.all_gather(weights, "dp", axis=0, tiled=True)
    kernel = gathered.reshape(3, 3, 3, channels, channels)
    fields = acts[0]
    micro_count, size_x, size_y, size_z = fields.shape[:4]
    cell_count = size_x * size_y * size_z
    pos_gain = pos_weight[0]
    position_all = jnp.stack(
        [position_term(anchors[m], pos_gain, size_x, size_y, size_z) for m in range(micro_count)]
    )
    pre_act = conv_forward(fields, kernel) + position_all
    sigmoid_h = jax.nn.sigmoid(pre_act)
    silu_slope = sigmoid_h * (1.0 + pre_act * (1.0 - sigmoid_h))

    is_top = segment_index == segments - 1
    incoming = jnp.zeros(top_grad.shape, jnp.bfloat16)
    grads_held = jnp.zeros(top_grad.shape, jnp.bfloat16)
    slope_held = jnp.zeros(top_grad.shape, jnp.bfloat16)
    for tick in range(segments):
        cotangent = jnp.where(is_top, top_grad, incoming).astype(jnp.float32)
        slope = (cotangent * silu_slope).astype(jnp.bfloat16)
        down_grad = (cotangent + conv_transposed(slope, kernel)).astype(jnp.bfloat16)
        mine = segment_index == segments - 1 - tick
        grads_held = jnp.where(mine, down_grad, grads_held)
        slope_held = jnp.where(mine, slope, slope_held)
        if tick + 1 < segments:
            incoming = passed_along(down_grad, "segment", -1)

    grad_term = conv_kernel_grad(fields, slope_held).reshape(dp_count, -1, channels)
    reduced = lax.psum_scatter(grad_term, "dp", scatter_dimension=0, tiled=True)
    scale_factor = 1.0 / math.sqrt(dp_count * micro_count * cell_count)
    return (grads_held[None], reduced * scale_factor)


def solution(mesh):
    return jax.shard_map(
        local,
        mesh=mesh,
        in_specs=(
            P("segment", "dp", None, None, None, None),
            P("segment", "dp", None),
            P("segment", None, None),
            P("dp", None),
            P("dp", None, None, None, None),
        ),
        out_specs=(P("segment", "dp", None, None, None, None), P("segment", "dp", None)),
        check_vma=False,
    )
```

time: 429 us -> 407 us (0.949)
  the two profiles are of different devices: /device:TPU:1 before, /device:TPU:2 now
where the time goes in v1:
time: 407 us; the launch traced here: 406 us
  waiting for transfers between devices  271 us (67%)
  blocking collectives  72.5 us (18%)
  matrix products  22.1 us (5%)
  starting transfers between devices  15.2 us (4%)
  between operations  14.3 us (4%)
  local copies, waits for them, and re-layouts  6.39 us (2%)
  other arithmetic  5.23 us (1%)
    unnamed x2, waiting for transfers between devices  220 us
    all_gather x1, blocking collectives, local(): gathered = lax.all_gather(weights, 'dp', axis=0, tiled=True)  72.5 us
    ppermute x7, waiting for transfers between devices, passed_along(): return lax.ppermute(array, axis, pairs)  50.4 us
    conv_general_dilated x8, matrix products, conv_transposed(): lax.conv_general_dilated(slope, flipped, (1, 1, 1), [(1, 1)] * 3, dimensi...  15.6 us
    ppermute x7, starting transfers between devices, passed_along(): return lax.ppermute(array, axis, pairs)  15.2 us
  transfers between devices with their start and end apart: 8, of which 8 were waited for; matrix products, arithmetic and copies ran while one was open for 1% of the time, Pallas kernels for 0%

profile of v1, /device:TPU:2, one launch (start us, length us, event | category | flops | bytes accessed | tf_op | source)
XLA Modules:
  0.0 406.5 jit_solution(4203075434168369874)
XLA Ops:
  12.4 72.5 %all_gather.3 = bf16[64,54,128]{2,1,0:T(8,128)(2,1)S(1)} all-gather(bf16[1,54,128]{2,1,0:T(8,128)(2,1)} %param.6), channel_id=1, replica_groups=mesh['segment'=8,'dp'=64] {'dp'}, dimensions={0}, use_global_device_ids=true | all-gather | bytes 898560 | tf_op jit(solution)/shard_map/all_gather | solution.py:61
  86.7 1.9 add_multiply_fusion
  90.4 2.4 collective-permute-start
  92.8 5.2 %collective-permute-done = bf16[2,4,8,8,128]{4,0,3,2,1:T(2,128)(2,1)S(1)} collective-permute-done((bf16[2,4,8,8,128]{4,0,3,2,1:T(2,128)(2,1)S(1)}, bf16[2,4,8,8,128]{4,0,3,2,1:T(2,128)(2,1)S(1)}, u32[]{:S(2)}, u32[]{:S(2)}) %collective-permute-start) | collective-permute-done | bytes 131104 | tf_op jit(solution)/shard_map/ppermute | solution.py:15
  98.0 1.8 fusion.1
  99.8 2.4 collective-permute-start.1
  102.3 4.4 %collective-permute-done.1 = bf16[2,4,8,8,128]{4,0,3,2,1:T(2,128)(2,1)S(1)} collective-permute-done((bf16[2,4,8,8,128]{4,0,3,2,1:T(2,128)(2,1)S(1)}, bf16[2,4,8,8,128]{4,0,3,2,1:T(2,128)(2,1)S(1)}, u32[]{:S(2)}, u32[]{:S(2)}) %collective-permute-start.1) | collective-permute-done | bytes 131104 | tf_op jit(solution)/shard_map/ppermute | solution.py:15
  106.7 1.8 fusion.2
  108.5 2.4 collective-permute-start.2
  110.9 6.9 %collective-permute-done.2 = bf16[2,4,8,8,128]{4,0,3,2,1:T(2,128)(2,1)S(1)} collective-permute-done((bf16[2,4,8,8,128]{4,0,3,2,1:T(2,128)(2,1)S(1)}, bf16[2,4,8,8,128]{4,0,3,2,1:T(2,128)(2,1)S(1)}, u32[]{:S(2)}, u32[]{:S(2)}) %collective-permute-start.2) | collective-permute-done | bytes 131104 | tf_op jit(solution)/shard_map/ppermute | solution.py:15
  117.9 1.8 fusion.3
  119.6 2.1 collective-permute-start.3
  121.7 8.1 %collective-permute-done.3 = bf16[2,4,8,8,128]{4,0,3,2,1:T(2,128)(2,1)S(1)} collective-permute-done((bf16[2,4,8,8,128]{4,0,3,2,1:T(2,128)(2,1)S(1)}, bf16[2,4,8,8,128]{4,0,3,2,1:T(2,128)(2,1)S(1)}, u32[]{:S(2)}, u32[]{:S(2)}) %collective-permute-start.3) | collective-permute-done | bytes 131104 | tf_op jit(solution)/shard_map/ppermute | solution.py:15
  129.9 1.8 fusion.4
  131.7 1.9 collective-permute-start.4
  133.6 8.5 %collective-permute-done.4 = bf16[2,4,8,8,128]{4,0,3,2,1:T(2,128)(2,1)S(1)} collective-permute-done((bf16[2,4,8,8,128]{4,0,3,2,1:T(2,128)(2,1)S(1)}, bf16[2,4,8,8,128]{4,0,3,2,1:T(2,128)(2,1)S(1)}, u32[]{:S(2)}, u32[]{:S(2)}) %collective-permute-start.4) | collective-permute-done | bytes 131104 | tf_op jit(solution)/shard_map/ppermute | solution.py:15
  143.9 1.9 collective-permute-start.5
  145.9 8.5 %collective-permute-done.5 = bf16[2,4,8,8,128]{4,0,3,2,1:T(2,128)(2,1)S(1)} collective-permute-done((bf16[2,4,8,8,128]{4,0,3,2,1:T(2,128)(2,1)S(1)}, bf16[2,4,8,8,128]{4,0,3,2,1:T(2,128)(2,1)S(1)}, u32[]{:S(2)}, u32[]{:S(2)}) %collective-permute-start.5) | collective-permute-done | bytes 131104 | tf_op jit(solution)/shard_map/ppermute | solution.py:15
  154.4 1.8 fusion.6
  156.2 1.9 collective-permute-start.6
  158.2 8.6 %collective-permute-done.6 = bf16[2,4,8,8,128]{4,0,3,2,1:T(2,128)(2,1)} collective-permute-done((bf16[2,4,8,8,128]{4,0,3,2,1:T(2,128)(2,1)S(1)}, bf16[2,4,8,8,128]{4,0,3,2,1:T(2,128)(2,1)}, u32[]{:S(2)}, u32[]{:S(2)}) %collective-permute-start.6) | collective-permute-done | bytes 131104 | tf_op jit(solution)/shard_map/ppermute | solution.py:15
  166.8 4.6 %fusion.18 = f32[3,3,3,128,128]{4,3,2,1,0:T(8,128)S(1)} fusion(pred[]{:T(512)S(6)} %eq.33, pred[]{:T(512)S(6)} %eq.35, pred[]{:T(512)S(6)} %eq.36, pred[]{:T(512)S(6)} %eq.37, pred[]{:T(512)S(6)} %eq.38, pred[]{:T(512)S(6)} %eq.39, pred[]{:T(512)S(6)} %eq.40, pred[]{:T(512)S(6)} %eq.34, bf16[2,4,8,8,128]{4,3,2,1,0:T(8,128)(2,1)S(1)} %bitcast.28, ...), kind=kOutput, calls=%fused_computation.59 | convolution fusion | flops 319815680 | bytes 3211272 | tf_op jit(solution)/shard_map/conv_general_dilated | solution.py:36
  174.0 3.3 fusion.9
  177.9 220.3 %reduce-scatter.5.cloned.1.call-done = f32[1,54,128]{2,1,0:T(8,128)} async-done(((f32[64,54,128]{2,1,0:T(8,128)}), f32[1,54,128]{2,1,0:T(8,128)}) %reduce-scatter.5.cloned.1.call-update) | async-done | bytes 27664
  (54 shorter events, 15.1 us)
Async XLA Ops:
  7.2 79.6 %copy-start = (bf16[1,2,4,8,8,128]{5,4,3,2,1,0:T(8,128)(2,1)S(1)}, bf16[1,2,4,8,8,128]{5,4,3,2,1,0:T(8,128)(2,1)}, u32[]{:S(2)}) copy-start(bf16[1,2,4,8,8,128]{5,4,3,2,1,0:T(8,128)(2,1)} %param.5) | copy-start | bytes 393220
  7.2 391.1 %reduce-scatter.5.cloned.1.call-start = ((), (), s32[]{:S(2)}) async-start(), calls=%async_computation.1 | async-start | bytes 1863680
  86.7 1.9 copy-start.1
  88.7 65.7 %copy-start.14 = (f32[2,4,8,8,128]{4,0,3,2,1:T(2,128)}, f32[2,4,8,8,128]{4,0,3,2,1:T(2,128)S(1)}, u32[]{:S(2)}) copy-start(f32[2,4,8,8,128]{4,0,3,2,1:T(2,128)S(1)} %add_multiply_fusion) | copy-start | bytes 786436
  90.4 7.6 %collective-permute-start = (bf16[2,4,8,8,128]{4,0,3,2,1:T(2,128)(2,1)S(1)}, bf16[2,4,8,8,128]{4,0,3,2,1:T(2,128)(2,1)S(1)}, u32[]{:S(2)}, u32[]{:S(2)}) collective-permute-start(bf16[2,4,8,8,128]{4,0,3,2,1:T(2,128)(2,1)S(1)} %fusion), channel_id=1, source_target_pairs={{64,0},{128,64},{192,128},{256,192},{320,256},{384,320},{448,384},... | collective-permute-start | bytes 393224 | tf_op jit(solution)/shard_map/ppermute | solution.py:15
  98.0 1.8 copy-start.2
  99.8 6.9 %collective-permute-start.1 = (bf16[2,4,8,8,128]{4,0,3,2,1:T(2,128)(2,1)S(1)}, bf16[2,4,8,8,128]{4,0,3,2,1:T(2,128)(2,1)S(1)}, u32[]{:S(2)}, u32[]{:S(2)}) collective-permute-start(bf16[2,4,8,8,128]{4,0,3,2,1:T(2,128)(2,1)S(1)} %fusion.1), channel_id=1, source_target_pairs={{64,0},{128,64},{192,128},{256,192},{320,256},{384,320},{448,384},... | collective-permute-start | bytes 393224 | tf_op jit(solution)/shard_map/ppermute | solution.py:15
  106.7 1.8 copy-start.5
  108.5 9.4 %collective-permute-start.2 = (bf16[2,4,8,8,128]{4,0,3,2,1:T(2,128)(2,1)S(1)}, bf16[2,4,8,8,128]{4,0,3,2,1:T(2,128)(2,1)S(1)}, u32[]{:S(2)}, u32[]{:S(2)}) collective-permute-start(bf16[2,4,8,8,128]{4,0,3,2,1:T(2,128)(2,1)S(1)} %fusion.2), channel_id=1, source_target_pairs={{64,0},{128,64},{192,128},{256,192},{320,256},{384,320},{448,384},... | collective-permute-start | bytes 393224 | tf_op jit(solution)/shard_map/ppermute | solution.py:15
  117.9 1.8 copy-start.8
  119.6 10.2 %collective-permute-start.3 = (bf16[2,4,8,8,128]{4,0,3,2,1:T(2,128)(2,1)S(1)}, bf16[2,4,8,8,128]{4,0,3,2,1:T(2,128)(2,1)S(1)}, u32[]{:S(2)}, u32[]{:S(2)}) collective-permute-start(bf16[2,4,8,8,128]{4,0,3,2,1:T(2,128)(2,1)S(1)} %fusion.3), channel_id=1, source_target_pairs={{64,0},{128,64},{192,128},{256,192},{320,256},{384,320},{448,384},... | collective-permute-start | bytes 393224 | tf_op jit(solution)/shard_map/ppermute | solution.py:15
  129.9 1.8 copy-start.11
  131.6 12.3 %copy-start.3 = (bf16[2,4,8,8,128]{4,0,3,2,1:T(2,128)(2,1)}, bf16[2,4,8,8,128]{4,0,3,2,1:T(2,128)(2,1)S(1)}, u32[]{:S(2)}) copy-start(bf16[2,4,8,8,128]{4,0,3,2,1:T(2,128)(2,1)S(1)} %fusion.4) | copy-start | bytes 393220
  131.7 10.5 %collective-permute-start.4 = (bf16[2,4,8,8,128]{4,0,3,2,1:T(2,128)(2,1)S(1)}, bf16[2,4,8,8,128]{4,0,3,2,1:T(2,128)(2,1)S(1)}, u32[]{:S(2)}, u32[]{:S(2)}) collective-permute-start(bf16[2,4,8,8,128]{4,0,3,2,1:T(2,128)(2,1)S(1)} %fusion.4), channel_id=1, source_target_pairs={{64,0},{128,64},{192,128},{256,192},{320,256},{384,320},{448,384},... | collective-permute-start | bytes 393224 | tf_op jit(solution)/shard_map/ppermute | solution.py:15
  142.1 1.8 copy-start.12
  143.9 12.3 %copy-start.6 = (bf16[2,4,8,8,128]{4,0,3,2,1:T(2,128)(2,1)}, bf16[2,4,8,8,128]{4,0,3,2,1:T(2,128)(2,1)S(1)}, u32[]{:S(2)}) copy-start(bf16[2,4,8,8,128]{4,0,3,2,1:T(2,128)(2,1)S(1)} %fusion.5) | copy-start | bytes 393220
  143.9 10.5 %collective-permute-start.5 = (bf16[2,4,8,8,128]{4,0,3,2,1:T(2,128)(2,1)S(1)}, bf16[2,4,8,8,128]{4,0,3,2,1:T(2,128)(2,1)S(1)}, u32[]{:S(2)}, u32[]{:S(2)}) collective-permute-start(bf16[2,4,8,8,128]{4,0,3,2,1:T(2,128)(2,1)S(1)} %fusion.5), channel_id=1, source_target_pairs={{64,0},{128,64},{192,128},{256,192},{320,256},{384,320},{448,384},... | collective-permute-start | bytes 393224 | tf_op jit(solution)/shard_map/ppermute | solution.py:15
  154.4 1.8 copy-start.13
  156.2 2.0 copy-start.9
  156.2 10.6 %collective-permute-start.6 = (bf16[2,4,8,8,128]{4,0,3,2,1:T(2,128)(2,1)S(1)}, bf16[2,4,8,8,128]{4,0,3,2,1:T(2,128)(2,1)}, u32[]{:S(2)}, u32[]{:S(2)}) collective-permute-start(bf16[2,4,8,8,128]{4,0,3,2,1:T(2,128)(2,1)S(1)} %fusion.6), channel_id=1, source_target_pairs={{64,0},{128,64},{192,128},{256,192},{320,256},{384,320},{448,384},... | collective-permute-start | bytes 393224 | tf_op jit(solution)/shard_map/ppermute | solution.py:15
  172.8 0.9 copy-start.4
  172.8 1.0 copy-start.7
  172.8 1.0 copy-start.10
  172.8 1.1 copy-start.15
Sparse Core Ops, SparseCore 0:
  173.0 225.2 reduce-scatter.4

commit v2 on v1

--- a/solution.py
+++ b/solution.py
@@ -13,6 +13,43 @@
     length = lax.axis_size(axis)
     pairs = [(i, i + by) for i in range(length) if 0 <= i + by < length]
     return lax.ppermute(array, axis, pairs)
+
+
+def exchanged(array, axis, mask):
+    length = lax.axis_size(axis)
+    return lax.ppermute(array, axis, [(i, i ^ mask) for i in range(length)])
+
+
+def bit_count(length):
+    return length.bit_length() - 1
+
+
+def gather_by_halves(block, axis, order):
+    index = lax.axis_index(axis)
+    held = block
+    for bit in order:
+        upper = ((index >> bit) & 1) == 1
+        received = exchanged(held, axis, 1 << bit)
+        low = jnp.where(upper, received, held)
+        high = jnp.where(upper, held, received)
+        held = jnp.stack([low, high])
+    done = len(order)
+    natural = [done - 1 - order.index(bit) for bit in range(done - 1, -1, -1)]
+    held = jnp.transpose(held, natural + list(range(done, held.ndim)))
+    return held.reshape((-1,) + block.shape[1:])
+
+
+def reduce_by_halves(chunks, axis, order):
+    index = lax.axis_index(axis)
+    done = len(order)
+    held = chunks.reshape((2,) * done + chunks.shape[1:])
+    held = jnp.transpose(held, [done - 1 - bit for bit in order] + list(range(done, held.ndim)))
+    for bit in order:
+        mine = (index >> bit) & 1
+        kept = lax.dynamic_index_in_dim(held, mine, 0, keepdims=False)
+        sent = lax.dynamic_index_in_dim(held, 1 - mine, 0, keepdims=False)
+        held = kept + exchanged(sent, axis, 1 << bit)
+    return held.reshape((1,) + chunks.shape[1:])
 
 
 def conv_forward(field, kernel):
@@ -58,7 +95,9 @@
     dp_count = lax.axis_size("dp")
     segment_index = lax.axis_index("segment")
     channels = weights.shape[2]
-    gathered = lax.all_gather(weights, "dp", axis=0, tiled=True)
+    bits = bit_count(dp_count)
+    gather_order = list(range(bits - 1, -1, -1))
+    gathered = gather_by_halves(weights[0][None], "dp", gather_order)
     kernel = gathered.reshape(3, 3, 3, channels, channels)
     fields = acts[0]
     micro_count, size_x, size_y, size_z = fields.shape[:4]
@@ -86,7 +125,7 @@
             incoming = passed_along(down_grad, "segment", -1)
 
     grad_term = conv_kernel_grad(fields, slope_held).reshape(dp_count, -1, channels)
-    reduced = lax.psum_scatter(grad_term, "dp", scatter_dimension=0, tiled=True)
+    reduced = reduce_by_halves(grad_term, "dp", list(range(bits)))
     scale_factor = 1.0 / math.sqrt(dp_count * micro_count * cell_count)
     return (grads_held[None], reduced * scale_factor)
 

time: 407 us -> 233 us (0.57)
  the two profiles are of different devices: /device:TPU:2 before, /device:TPU:6 now
where the time goes in v2:
time: 233 us; the launch traced here: 232 us
  waiting for transfers between devices  123 us (53%)
  starting transfers between devices  72 us (31%)
  matrix products  21.2 us (9%)
  local copies, waits for them, and re-layouts  8.48 us (4%)
  other arithmetic  6.85 us (3%)
    ppermute x12, waiting for transfers between devices, exchanged(): return lax.ppermute(array, axis, [(i, i ^ mask) for i in range(length)])  63.2 us
    ppermute x7, waiting for transfers between devices, passed_along(): return lax.ppermute(array, axis, pairs)  59.4 us
    ppermute x12, starting transfers between devices, exchanged(): return lax.ppermute(array, axis, [(i, i ^ mask) for i in range(length)])  57.6 us
    conv_general_dilated x8, matrix products, conv_transposed(): lax.conv_general_dilated(slope, flipped, (1, 1, 1), [(1, 1)] * 3, dimensi...  14.6 us
    ppermute x7, starting transfers between devices, passed_along(): return lax.ppermute(array, axis, pairs)  14.4 us
    conv_general_dilated x1, matrix products, conv_kernel_grad(): lax.conv_general_dilated(field, slope, (1, 1, 1), [(1, 1)] * 3, dimension...  4.67 us
  transfers between devices with their start and end apart: 19, of which 18 were waited for; matrix products, arithmetic and copies ran while one was open for 4% of the time, Pallas kernels for 0%

profile of v2, /device:TPU:6, one launch (start us, length us, event | category | flops | bytes accessed | tf_op | source)
XLA Modules:
  0.0 232.4 jit_solution(8957228234643321343)
XLA Ops:
  0.6 3.5 %collective-permute-start = (bf16[1,54,128]{2,1,0:T(8,128)(2,1)}, bf16[1,54,128]{2,1,0:T(8,128)(2,1)S(1)}, u32[]{:S(2)}, u32[]{:S(2)}) collective-permute-start(bf16[1,54,128]{2,1,0:T(8,128)(2,1)} %param.6), channel_id=1, source_target_pairs={{0,32},{1,33},{2,34},{3,35},{4,36},{5,37},{6,38},{7,39},{8,40},{9,... | collective-permute-start | bytes 41480 | tf_op jit(solution)/shard_map/ppermute | solution.py:20
  11.1 15.7 %collective-permute-start.1 = (bf16[2,1,54,128]{3,2,0,1:T(8,128)(2,1)S(1)}, bf16[2,1,54,128]{3,2,0,1:T(8,128)(2,1)S(1)}, u32[]{:S(2)}, u32[]{:S(2)}) collective-permute-start(bf16[2,1,54,128]{3,2,0,1:T(8,128)(2,1)S(1)} %fusion.32), channel_id=1, source_target_pairs={{0,16},{1,17},{2,18},{3,19},{4,20},{5,21},{6,22},{7,23},{8,24},{9,... | collective-permute-start | bytes 82952 | tf_op jit(solution)/shard_map/ppermute | solution.py:20
  28.7 6.7 %collective-permute-start.2 = (bf16[2,2,1,54,128]{4,3,1,0,2:T(8,128)(2,1)S(1)}, bf16[2,2,1,54,128]{4,3,1,0,2:T(8,128)(2,1)S(1)}, u32[]{:S(2)}, u32[]{:S(2)}) collective-permute-start(bf16[2,2,1,54,128]{4,3,1,0,2:T(8,128)(2,1)S(1)} %fusion.29), channel_id=1, source_target_pairs={{0,8},{1,9},{2,10},{3,11},{4,12},{5,13},{6,14},{7,15},{8,0},{9,1},... | collective-permute-start | bytes 165896 | tf_op jit(solution)/shard_map/ppermute | solution.py:20
  35.5 5.6 %collective-permute-done.2 = bf16[2,2,1,54,128]{4,3,1,0,2:T(8,128)(2,1)S(1)} collective-permute-done((bf16[2,2,1,54,128]{4,3,1,0,2:T(8,128)(2,1)S(1)}, bf16[2,2,1,54,128]{4,3,1,0,2:T(8,128)(2,1)S(1)}, u32[]{:S(2)}, u32[]{:S(2)}) %collective-permute-start.2) | collective-permute-done | bytes 55328 | tf_op jit(solution)/shard_map/ppermute | solution.py:20
  43.2 5.6 %collective-permute-done.3 = bf16[2,2,2,1,54,128]{5,4,2,1,0,3:T(8,128)(2,1)S(1)} collective-permute-done((bf16[2,2,2,1,54,128]{5,4,2,1,0,3:T(8,128)(2,1)S(1)}, bf16[2,2,2,1,54,128]{5,4,2,1,0,3:T(8,128)(2,1)S(1)}, u32[]{:S(2)}, u32[]{:S(2)}) %collective-permute-start.3) | collective-permute-done | bytes 110624 | tf_op jit(solution)/shard_map/ppermute | solution.py:20
  50.8 5.9 %collective-permute-done.4 = bf16[2,2,2,2,1,54,128]{6,5,3,2,1,0,4:T(8,128)(2,1)S(1)} collective-permute-done((bf16[2,2,2,2,1,54,128]{6,5,3,2,1,0,4:T(8,128)(2,1)S(1)}, bf16[2,2,2,2,1,54,128]{6,5,3,2,1,0,4:T(8,128)(2,1)S(1)}, u32[]{:S(2)}, u32[]{:S(2)}) %collective-permute-start.4) | collective-permute-done | bytes 221216 | tf_op jit(solution)/shard_map/ppermute | solution.py:20
  65.4 2.7 %collective-permute-start.6 = (bf16[2,4,8,8,128]{4,0,3,2,1:T(2,128)(2,1)S(1)}, bf16[2,4,8,8,128]{4,0,3,2,1:T(2,128)(2,1)S(1)}, u32[]{:S(2)}, u32[]{:S(2)}) collective-permute-start(bf16[2,4,8,8,128]{4,0,3,2,1:T(2,128)(2,1)S(1)} %fusion), channel_id=1, source_target_pairs={{64,0},{128,64},{192,128},{256,192},{320,256},{384,320},{448,384},... | collective-permute-start | bytes 393224 | tf_op jit(solution)/shard_map/ppermute | solution.py:15
  68.1 8.3 %collective-permute-done.6 = bf16[2,4,8,8,128]{4,0,3,2,1:T(2,128)(2,1)S(1)} collective-permute-done((bf16[2,4,8,8,128]{4,0,3,2,1:T(2,128)(2,1)S(1)}, bf16[2,4,8,8,128]{4,0,3,2,1:T(2,128)(2,1)S(1)}, u32[]{:S(2)}, u32[]{:S(2)}) %collective-permute-start.6) | collective-permute-done | bytes 131104 | tf_op jit(solution)/shard_map/ppermute | solution.py:15
  80.1 8.5 %collective-permute-done.7 = bf16[2,4,8,8,128]{4,0,3,2,1:T(2,128)(2,1)S(1)} collective-permute-done((bf16[2,4,8,8,128]{4,0,3,2,1:T(2,128)(2,1)S(1)}, bf16[2,4,8,8,128]{4,0,3,2,1:T(2,128)(2,1)S(1)}, u32[]{:S(2)}, u32[]{:S(2)}) %collective-permute-start.7) | collective-permute-done | bytes 131104 | tf_op jit(solution)/shard_map/ppermute | solution.py:15
  92.4 8.5 %collective-permute-done.8 = bf16[2,4,8,8,128]{4,0,3,2,1:T(2,128)(2,1)S(1)} collective-permute-done((bf16[2,4,8,8,128]{4,0,3,2,1:T(2,128)(2,1)S(1)}, bf16[2,4,8,8,128]{4,0,3,2,1:T(2,128)(2,1)S(1)}, u32[]{:S(2)}, u32[]{:S(2)}) %collective-permute-start.8) | collective-permute-done | bytes 131104 | tf_op jit(solution)/shard_map/ppermute | solution.py:15
  104.8 8.4 %collective-permute-done.9 = bf16[2,4,8,8,128]{4,0,3,2,1:T(2,128)(2,1)S(1)} collective-permute-done((bf16[2,4,8,8,128]{4,0,3,2,1:T(2,128)(2,1)S(1)}, bf16[2,4,8,8,128]{4,0,3,2,1:T(2,128)(2,1)S(1)}, u32[]{:S(2)}, u32[]{:S(2)}) %collective-permute-start.9) | collective-permute-done | bytes 131104 | tf_op jit(solution)/shard_map/ppermute | solution.py:15
  116.9 8.5 %collective-permute-done.10 = bf16[2,4,8,8,128]{4,0,3,2,1:T(2,128)(2,1)S(1)} collective-permute-done((bf16[2,4,8,8,128]{4,0,3,2,1:T(2,128)(2,1)S(1)}, bf16[2,4,8,8,128]{4,0,3,2,1:T(2,128)(2,1)S(1)}, u32[]{:S(2)}, u32[]{:S(2)}) %collective-permute-start.10) | collective-permute-done | bytes 131104 | tf_op jit(solution)/shard_map/ppermute | solution.py:15
  129.1 8.5 %collective-permute-done.11 = bf16[2,4,8,8,128]{4,0,3,2,1:T(2,128)(2,1)S(1)} collective-permute-done((bf16[2,4,8,8,128]{4,0,3,2,1:T(2,128)(2,1)S(1)}, bf16[2,4,8,8,128]{4,0,3,2,1:T(2,128)(2,1)S(1)}, u32[]{:S(2)}, u32[]{:S(2)}) %collective-permute-start.11) | collective-permute-done | bytes 131104 | tf_op jit(solution)/shard_map/ppermute | solution.py:15
  141.4 8.5 %collective-permute-done.12 = bf16[2,4,8,8,128]{4,0,3,2,1:T(2,128)(2,1)S(1)} collective-permute-done((bf16[2,4,8,8,128]{4,0,3,2,1:T(2,128)(2,1)S(1)}, bf16[2,4,8,8,128]{4,0,3,2,1:T(2,128)(2,1)S(1)}, u32[]{:S(2)}, u32[]{:S(2)}) %collective-permute-start.12) | collective-permute-done | bytes 131104 | tf_op jit(solution)/shard_map/ppermute | solution.py:15
  150.6 4.7 %fusion.22 = f32[3,3,3,128,128]{4,3,2,1,0:T(8,128)} fusion(pred[]{:T(512)S(6)} %eq.51, pred[]{:T(512)S(6)} %eq.59, pred[]{:T(512)S(6)} %eq.60, pred[]{:T(512)S(6)} %eq.61, pred[]{:T(512)S(6)} %eq.62, pred[]{:T(512)S(6)} %eq.63, pred[]{:T(512)S(6)} %eq.64, pred[]{:T(512)S(6)} %eq.52, bf16[2,4,8,8,128]{4,3,2,1,0:T(8,128)(2,1)S(1)} %bitcast.137, ...), kind=kOutput, calls=%fused_computation.77 | convolution fusion | flops 319815680 | bytes 3211272 | tf_op jit(solution)/shard_map/conv_general_dilated | solution.py:73
  160.4 2.7 %collective-permute-done.13 = f32[2,2,2,2,2,54,128]{6,4,5,3,2,1,0:T(2,128)} collective-permute-done((f32[2,2,2,2,2,54,128]{6,4,5,3,2,1,0:T(2,128)}, f32[2,2,2,2,2,54,128]{6,4,5,3,2,1,0:T(2,128)}, u32[]{:S(2)}, u32[]{:S(2)}) %collective-permute-start.13) | collective-permute-done | bytes 884768 | tf_op jit(solution)/shard_map/ppermute | solution.py:20
  166.6 12.5 %collective-permute-done.14 = f32[2,2,2,2,54,128]{5,4,3,2,1,0:T(8,128)S(1)} collective-permute-done((f32[2,2,2,2,54,128]{5,4,3,2,1,0:T(8,128)S(1)}, f32[2,2,2,2,54,128]{5,4,3,2,1,0:T(8,128)S(1)}, u32[]{:S(2)}, u32[]{:S(2)}) %collective-permute-start.14) | collective-permute-done | bytes 442400 | tf_op jit(solution)/shard_map/ppermute | solution.py:20
  179.3 3.0 %collective-permute-start.15 = (f32[2,2,2,54,128]{4,3,2,1,0:T(8,128)S(1)}, f32[2,2,2,54,128]{4,3,2,1,0:T(8,128)S(1)}, u32[]{:S(2)}, u32[]{:S(2)}) collective-permute-start(f32[2,2,2,54,128]{4,3,2,1,0:T(8,128)S(1)} %dynamic-slice_bitcast_fusion.1), channel_id=1, source_target_pairs={{0,4},{1,5},{2,6},{3,7},{4,0},{5,1},{6,2},{7,3},{8,12},{9,13},{10,... | collective-permute-start | bytes 663560 | tf_op jit(solution)/shard_map/ppermute | solution.py:20
  182.3 11.7 %collective-permute-done.15 = f32[2,2,2,54,128]{4,3,2,1,0:T(8,128)S(1)} collective-permute-done((f32[2,2,2,54,128]{4,3,2,1,0:T(8,128)S(1)}, f32[2,2,2,54,128]{4,3,2,1,0:T(8,128)S(1)}, u32[]{:S(2)}, u32[]{:S(2)}) %collective-permute-start.15) | collective-permute-done | bytes 221216 | tf_op jit(solution)/shard_map/ppermute | solution.py:20
  194.0 6.4 %collective-permute-start.16 = (f32[2,2,54,128]{3,2,1,0:T(8,128)S(1)}, f32[2,2,54,128]{3,2,1,0:T(8,128)S(1)}, u32[]{:S(2)}, u32[]{:S(2)}) collective-permute-start(f32[2,2,54,128]{3,2,1,0:T(8,128)S(1)} %dynamic-slice_bitcast_fusion.2), channel_id=1, source_target_pairs={{0,8},{1,9},{2,10},{3,11},{4,12},{5,13},{6,14},{7,15},{8,0},{9,1},... | collective-permute-start | bytes 331784 | tf_op jit(solution)/shard_map/ppermute | solution.py:20
  200.4 10.7 %collective-permute-done.16 = f32[2,2,54,128]{3,2,1,0:T(8,128)S(1)} collective-permute-done((f32[2,2,54,128]{3,2,1,0:T(8,128)S(1)}, f32[2,2,54,128]{3,2,1,0:T(8,128)S(1)}, u32[]{:S(2)}, u32[]{:S(2)}) %collective-permute-start.16) | collective-permute-done | bytes 110624 | tf_op jit(solution)/shard_map/ppermute | solution.py:20
  211.2 10.2 %collective-permute-start.17 = (f32[2,54,128]{2,1,0:T(8,128)S(1)}, f32[2,54,128]{2,1,0:T(8,128)S(1)}, u32[]{:S(2)}, u32[]{:S(2)}) collective-permute-start(f32[2,54,128]{2,1,0:T(8,128)S(1)} %dynamic-slice_bitcast_fusion.3), channel_id=1, source_target_pairs={{0,16},{1,17},{2,18},{3,19},{4,20},{5,21},{6,22},{7,23},{8,24},{9,... | collective-permute-start | bytes 165896 | tf_op jit(solution)/shard_map/ppermute | solution.py:20
  221.4 4.6 %collective-permute-done.17 = f32[2,54,128]{2,1,0:T(8,128)S(1)} collective-permute-done((f32[2,54,128]{2,1,0:T(8,128)S(1)}, f32[2,54,128]{2,1,0:T(8,128)S(1)}, u32[]{:S(2)}, u32[]{:S(2)}) %collective-permute-start.17) | collective-permute-done | bytes 55328 | tf_op jit(solution)/shard_map/ppermute | solution.py:20
  226.0 2.4 %collective-permute-start.18 = (f32[54,128]{1,0:T(8,128)S(1)}, f32[54,128]{1,0:T(8,128)S(1)}, u32[]{:S(2)}, u32[]{:S(2)}) collective-permute-start(f32[54,128]{1,0:T(8,128)S(1)} %dynamic-slice_bitcast_fusion.4), channel_id=1, source_target_pairs={{0,32},{1,33},{2,34},{3,35},{4,36},{5,37},{6,38},{7,39},{8,40},{9,... | collective-permute-start | bytes 82952 | tf_op jit(solution)/shard_map/ppermute | solution.py:20
  (92 shorter events, 57.1 us)
Async XLA Ops:
  0.6 9.7 %collective-permute-start = (bf16[1,54,128]{2,1,0:T(8,128)(2,1)}, bf16[1,54,128]{2,1,0:T(8,128)(2,1)S(1)}, u32[]{:S(2)}, u32[]{:S(2)}) collective-permute-start(bf16[1,54,128]{2,1,0:T(8,128)(2,1)} %param.6), channel_id=1, source_target_pairs={{0,32},{1,33},{2,34},{3,35},{4,36},{5,37},{6,38},{7,39},{8,40},{9,... | collective-permute-start | bytes 41480 | tf_op jit(solution)/shard_map/ppermute | solution.py:20
  11.1 17.6 %collective-permute-start.1 = (bf16[2,1,54,128]{3,2,0,1:T(8,128)(2,1)S(1)}, bf16[2,1,54,128]{3,2,0,1:T(8,128)(2,1)S(1)}, u32[]{:S(2)}, u32[]{:S(2)}) collective-permute-start(bf16[2,1,54,128]{3,2,0,1:T(8,128)(2,1)S(1)} %fusion.32), channel_id=1, source_target_pairs={{0,16},{1,17},{2,18},{3,19},{4,20},{5,21},{6,22},{7,23},{8,24},{9,... | collective-permute-start | bytes 82952 | tf_op jit(solution)/shard_map/ppermute | solution.py:20
  28.7 12.4 %collective-permute-start.2 = (bf16[2,2,1,54,128]{4,3,1,0,2:T(8,128)(2,1)S(1)}, bf16[2,2,1,54,128]{4,3,1,0,2:T(8,128)(2,1)S(1)}, u32[]{:S(2)}, u32[]{:S(2)}) collective-permute-start(bf16[2,2,1,54,128]{4,3,1,0,2:T(8,128)(2,1)S(1)} %fusion.29), channel_id=1, source_target_pairs={{0,8},{1,9},{2,10},{3,11},{4,12},{5,13},{6,14},{7,15},{8,0},{9,1},... | collective-permute-start | bytes 165896 | tf_op jit(solution)/shard_map/ppermute | solution.py:20
  41.2 7.6 %collective-permute-start.3 = (bf16[2,2,2,1,54,128]{5,4,2,1,0,3:T(8,128)(2,1)S(1)}, bf16[2,2,2,1,54,128]{5,4,2,1,0,3:T(8,128)(2,1)S(1)}, u32[]{:S(2)}, u32[]{:S(2)}) collective-permute-start(bf16[2,2,2,1,54,128]{5,4,2,1,0,3:T(8,128)(2,1)S(1)} %fusion.24), channel_id=1, source_target_pairs={{0,4},{1,5},{2,6},{3,7},{4,0},{5,1},{6,2},{7,3},{8,12},{9,13},{10,... | collective-permute-start | bytes 331784 | tf_op jit(solution)/shard_map/ppermute | solution.py:20
  48.8 7.9 %collective-permute-start.4 = (bf16[2,2,2,2,1,54,128]{6,5,3,2,1,0,4:T(8,128)(2,1)S(1)}, bf16[2,2,2,2,1,54,128]{6,5,3,2,1,0,4:T(8,128)(2,1)S(1)}, u32[]{:S(2)}, u32[]{:S(2)}) collective-permute-start(bf16[2,2,2,2,1,54,128]{6,5,3,2,1,0,4:T(8,128)(2,1)S(1)} %fusion.21), channel_id=1, source_target_pairs={{0,2},{1,3},{2,0},{3,1},{4,6},{5,7},{6,4},{7,5},{8,10},{9,11},{10,... | collective-permute-start | bytes 663560 | tf_op jit(solution)/shard_map/ppermute | solution.py:20
  56.9 3.7 %collective-permute-start.5 = (bf16[2,2,2,2,2,1,54,128]{7,6,4,3,2,1,0,5:T(8,128)(2,1)S(1)}, bf16[2,2,2,2,2,1,54,128]{7,6,4,3,2,1,0,5:T(8,128)(2,1)S(1)}, u32[]{:S(2)}, u32[]{:S(2)}) collective-permute-start(bf16[2,2,2,2,2,1,54,128]{7,6,4,3,2,1,0,5:T(8,128)(2,1)S(1)} %fusion.11), channel_id=1, source_target_pairs={{0,1},{1,0},{2,3},{3,2},{4,5},{5,4},{6,7},{7,6},{8,9},{9,8},{10,11... | collective-permute-start | bytes 1327112 | tf_op jit(solution)/shard_map/ppermute | solution.py:20
  63.6 86.3 %copy-start.8 = (f32[2,4,8,8,128]{4,0,3,2,1:T(2,128)}, f32[2,4,8,8,128]{4,0,3,2,1:T(2,128)S(1)}, u32[]{:S(2)}) copy-start(f32[2,4,8,8,128]{4,0,3,2,1:T(2,128)S(1)} %add_multiply_fusion) | copy-start | bytes 786436
  65.4 11.0 %collective-permute-start.6 = (bf16[2,4,8,8,128]{4,0,3,2,1:T(2,128)(2,1)S(1)}, bf16[2,4,8,8,128]{4,0,3,2,1:T(2,128)(2,1)S(1)}, u32[]{:S(2)}, u32[]{:S(2)}) collective-permute-start(bf16[2,4,8,8,128]{4,0,3,2,1:T(2,128)(2,1)S(1)} %fusion), channel_id=1, source_target_pairs={{64,0},{128,64},{192,128},{256,192},{320,256},{384,320},{448,384},... | collective-permute-start | bytes 393224 | tf_op jit(solution)/shard_map/ppermute | solution.py:15
  78.2 10.5 %collective-permute-start.7 = (bf16[2,4,8,8,128]{4,0,3,2,1:T(2,128)(2,1)S(1)}, bf16[2,4,8,8,128]{4,0,3,2,1:T(2,128)(2,1)S(1)}, u32[]{:S(2)}, u32[]{:S(2)}) collective-permute-start(bf16[2,4,8,8,128]{4,0,3,2,1:T(2,128)(2,1)S(1)} %fusion.1), channel_id=1, source_target_pairs={{64,0},{128,64},{192,128},{256,192},{320,256},{384,320},{448,384},... | collective-permute-start | bytes 393224 | tf_op jit(solution)/shard_map/ppermute | solution.py:15
  90.4 10.5 %collective-permute-start.8 = (bf16[2,4,8,8,128]{4,0,3,2,1:T(2,128)(2,1)S(1)}, bf16[2,4,8,8,128]{4,0,3,2,1:T(2,128)(2,1)S(1)}, u32[]{:S(2)}, u32[]{:S(2)}) collective-permute-start(bf16[2,4,8,8,128]{4,0,3,2,1:T(2,128)(2,1)S(1)} %fusion.2), channel_id=1, source_target_pairs={{64,0},{128,64},{192,128},{256,192},{320,256},{384,320},{448,384},... | collective-permute-start | bytes 393224 | tf_op jit(solution)/shard_map/ppermute | solution.py:15
  102.7 10.5 %collective-permute-start.9 = (bf16[2,4,8,8,128]{4,0,3,2,1:T(2,128)(2,1)S(1)}, bf16[2,4,8,8,128]{4,0,3,2,1:T(2,128)(2,1)S(1)}, u32[]{:S(2)}, u32[]{:S(2)}) collective-permute-start(bf16[2,4,8,8,128]{4,0,3,2,1:T(2,128)(2,1)S(1)} %fusion.3), channel_id=1, source_target_pairs={{64,0},{128,64},{192,128},{256,192},{320,256},{384,320},{448,384},... | collective-permute-start | bytes 393224 | tf_op jit(solution)/shard_map/ppermute | solution.py:15
  114.9 10.5 %collective-permute-start.10 = (bf16[2,4,8,8,128]{4,0,3,2,1:T(2,128)(2,1)S(1)}, bf16[2,4,8,8,128]{4,0,3,2,1:T(2,128)(2,1)S(1)}, u32[]{:S(2)}, u32[]{:S(2)}) collective-permute-start(bf16[2,4,8,8,128]{4,0,3,2,1:T(2,128)(2,1)S(1)} %fusion.4), channel_id=1, source_target_pairs={{64,0},{128,64},{192,128},{256,192},{320,256},{384,320},{448,384},... | collective-permute-start | bytes 393224 | tf_op jit(solution)/shard_map/ppermute | solution.py:15
  127.2 10.5 %collective-permute-start.11 = (bf16[2,4,8,8,128]{4,0,3,2,1:T(2,128)(2,1)S(1)}, bf16[2,4,8,8,128]{4,0,3,2,1:T(2,128)(2,1)S(1)}, u32[]{:S(2)}, u32[]{:S(2)}) collective-permute-start(bf16[2,4,8,8,128]{4,0,3,2,1:T(2,128)(2,1)S(1)} %fusion.5), channel_id=1, source_target_pairs={{64,0},{128,64},{192,128},{256,192},{320,256},{384,320},{448,384},... | collective-permute-start | bytes 393224 | tf_op jit(solution)/shard_map/ppermute | solution.py:15
  139.5 10.5 %collective-permute-start.12 = (bf16[2,4,8,8,128]{4,0,3,2,1:T(2,128)(2,1)S(1)}, bf16[2,4,8,8,128]{4,0,3,2,1:T(2,128)(2,1)S(1)}, u32[]{:S(2)}, u32[]{:S(2)}) collective-permute-start(bf16[2,4,8,8,128]{4,0,3,2,1:T(2,128)(2,1)S(1)} %fusion.6), channel_id=1, source_target_pairs={{64,0},{128,64},{192,128},{256,192},{320,256},{384,320},{448,384},... | collective-permute-start | bytes 393224 | tf_op jit(solution)/shard_map/ppermute | solution.py:15
  158.5 4.7 %collective-permute-start.13 = (f32[2,2,2,2,2,54,128]{6,4,5,3,2,1,0:T(2,128)}, f32[2,2,2,2,2,54,128]{6,4,5,3,2,1,0:T(2,128)}, u32[]{:S(2)}, u32[]{:S(2)}) collective-permute-start(f32[2,2,2,2,2,54,128]{6,4,5,3,2,1,0:T(2,128)} %copy.139), channel_id=1, source_target_pairs={{0,1},{1,0},{2,3},{3,2},{4,5},{5,4},{6,7},{7,6},{8,9},{9,8},{10,11... | collective-permute-start | bytes 2654216 | tf_op jit(solution)/shard_map/ppermute | solution.py:20
  164.5 63.8 %copy-start.3 = (bf16[2,4,8,8,128]{4,0,3,2,1:T(2,128)(2,1)S(1)}, bf16[2,4,8,8,128]{4,0,3,2,1:T(2,128)(2,1)}, u32[]{:S(2)}) copy-start(bf16[2,4,8,8,128]{4,0,3,2,1:T(2,128)(2,1)} %copy-done.2) | copy-start | bytes 393220
  164.5 63.8 %copy-start.5 = (bf16[2,4,8,8,128]{4,0,3,2,1:T(2,128)(2,1)S(1)}, bf16[2,4,8,8,128]{4,0,3,2,1:T(2,128)(2,1)}, u32[]{:S(2)}) copy-start(bf16[2,4,8,8,128]{4,0,3,2,1:T(2,128)(2,1)} %copy-done.4) | copy-start | bytes 393220
  164.5 63.8 %copy-start.7 = (bf16[2,4,8,8,128]{4,0,3,2,1:T(2,128)(2,1)S(1)}, bf16[2,4,8,8,128]{4,0,3,2,1:T(2,128)(2,1)}, u32[]{:S(2)}) copy-start(bf16[2,4,8,8,128]{4,0,3,2,1:T(2,128)(2,1)} %copy-done.6) | copy-start | bytes 393220
  164.6 14.6 %collective-permute-start.14 = (f32[2,2,2,2,54,128]{5,4,3,2,1,0:T(8,128)S(1)}, f32[2,2,2,2,54,128]{5,4,3,2,1,0:T(8,128)S(1)}, u32[]{:S(2)}, u32[]{:S(2)}) collective-permute-start(f32[2,2,2,2,54,128]{5,4,3,2,1,0:T(8,128)S(1)} %bitcast.135), channel_id=1, source_target_pairs={{0,2},{1,3},{2,0},{3,1},{4,6},{5,7},{6,4},{7,5},{8,10},{9,11},{10,... | collective-permute-start | bytes 1327112 | tf_op jit(solution)/shard_map/ppermute | solution.py:20
  179.2 49.2 %copy-start.9 = (f32[2,4,8,8,128]{4,0,3,2,1:T(2,128)S(1)}, f32[2,4,8,8,128]{4,0,3,2,1:T(2,128)}, u32[]{:S(2)}) copy-start(f32[2,4,8,8,128]{4,0,3,2,1:T(2,128)} %copy-done.8) | copy-start | bytes 786436
  179.3 14.7 %collective-permute-start.15 = (f32[2,2,2,54,128]{4,3,2,1,0:T(8,128)S(1)}, f32[2,2,2,54,128]{4,3,2,1,0:T(8,128)S(1)}, u32[]{:S(2)}, u32[]{:S(2)}) collective-permute-start(f32[2,2,2,54,128]{4,3,2,1,0:T(8,128)S(1)} %dynamic-slice_bitcast_fusion.1), channel_id=1, source_target_pairs={{0,4},{1,5},{2,6},{3,7},{4,0},{5,1},{6,2},{7,3},{8,12},{9,13},{10,... | collective-permute-start | bytes 663560 | tf_op jit(solution)/shard_map/ppermute | solution.py:20
  194.0 17.1 %collective-permute-start.16 = (f32[2,2,54,128]{3,2,1,0:T(8,128)S(1)}, f32[2,2,54,128]{3,2,1,0:T(8,128)S(1)}, u32[]{:S(2)}, u32[]{:S(2)}) collective-permute-start(f32[2,2,54,128]{3,2,1,0:T(8,128)S(1)} %dynamic-slice_bitcast_fusion.2), channel_id=1, source_target_pairs={{0,8},{1,9},{2,10},{3,11},{4,12},{5,13},{6,14},{7,15},{8,0},{9,1},... | collective-permute-start | bytes 331784 | tf_op jit(solution)/shard_map/ppermute | solution.py:20
  211.2 14.8 %collective-permute-start.17 = (f32[2,54,128]{2,1,0:T(8,128)S(1)}, f32[2,54,128]{2,1,0:T(8,128)S(1)}, u32[]{:S(2)}, u32[]{:S(2)}) collective-permute-start(f32[2,54,128]{2,1,0:T(8,128)S(1)} %dynamic-slice_bitcast_fusion.3), channel_id=1, source_target_pairs={{0,16},{1,17},{2,18},{3,19},{4,20},{5,21},{6,22},{7,23},{8,24},{9,... | collective-permute-start | bytes 165896 | tf_op jit(solution)/shard_map/ppermute | solution.py:20
  226.0 5.8 %collective-permute-start.18 = (f32[54,128]{1,0:T(8,128)S(1)}, f32[54,128]{1,0:T(8,128)S(1)}, u32[]{:S(2)}, u32[]{:S(2)}) collective-permute-start(f32[54,128]{1,0:T(8,128)S(1)} %dynamic-slice_bitcast_fusion.4), channel_id=1, source_target_pairs={{0,32},{1,33},{2,34},{3,35},{4,36},{5,37},{6,38},{7,39},{8,40},{9,... | collective-permute-start | bytes 82952 | tf_op jit(solution)/shard_map/ppermute | solution.py:20
  (5 other events, 26.2 us)

commit v3 on v2

--- a/solution.py
+++ b/solution.py
@@ -48,7 +48,8 @@
         mine = (index >> bit) & 1
         kept = lax.dynamic_index_in_dim(held, mine, 0, keepdims=False)
         sent = lax.dynamic_index_in_dim(held, 1 - mine, 0, keepdims=False)
-        held = kept + exchanged(sent, axis, 1 << bit)
+        received = exchanged(sent.astype(jnp.bfloat16), axis, 1 << bit)
+        held = kept + received.astype(jnp.float32)
     return held.reshape((1,) + chunks.shape[1:])
 
 
@@ -96,7 +97,7 @@
     segment_index = lax.axis_index("segment")
     channels = weights.shape[2]
     bits = bit_count(dp_count)
-    gather_order = list(range(bits - 1, -1, -1))
+    gather_order = list(range(bits - 2, 0, -1)) + [bits - 1, 0]
     gathered = gather_by_halves(weights[0][None], "dp", gather_order)
     kernel = gathered.reshape(3, 3, 3, channels, channels)
     fields = acts[0]
@@ -125,7 +126,7 @@
             incoming = passed_along(down_grad, "segment", -1)
 
     grad_term = conv_kernel_grad(fields, slope_held).reshape(dp_count, -1, channels)
-    reduced = reduce_by_halves(grad_term, "dp", list(range(bits)))
+    reduced = reduce_by_halves(grad_term, "dp", gather_order[::-1])
     scale_factor = 1.0 / math.sqrt(dp_count * micro_count * cell_count)
     return (grads_held[None], reduced * scale_factor)
 

time: 233 us -> 209 us (0.90)
  the two profiles are of different devices: /device:TPU:6 before, /device:TPU:14 now
where the time goes in v3:
time: 209 us; the launch traced here: 208 us
  waiting for transfers between devices  107 us (51%)
  starting transfers between devices  65.1 us (31%)
  matrix products  22.2 us (11%)
  local copies, waits for them, and re-layouts  6.18 us (3%)
  other arithmetic  5.69 us (3%)
    ppermute x7, waiting for transfers between devices, passed_along(): return lax.ppermute(array, axis, pairs)  59.5 us
    ppermute x12, starting transfers between devices, exchanged(): return lax.ppermute(array, axis, [(i, i ^ mask) for i in range(length)])  50.7 us
    ppermute x12, waiting for transfers between devices, exchanged(): return lax.ppermute(array, axis, [(i, i ^ mask) for i in range(length)])  47.9 us
    conv_general_dilated x8, matrix products, conv_transposed(): lax.conv_general_dilated(slope, flipped, (1, 1, 1), [(1, 1)] * 3, dimensi...  15.6 us
    ppermute x7, starting transfers between devices, passed_along(): return lax.ppermute(array, axis, pairs)  14.4 us
    conv_general_dilated x1, matrix products, conv_kernel_grad(): lax.conv_general_dilated(field, slope, (1, 1, 1), [(1, 1)] * 3, dimension...  4.66 us
  transfers between devices with their start and end apart: 19, of which 18 were waited for; matrix products, arithmetic and copies ran while one was open for 5% of the time, Pallas kernels for 0%

profile of v3, /device:TPU:14, one launch (start us, length us, event | category | flops | bytes accessed | tf_op | source)
XLA Modules:
  0.0 207.9 jit_solution(8428618901182995586)
XLA Ops:
  0.6 15.7 %collective-permute-start = (bf16[1,54,128]{2,1,0:T(8,128)(2,1)}, bf16[1,54,128]{2,1,0:T(8,128)(2,1)S(1)}, u32[]{:S(2)}, u32[]{:S(2)}) collective-permute-start(bf16[1,54,128]{2,1,0:T(8,128)(2,1)} %param.6), channel_id=1, source_target_pairs={{0,16},{1,17},{2,18},{3,19},{4,20},{5,21},{6,22},{7,23},{8,24},{9,... | collective-permute-start | bytes 41480 | tf_op jit(solution)/shard_map/ppermute | solution.py:20
  23.4 4.3 %collective-permute-start.1 = (bf16[2,1,54,128]{3,2,0,1:T(8,128)(2,1)S(1)}, bf16[2,1,54,128]{3,2,0,1:T(8,128)(2,1)S(1)}, u32[]{:S(2)}, u32[]{:S(2)}) collective-permute-start(bf16[2,1,54,128]{3,2,0,1:T(8,128)(2,1)S(1)} %fusion.38), channel_id=1, source_target_pairs={{0,8},{1,9},{2,10},{3,11},{4,12},{5,13},{6,14},{7,15},{8,0},{9,1},... | collective-permute-start | bytes 82952 | tf_op jit(solution)/shard_map/ppermute | solution.py:20
  27.7 5.9 %collective-permute-done.1 = bf16[2,1,54,128]{3,2,0,1:T(8,128)(2,1)S(1)} collective-permute-done((bf16[2,1,54,128]{3,2,0,1:T(8,128)(2,1)S(1)}, bf16[2,1,54,128]{3,2,0,1:T(8,128)(2,1)S(1)}, u32[]{:S(2)}, u32[]{:S(2)}) %collective-permute-start.1) | collective-permute-done | bytes 27680 | tf_op jit(solution)/shard_map/ppermute | solution.py:20
  33.7 2.8 %collective-permute-start.2 = (bf16[2,2,1,54,128]{4,3,1,0,2:T(8,128)(2,1)S(1)}, bf16[2,2,1,54,128]{4,3,1,0,2:T(8,128)(2,1)S(1)}, u32[]{:S(2)}, u32[]{:S(2)}) collective-permute-start(bf16[2,2,1,54,128]{4,3,1,0,2:T(8,128)(2,1)S(1)} %fusion.33), channel_id=1, source_target_pairs={{0,4},{1,5},{2,6},{3,7},{4,0},{5,1},{6,2},{7,3},{8,12},{9,13},{10,... | collective-permute-start | bytes 165896 | tf_op jit(solution)/shard_map/ppermute | solution.py:20
  36.5 4.6 %collective-permute-done.2 = bf16[2,2,1,54,128]{4,3,1,0,2:T(8,128)(2,1)S(1)} collective-permute-done((bf16[2,2,1,54,128]{4,3,1,0,2:T(8,128)(2,1)S(1)}, bf16[2,2,1,54,128]{4,3,1,0,2:T(8,128)(2,1)S(1)}, u32[]{:S(2)}, u32[]{:S(2)}) %collective-permute-start.2) | collective-permute-done | bytes 55328 | tf_op jit(solution)/shard_map/ppermute | solution.py:20
  43.2 4.7 %collective-permute-done.3 = bf16[2,2,2,1,54,128]{5,4,2,1,0,3:T(8,128)(2,1)S(1)} collective-permute-done((bf16[2,2,2,1,54,128]{5,4,2,1,0,3:T(8,128)(2,1)S(1)}, bf16[2,2,2,1,54,128]{5,4,2,1,0,3:T(8,128)(2,1)S(1)}, u32[]{:S(2)}, u32[]{:S(2)}) %collective-permute-start.3) | collective-permute-done | bytes 110624 | tf_op jit(solution)/shard_map/ppermute | solution.py:20
  50.4 5.5 %collective-permute-done.4 = bf16[2,2,2,2,1,54,128]{6,5,3,2,1,0,4:T(8,128)(2,1)S(1)} collective-permute-done((bf16[2,2,2,2,1,54,128]{6,5,3,2,1,0,4:T(8,128)(2,1)S(1)}, bf16[2,2,2,2,1,54,128]{6,5,3,2,1,0,4:T(8,128)(2,1)S(1)}, u32[]{:S(2)}, u32[]{:S(2)}) %collective-permute-start.4) | collective-permute-done | bytes 221216 | tf_op jit(solution)/shard_map/ppermute | solution.py:20
  64.5 2.7 %collective-permute-start.6 = (bf16[2,4,8,8,128]{4,0,3,2,1:T(2,128)(2,1)S(1)}, bf16[2,4,8,8,128]{4,0,3,2,1:T(2,128)(2,1)S(1)}, u32[]{:S(2)}, u32[]{:S(2)}) collective-permute-start(bf16[2,4,8,8,128]{4,0,3,2,1:T(2,128)(2,1)S(1)} %fusion), channel_id=1, source_target_pairs={{64,0},{128,64},{192,128},{256,192},{320,256},{384,320},{448,384},... | collective-permute-start | bytes 393224 | tf_op jit(solution)/shard_map/ppermute | solution.py:15
  67.2 8.3 %collective-permute-done.6 = bf16[2,4,8,8,128]{4,0,3,2,1:T(2,128)(2,1)S(1)} collective-permute-done((bf16[2,4,8,8,128]{4,0,3,2,1:T(2,128)(2,1)S(1)}, bf16[2,4,8,8,128]{4,0,3,2,1:T(2,128)(2,1)S(1)}, u32[]{:S(2)}, u32[]{:S(2)}) %collective-permute-start.6) | collective-permute-done | bytes 131104 | tf_op jit(solution)/shard_map/ppermute | solution.py:15
  79.2 8.5 %collective-permute-done.7 = bf16[2,4,8,8,128]{4,0,3,2,1:T(2,128)(2,1)S(1)} collective-permute-done((bf16[2,4,8,8,128]{4,0,3,2,1:T(2,128)(2,1)S(1)}, bf16[2,4,8,8,128]{4,0,3,2,1:T(2,128)(2,1)S(1)}, u32[]{:S(2)}, u32[]{:S(2)}) %collective-permute-start.7) | collective-permute-done | bytes 131104 | tf_op jit(solution)/shard_map/ppermute | solution.py:15
  91.5 8.5 %collective-permute-done.8 = bf16[2,4,8,8,128]{4,0,3,2,1:T(2,128)(2,1)S(1)} collective-permute-done((bf16[2,4,8,8,128]{4,0,3,2,1:T(2,128)(2,1)S(1)}, bf16[2,4,8,8,128]{4,0,3,2,1:T(2,128)(2,1)S(1)}, u32[]{:S(2)}, u32[]{:S(2)}) %collective-permute-start.8) | collective-permute-done | bytes 131104 | tf_op jit(solution)/shard_map/ppermute | solution.py:15
  104.0 8.4 %collective-permute-done.9 = bf16[2,4,8,8,128]{4,0,3,2,1:T(2,128)(2,1)S(1)} collective-permute-done((bf16[2,4,8,8,128]{4,0,3,2,1:T(2,128)(2,1)S(1)}, bf16[2,4,8,8,128]{4,0,3,2,1:T(2,128)(2,1)S(1)}, u32[]{:S(2)}, u32[]{:S(2)}) %collective-permute-start.9) | collective-permute-done | bytes 131104 | tf_op jit(solution)/shard_map/ppermute | solution.py:15
  116.1 8.5 %collective-permute-done.10 = bf16[2,4,8,8,128]{4,0,3,2,1:T(2,128)(2,1)S(1)} collective-permute-done((bf16[2,4,8,8,128]{4,0,3,2,1:T(2,128)(2,1)S(1)}, bf16[2,4,8,8,128]{4,0,3,2,1:T(2,128)(2,1)S(1)}, u32[]{:S(2)}, u32[]{:S(2)}) %collective-permute-start.10) | collective-permute-done | bytes 131104 | tf_op jit(solution)/shard_map/ppermute | solution.py:15
  128.3 8.5 %collective-permute-done.11 = bf16[2,4,8,8,128]{4,0,3,2,1:T(2,128)(2,1)S(1)} collective-permute-done((bf16[2,4,8,8,128]{4,0,3,2,1:T(2,128)(2,1)S(1)}, bf16[2,4,8,8,128]{4,0,3,2,1:T(2,128)(2,1)S(1)}, u32[]{:S(2)}, u32[]{:S(2)}) %collective-permute-start.11) | collective-permute-done | bytes 131104 | tf_op jit(solution)/shard_map/ppermute | solution.py:15
  140.6 8.6 %collective-permute-done.12 = bf16[2,4,8,8,128]{4,0,3,2,1:T(2,128)(2,1)S(1)} collective-permute-done((bf16[2,4,8,8,128]{4,0,3,2,1:T(2,128)(2,1)S(1)}, bf16[2,4,8,8,128]{4,0,3,2,1:T(2,128)(2,1)S(1)}, u32[]{:S(2)}, u32[]{:S(2)}) %collective-permute-start.12) | collective-permute-done | bytes 131104 | tf_op jit(solution)/shard_map/ppermute | solution.py:15
  149.3 4.7 %fusion.24 = f32[3,3,3,128,128]{4,3,2,1,0:T(8,128)} fusion(pred[]{:T(512)S(6)} %eq.51, pred[]{:T(512)S(6)} %eq.59, pred[]{:T(512)S(6)} %eq.60, pred[]{:T(512)S(6)} %eq.61, pred[]{:T(512)S(6)} %eq.62, pred[]{:T(512)S(6)} %eq.63, pred[]{:T(512)S(6)} %eq.64, pred[]{:T(512)S(6)} %eq.52, bf16[2,4,8,8,128]{4,3,2,1,0:T(8,128)(2,1)S(1)} %bitcast.141, ...), kind=kOutput, calls=%fused_computation.79 | convolution fusion | flops 319815680 | bytes 3211272 | tf_op jit(solution)/shard_map/conv_general_dilated | solution.py:74
  159.4 2.5 %collective-permute-start.14 = (bf16[2,2,2,2,54,128]{5,4,0,1,2,3:T(8,128)(2,1)S(1)}, bf16[2,2,2,2,54,128]{5,4,0,1,2,3:T(8,128)(2,1)S(1)}, u32[]{:S(2)}, u32[]{:S(2)}) collective-permute-start(bf16[2,2,2,2,54,128]{5,4,0,1,2,3:T(8,128)(2,1)S(1)} %fusion.22), channel_id=1, source_target_pairs={{0,32},{1,33},{2,34},{3,35},{4,36},{5,37},{6,38},{7,39},{8,40},{9,... | collective-permute-start | bytes 663560 | tf_op jit(solution)/shard_map/ppermute | solution.py:20
  161.9 7.2 %collective-permute-done.14 = bf16[2,2,2,2,54,128]{5,4,0,1,2,3:T(8,128)(2,1)S(1)} collective-permute-done((bf16[2,2,2,2,54,128]{5,4,0,1,2,3:T(8,128)(2,1)S(1)}, bf16[2,2,2,2,54,128]{5,4,0,1,2,3:T(8,128)(2,1)S(1)}, u32[]{:S(2)}, u32[]{:S(2)}) %collective-permute-start.14) | collective-permute-done | bytes 221216 | tf_op jit(solution)/shard_map/ppermute | solution.py:20
  171.1 4.8 %collective-permute-done.15 = bf16[2,2,2,54,128]{4,3,0,1,2:T(8,128)(2,1)S(1)} collective-permute-done((bf16[2,2,2,54,128]{4,3,0,1,2:T(8,128)(2,1)S(1)}, bf16[2,2,2,54,128]{4,3,0,1,2:T(8,128)(2,1)S(1)}, u32[]{:S(2)}, u32[]{:S(2)}) %collective-permute-start.15) | collective-permute-done | bytes 110624 | tf_op jit(solution)/shard_map/ppermute | solution.py:20
  178.3 4.6 %collective-permute-done.16 = bf16[2,2,54,128]{3,2,0,1:T(8,128)(2,1)S(1)} collective-permute-done((bf16[2,2,54,128]{3,2,0,1:T(8,128)(2,1)S(1)}, bf16[2,2,54,128]{3,2,0,1:T(8,128)(2,1)S(1)}, u32[]{:S(2)}, u32[]{:S(2)}) %collective-permute-start.16) | collective-permute-done | bytes 55328 | tf_op jit(solution)/shard_map/ppermute | solution.py:20
  183.0 4.3 %collective-permute-start.17 = (bf16[2,54,128]{2,1,0:T(8,128)(2,1)S(1)}, bf16[2,54,128]{2,1,0:T(8,128)(2,1)S(1)}, u32[]{:S(2)}, u32[]{:S(2)}) collective-permute-start(bf16[2,54,128]{2,1,0:T(8,128)(2,1)S(1)} %fusion.35), channel_id=1, source_target_pairs={{0,8},{1,9},{2,10},{3,11},{4,12},{5,13},{6,14},{7,15},{8,0},{9,1},... | collective-permute-start | bytes 82952 | tf_op jit(solution)/shard_map/ppermute | solution.py:20
  187.3 5.6 %collective-permute-done.17 = bf16[2,54,128]{2,1,0:T(8,128)(2,1)S(1)} collective-permute-done((bf16[2,54,128]{2,1,0:T(8,128)(2,1)S(1)}, bf16[2,54,128]{2,1,0:T(8,128)(2,1)S(1)}, u32[]{:S(2)}, u32[]{:S(2)}) %collective-permute-start.17) | collective-permute-done | bytes 27680 | tf_op jit(solution)/shard_map/ppermute | solution.py:20
  192.9 8.6 %collective-permute-start.18 = (bf16[54,128]{1,0:T(8,128)(2,1)S(1)}, bf16[54,128]{1,0:T(8,128)(2,1)S(1)}, u32[]{:S(2)}, u32[]{:S(2)}) collective-permute-start(bf16[54,128]{1,0:T(8,128)(2,1)S(1)} %fusion.39), channel_id=1, source_target_pairs={{0,16},{1,17},{2,18},{3,19},{4,20},{5,21},{6,22},{7,23},{8,24},{9,... | collective-permute-start | bytes 41480 | tf_op jit(solution)/shard_map/ppermute | solution.py:20
  201.6 3.3 %fusion.9 = bf16[1,2,4,8,8,128]{5,1,4,3,2,0:T(2,128)(2,1)S(1)} fusion(bf16[3,3,3,128,128]{4,3,2,1,0:T(8,128)(2,1)S(1)} %copy-done.1, pred[]{:T(512)S(6)} %eq.51, bf16[2,4,8,8,128]{4,0,3,2,1:T(2,128)(2,1)} %copy-done.13, pred[]{:T(512)S(6)} %eq.59, bf16[2,4,8,8,128]{4,0,3,2,1:T(2,128)(2,1)} %copy-done.12, pred[]{:T(512)S(6)} %eq.60, ...), kind=kOutput, calls=%fused_computation.18 | convolution fusion | flops 318242816 | bytes 2457608 | tf_op jit(solution)/shard_map/conv_general_dilated | solution.py:66
  (102 shorter events, 55.4 us)
Async XLA Ops:
  0.6 22.0 %collective-permute-start = (bf16[1,54,128]{2,1,0:T(8,128)(2,1)}, bf16[1,54,128]{2,1,0:T(8,128)(2,1)S(1)}, u32[]{:S(2)}, u32[]{:S(2)}) collective-permute-start(bf16[1,54,128]{2,1,0:T(8,128)(2,1)} %param.6), channel_id=1, source_target_pairs={{0,16},{1,17},{2,18},{3,19},{4,20},{5,21},{6,22},{7,23},{8,24},{9,... | collective-permute-start | bytes 41480 | tf_op jit(solution)/shard_map/ppermute | solution.py:20
  23.4 10.2 %collective-permute-start.1 = (bf16[2,1,54,128]{3,2,0,1:T(8,128)(2,1)S(1)}, bf16[2,1,54,128]{3,2,0,1:T(8,128)(2,1)S(1)}, u32[]{:S(2)}, u32[]{:S(2)}) collective-permute-start(bf16[2,1,54,128]{3,2,0,1:T(8,128)(2,1)S(1)} %fusion.38), channel_id=1, source_target_pairs={{0,8},{1,9},{2,10},{3,11},{4,12},{5,13},{6,14},{7,15},{8,0},{9,1},... | collective-permute-start | bytes 82952 | tf_op jit(solution)/shard_map/ppermute | solution.py:20
  33.7 7.5 %collective-permute-start.2 = (bf16[2,2,1,54,128]{4,3,1,0,2:T(8,128)(2,1)S(1)}, bf16[2,2,1,54,128]{4,3,1,0,2:T(8,128)(2,1)S(1)}, u32[]{:S(2)}, u32[]{:S(2)}) collective-permute-start(bf16[2,2,1,54,128]{4,3,1,0,2:T(8,128)(2,1)S(1)} %fusion.33), channel_id=1, source_target_pairs={{0,4},{1,5},{2,6},{3,7},{4,0},{5,1},{6,2},{7,3},{8,12},{9,13},{10,... | collective-permute-start | bytes 165896 | tf_op jit(solution)/shard_map/ppermute | solution.py:20
  41.2 6.7 %collective-permute-start.3 = (bf16[2,2,2,1,54,128]{5,4,2,1,0,3:T(8,128)(2,1)S(1)}, bf16[2,2,2,1,54,128]{5,4,2,1,0,3:T(8,128)(2,1)S(1)}, u32[]{:S(2)}, u32[]{:S(2)}) collective-permute-start(bf16[2,2,2,1,54,128]{5,4,2,1,0,3:T(8,128)(2,1)S(1)} %fusion.27), channel_id=1, source_target_pairs={{0,2},{1,3},{2,0},{3,1},{4,6},{5,7},{6,4},{7,5},{8,10},{9,11},{10,... | collective-permute-start | bytes 331784 | tf_op jit(solution)/shard_map/ppermute | solution.py:20
  48.0 7.9 %collective-permute-start.4 = (bf16[2,2,2,2,1,54,128]{6,5,3,2,1,0,4:T(8,128)(2,1)S(1)}, bf16[2,2,2,2,1,54,128]{6,5,3,2,1,0,4:T(8,128)(2,1)S(1)}, u32[]{:S(2)}, u32[]{:S(2)}) collective-permute-start(bf16[2,2,2,2,1,54,128]{6,5,3,2,1,0,4:T(8,128)(2,1)S(1)} %fusion.23), channel_id=1, source_target_pairs={{0,32},{1,33},{2,34},{3,35},{4,36},{5,37},{6,38},{7,39},{8,40},{9,... | collective-permute-start | bytes 663560 | tf_op jit(solution)/shard_map/ppermute | solution.py:20
  56.0 3.7 %collective-permute-start.5 = (bf16[2,2,2,2,2,1,54,128]{7,6,4,3,2,1,0,5:T(8,128)(2,1)S(1)}, bf16[2,2,2,2,2,1,54,128]{7,6,4,3,2,1,0,5:T(8,128)(2,1)S(1)}, u32[]{:S(2)}, u32[]{:S(2)}) collective-permute-start(bf16[2,2,2,2,2,1,54,128]{7,6,4,3,2,1,0,5:T(8,128)(2,1)S(1)} %fusion.12), channel_id=1, source_target_pairs={{0,1},{1,0},{2,3},{3,2},{4,5},{5,4},{6,7},{7,6},{8,9},{9,8},{10,11... | collective-permute-start | bytes 1327112 | tf_op jit(solution)/shard_map/ppermute | solution.py:20
  60.3 76.6 %copy-start = (bf16[3,3,3,128,128]{4,3,2,1,0:T(8,128)(2,1)}, bf16[3,3,3,128,128]{4,3,2,1,0:T(8,128)(2,1)S(1)}, u32[]{:S(2)}) copy-start(bf16[3,3,3,128,128]{4,3,2,1,0:T(8,128)(2,1)S(1)} %reshape_reshape.6) | copy-start | bytes 2654212
  62.8 86.5 %copy-start.15 = (f32[2,4,8,8,128]{4,0,3,2,1:T(2,128)}, f32[2,4,8,8,128]{4,0,3,2,1:T(2,128)S(1)}, u32[]{:S(2)}) copy-start(f32[2,4,8,8,128]{4,0,3,2,1:T(2,128)S(1)} %add_multiply_fusion) | copy-start | bytes 786436
  64.5 11.0 %collective-permute-start.6 = (bf16[2,4,8,8,128]{4,0,3,2,1:T(2,128)(2,1)S(1)}, bf16[2,4,8,8,128]{4,0,3,2,1:T(2,128)(2,1)S(1)}, u32[]{:S(2)}, u32[]{:S(2)}) collective-permute-start(bf16[2,4,8,8,128]{4,0,3,2,1:T(2,128)(2,1)S(1)} %fusion), channel_id=1, source_target_pairs={{64,0},{128,64},{192,128},{256,192},{320,256},{384,320},{448,384},... | collective-permute-start | bytes 393224 | tf_op jit(solution)/shard_map/ppermute | solution.py:15
  77.3 10.5 %collective-permute-start.7 = (bf16[2,4,8,8,128]{4,0,3,2,1:T(2,128)(2,1)S(1)}, bf16[2,4,8,8,128]{4,0,3,2,1:T(2,128)(2,1)S(1)}, u32[]{:S(2)}, u32[]{:S(2)}) collective-permute-start(bf16[2,4,8,8,128]{4,0,3,2,1:T(2,128)(2,1)S(1)} %fusion.1), channel_id=1, source_target_pairs={{64,0},{128,64},{192,128},{256,192},{320,256},{384,320},{448,384},... | collective-permute-start | bytes 393224 | tf_op jit(solution)/shard_map/ppermute | solution.py:15
  89.6 10.5 %collective-permute-start.8 = (bf16[2,4,8,8,128]{4,0,3,2,1:T(2,128)(2,1)S(1)}, bf16[2,4,8,8,128]{4,0,3,2,1:T(2,128)(2,1)S(1)}, u32[]{:S(2)}, u32[]{:S(2)}) collective-permute-start(bf16[2,4,8,8,128]{4,0,3,2,1:T(2,128)(2,1)S(1)} %fusion.2), channel_id=1, source_target_pairs={{64,0},{128,64},{192,128},{256,192},{320,256},{384,320},{448,384},... | collective-permute-start | bytes 393224 | tf_op jit(solution)/shard_map/ppermute | solution.py:15
  101.9 10.5 %collective-permute-start.9 = (bf16[2,4,8,8,128]{4,0,3,2,1:T(2,128)(2,1)S(1)}, bf16[2,4,8,8,128]{4,0,3,2,1:T(2,128)(2,1)S(1)}, u32[]{:S(2)}, u32[]{:S(2)}) collective-permute-start(bf16[2,4,8,8,128]{4,0,3,2,1:T(2,128)(2,1)S(1)} %fusion.3), channel_id=1, source_target_pairs={{64,0},{128,64},{192,128},{256,192},{320,256},{384,320},{448,384},... | collective-permute-start | bytes 393224 | tf_op jit(solution)/shard_map/ppermute | solution.py:15
  114.1 10.5 %collective-permute-start.10 = (bf16[2,4,8,8,128]{4,0,3,2,1:T(2,128)(2,1)S(1)}, bf16[2,4,8,8,128]{4,0,3,2,1:T(2,128)(2,1)S(1)}, u32[]{:S(2)}, u32[]{:S(2)}) collective-permute-start(bf16[2,4,8,8,128]{4,0,3,2,1:T(2,128)(2,1)S(1)} %fusion.4), channel_id=1, source_target_pairs={{64,0},{128,64},{192,128},{256,192},{320,256},{384,320},{448,384},... | collective-permute-start | bytes 393224 | tf_op jit(solution)/shard_map/ppermute | solution.py:15
  126.4 10.5 %collective-permute-start.11 = (bf16[2,4,8,8,128]{4,0,3,2,1:T(2,128)(2,1)S(1)}, bf16[2,4,8,8,128]{4,0,3,2,1:T(2,128)(2,1)S(1)}, u32[]{:S(2)}, u32[]{:S(2)}) collective-permute-start(bf16[2,4,8,8,128]{4,0,3,2,1:T(2,128)(2,1)S(1)} %fusion.5), channel_id=1, source_target_pairs={{64,0},{128,64},{192,128},{256,192},{320,256},{384,320},{448,384},... | collective-permute-start | bytes 393224 | tf_op jit(solution)/shard_map/ppermute | solution.py:15
  138.7 10.6 %collective-permute-start.12 = (bf16[2,4,8,8,128]{4,0,3,2,1:T(2,128)(2,1)S(1)}, bf16[2,4,8,8,128]{4,0,3,2,1:T(2,128)(2,1)S(1)}, u32[]{:S(2)}, u32[]{:S(2)}) collective-permute-start(bf16[2,4,8,8,128]{4,0,3,2,1:T(2,128)(2,1)S(1)} %fusion.6), channel_id=1, source_target_pairs={{64,0},{128,64},{192,128},{256,192},{320,256},{384,320},{448,384},... | collective-permute-start | bytes 393224 | tf_op jit(solution)/shard_map/ppermute | solution.py:15
  155.5 3.7 %collective-permute-start.13 = (bf16[2,2,2,2,2,54,128]{6,5,1,2,3,4,0:T(8,128)(2,1)S(1)}, bf16[2,2,2,2,2,54,128]{6,5,1,2,3,4,0:T(8,128)(2,1)S(1)}, u32[]{:S(2)}, u32[]{:S(2)}) collective-permute-start(bf16[2,2,2,2,2,54,128]{6,5,1,2,3,4,0:T(8,128)(2,1)S(1)} %fusion.11), channel_id=1, source_target_pairs={{0,1},{1,0},{2,3},{3,2},{4,5},{5,4},{6,7},{7,6},{8,9},{9,8},{10,11... | collective-permute-start | bytes 1327112 | tf_op jit(solution)/shard_map/ppermute | solution.py:20
  159.3 42.2 %copy-start.1 = (bf16[3,3,3,128,128]{4,3,2,1,0:T(8,128)(2,1)S(1)}, bf16[3,3,3,128,128]{4,3,2,1,0:T(8,128)(2,1)}, u32[]{:S(2)}) copy-start(bf16[3,3,3,128,128]{4,3,2,1,0:T(8,128)(2,1)} %copy-done) | copy-start | bytes 2654212
  159.3 42.2 %copy-start.5 = (bf16[2,4,8,8,128]{4,0,3,2,1:T(2,128)(2,1)S(1)}, bf16[2,4,8,8,128]{4,0,3,2,1:T(2,128)(2,1)}, u32[]{:S(2)}) copy-start(bf16[2,4,8,8,128]{4,0,3,2,1:T(2,128)(2,1)} %copy-done.4) | copy-start | bytes 393220
  159.3 42.2 %copy-start.7 = (bf16[2,4,8,8,128]{4,0,3,2,1:T(2,128)(2,1)S(1)}, bf16[2,4,8,8,128]{4,0,3,2,1:T(2,128)(2,1)}, u32[]{:S(2)}) copy-start(bf16[2,4,8,8,128]{4,0,3,2,1:T(2,128)(2,1)} %copy-done.6) | copy-start | bytes 393220
  159.4 9.7 %collective-permute-start.14 = (bf16[2,2,2,2,54,128]{5,4,0,1,2,3:T(8,128)(2,1)S(1)}, bf16[2,2,2,2,54,128]{5,4,0,1,2,3:T(8,128)(2,1)S(1)}, u32[]{:S(2)}, u32[]{:S(2)}) collective-permute-start(bf16[2,2,2,2,54,128]{5,4,0,1,2,3:T(8,128)(2,1)S(1)} %fusion.22), channel_id=1, source_target_pairs={{0,32},{1,33},{2,34},{3,35},{4,36},{5,37},{6,38},{7,39},{8,40},{9,... | collective-permute-start | bytes 663560 | tf_op jit(solution)/shard_map/ppermute | solution.py:20
  169.2 6.7 %collective-permute-start.15 = (bf16[2,2,2,54,128]{4,3,0,1,2:T(8,128)(2,1)S(1)}, bf16[2,2,2,54,128]{4,3,0,1,2:T(8,128)(2,1)S(1)}, u32[]{:S(2)}, u32[]{:S(2)}) collective-permute-start(bf16[2,2,2,54,128]{4,3,0,1,2:T(8,128)(2,1)S(1)} %fusion.26), channel_id=1, source_target_pairs={{0,2},{1,3},{2,0},{3,1},{4,6},{5,7},{6,4},{7,5},{8,10},{9,11},{10,... | collective-permute-start | bytes 331784 | tf_op jit(solution)/shard_map/ppermute | solution.py:20
  175.9 7.0 %collective-permute-start.16 = (bf16[2,2,54,128]{3,2,0,1:T(8,128)(2,1)S(1)}, bf16[2,2,54,128]{3,2,0,1:T(8,128)(2,1)S(1)}, u32[]{:S(2)}, u32[]{:S(2)}) collective-permute-start(bf16[2,2,54,128]{3,2,0,1:T(8,128)(2,1)S(1)} %fusion.32), channel_id=1, source_target_pairs={{0,4},{1,5},{2,6},{3,7},{4,0},{5,1},{6,2},{7,3},{8,12},{9,13},{10,... | collective-permute-start | bytes 165896 | tf_op jit(solution)/shard_map/ppermute | solution.py:20
  183.0 9.9 %collective-permute-start.17 = (bf16[2,54,128]{2,1,0:T(8,128)(2,1)S(1)}, bf16[2,54,128]{2,1,0:T(8,128)(2,1)S(1)}, u32[]{:S(2)}, u32[]{:S(2)}) collective-permute-start(bf16[2,54,128]{2,1,0:T(8,128)(2,1)S(1)} %fusion.35), channel_id=1, source_target_pairs={{0,8},{1,9},{2,10},{3,11},{4,12},{5,13},{6,14},{7,15},{8,0},{9,1},... | collective-permute-start | bytes 82952 | tf_op jit(solution)/shard_map/ppermute | solution.py:20
  192.9 14.3 %collective-permute-start.18 = (bf16[54,128]{1,0:T(8,128)(2,1)S(1)}, bf16[54,128]{1,0:T(8,128)(2,1)S(1)}, u32[]{:S(2)}, u32[]{:S(2)}) collective-permute-start(bf16[54,128]{1,0:T(8,128)(2,1)S(1)} %fusion.39), channel_id=1, source_target_pairs={{0,16},{1,17},{2,18},{3,19},{4,20},{5,21},{6,22},{7,23},{8,24},{9,... | collective-permute-start | bytes 41480 | tf_op jit(solution)/shard_map/ppermute | solution.py:20
  (11 other events, 179.1 us)

commit v4 on v1

--- a/solution.py
+++ b/solution.py
@@ -13,6 +13,62 @@
     length = lax.axis_size(axis)
     pairs = [(i, i + by) for i in range(length) if 0 <= i + by < length]
     return lax.ppermute(array, axis, pairs)
+
+
+def exchanged(array, axis, mask):
+    length = lax.axis_size(axis)
+    return lax.ppermute(array, axis, [(i, i ^ mask) for i in range(length)])
+
+
+def bit_count(length):
+    return length.bit_length() - 1
+
+
+def group_value(index, group):
+    width = len(group)
+    return sum(((index >> bit) & 1) << (width - 1 - j) for j, bit in enumerate(group))
+
+
+def group_mask(value, group):
+    width = len(group)
+    return sum(((value >> (width - 1 - j)) & 1) << bit for j, bit in enumerate(group))
+
+
+def gather_by_groups(block, axis, groups):
+    index = lax.axis_index(axis)
+    held = block
+    for group in groups:
+        count = 1 << len(group)
+        mine = group_value(index, group)
+        pieces = [held] + [exchanged(held, axis, group_mask(m, group)) for m in range(1, count)]
+        joined = jnp.zeros((count,) + held.shape, held.dtype)
+        for m, piece in enumerate(pieces):
+            joined = lax.dynamic_update_index_in_dim(joined, piece, mine ^ m, 0)
+        held = joined
+    order = [bit for group in groups[::-1] for bit in group]
+    held = held.reshape((2,) * len(order) + block.shape)
+    natural = [order.index(bit) for bit in range(len(order) - 1, -1, -1)]
+    held = jnp.transpose(held, natural + list(range(len(order), held.ndim)))
+    return held.reshape((-1,) + block.shape[1:])
+
+
+def reduce_by_groups(chunks, axis, groups):
+    index = lax.axis_index(axis)
+    order = [bit for group in groups for bit in group]
+    done = len(order)
+    held = chunks.reshape((2,) * done + chunks.shape[1:])
+    held = jnp.transpose(held, [done - 1 - bit for bit in order] + list(range(done, held.ndim)))
+    held = held.reshape(tuple(1 << len(group) for group in groups) + chunks.shape[1:])
+    for group in groups:
+        count = 1 << len(group)
+        mine = group_value(index, group)
+        total = lax.dynamic_index_in_dim(held, mine, 0, keepdims=False)
+        for m in range(1, count):
+            sent = lax.dynamic_index_in_dim(held, mine ^ m, 0, keepdims=False)
+            received = exchanged(sent.astype(jnp.bfloat16), axis, group_mask(m, group))
+            total = total + received.astype(jnp.float32)
+        held = total
+    return held.reshape((1,) + chunks.shape[1:])
 
 
 def conv_forward(field, kernel):
@@ -58,7 +114,9 @@
     dp_count = lax.axis_size("dp")
     segment_index = lax.axis_index("segment")
     channels = weights.shape[2]
-    gathered = lax.all_gather(weights, "dp", axis=0, tiled=True)
+    bits = bit_count(dp_count)
+    gather_groups = [list(range(bits - 2, 1, -1)), [1, bits - 1, 0]]
+    gathered = gather_by_groups(weights[0][None], "dp", gather_groups)
     kernel = gathered.reshape(3, 3, 3, channels, channels)
     fields = acts[0]
     micro_count, size_x, size_y, size_z = fields.shape[:4]
@@ -86,7 +144,7 @@
             incoming = passed_along(down_grad, "segment", -1)
 
     grad_term = conv_kernel_grad(fields, slope_held).reshape(dp_count, -1, channels)
-    reduced = lax.psum_scatter(grad_term, "dp", scatter_dimension=0, tiled=True)
+    reduced = reduce_by_groups(grad_term, "dp", [group[::-1] for group in gather_groups[::-1]])
     scale_factor = 1.0 / math.sqrt(dp_count * micro_count * cell_count)
     return (grads_held[None], reduced * scale_factor)
 

time: 407 us -> 256 us (0.63)
  the two profiles are of different devices: /device:TPU:2 before, /device:TPU:6 now
where the time goes in v4:
time: 256 us; the launch traced here: 254 us
  starting transfers between devices  134 us (52%)
  waiting for transfers between devices  79.6 us (31%)
  matrix products  22.1 us (9%)
  local copies, waits for them, and re-layouts  11.7 us (5%)
  other arithmetic  5.48 us (2%)
    ppermute x28, starting transfers between devices, exchanged(): return lax.ppermute(array, axis, [(i, i ^ mask) for i in range(length)])  119 us
    ppermute x7, waiting for transfers between devices, passed_along(): return lax.ppermute(array, axis, pairs)  59.8 us
    ppermute x28, waiting for transfers between devices, exchanged(): return lax.ppermute(array, axis, [(i, i ^ mask) for i in range(length)])  19.8 us
    conv_general_dilated x8, matrix products, conv_transposed(): lax.conv_general_dilated(slope, flipped, (1, 1, 1), [(1, 1)] * 3, dimensi...  15.5 us
    ppermute x7, starting transfers between devices, passed_along(): return lax.ppermute(array, axis, pairs)  14.7 us
  transfers between devices with their start and end apart: 35, of which 13 were waited for; matrix products, arithmetic and copies ran while one was open for 5% of the time, Pallas kernels for 0%

profile of v4, /device:TPU:6, one launch (start us, length us, event | category | flops | bytes accessed | tf_op | source)
XLA Modules:
  0.0 254.4 jit_solution(9322689359714662804)
XLA Ops:
  0.6 5.2 %collective-permute-start = (bf16[1,54,128]{2,1,0:T(8,128)(2,1)}, bf16[1,54,128]{2,1,0:T(8,128)(2,1)S(1)}, u32[]{:S(2)}, u32[]{:S(2)}) collective-permute-start(bf16[1,54,128]{2,1,0:T(8,128)(2,1)} %param.6), channel_id=1, source_target_pairs={{0,4},{1,5},{2,6},{3,7},{4,0},{5,1},{6,2},{7,3},{8,12},{9,13},{10,... | collective-permute-start | bytes 41480 | tf_op jit(solution)/shard_map/ppermute | solution.py:20
  5.8 9.1 %collective-permute-start.1 = (bf16[1,54,128]{2,1,0:T(8,128)(2,1)}, bf16[1,54,128]{2,1,0:T(8,128)(2,1)S(1)}, u32[]{:S(2)}, u32[]{:S(2)}) collective-permute-start(bf16[1,54,128]{2,1,0:T(8,128)(2,1)} %param.6), channel_id=1, source_target_pairs={{0,8},{1,9},{2,10},{3,11},{4,12},{5,13},{6,14},{7,15},{8,0},{9,1},... | collective-permute-start | bytes 41480 | tf_op jit(solution)/shard_map/ppermute | solution.py:20
  16.9 13.5 %collective-permute-start.3 = (bf16[1,54,128]{2,1,0:T(8,128)(2,1)}, bf16[1,54,128]{2,1,0:T(8,128)(2,1)S(1)}, u32[]{:S(2)}, u32[]{:S(2)}) collective-permute-start(bf16[1,54,128]{2,1,0:T(8,128)(2,1)} %param.6), channel_id=1, source_target_pairs={{0,16},{1,17},{2,18},{3,19},{4,20},{5,21},{6,22},{7,23},{8,24},{9,... | collective-permute-start | bytes 41480 | tf_op jit(solution)/shard_map/ppermute | solution.py:20
  39.0 8.8 %collective-permute-start.5 = (bf16[1,54,128]{2,1,0:T(8,128)(2,1)}, bf16[1,54,128]{2,1,0:T(8,128)(2,1)S(1)}, u32[]{:S(2)}, u32[]{:S(2)}) collective-permute-start(bf16[1,54,128]{2,1,0:T(8,128)(2,1)} %param.6), channel_id=1, source_target_pairs={{0,24},{1,25},{2,26},{3,27},{4,28},{5,29},{6,30},{7,31},{8,16},{9,... | collective-permute-start | bytes 41480 | tf_op jit(solution)/shard_map/ppermute | solution.py:20
  51.0 4.6 %collective-permute-done.6 = bf16[1,54,128]{2,1,0:T(8,128)(2,1)S(1)} collective-permute-done((bf16[1,54,128]{2,1,0:T(8,128)(2,1)}, bf16[1,54,128]{2,1,0:T(8,128)(2,1)S(1)}, u32[]{:S(2)}, u32[]{:S(2)}) %collective-permute-start.6) | collective-permute-done | bytes 13856 | tf_op jit(solution)/shard_map/ppermute | solution.py:20
  58.5 3.5 %collective-permute-start.8 = (bf16[8,1,54,128]{3,0,2,1:T(8,128)(2,1)S(1)}, bf16[8,1,54,128]{3,0,2,1:T(8,128)(2,1)S(1)}, u32[]{:S(2)}, u32[]{:S(2)}) collective-permute-start(bf16[8,1,54,128]{3,0,2,1:T(8,128)(2,1)S(1)} %dynamic_update_slice.57), channel_id=1, source_target_pairs={{0,32},{1,33},{2,34},{3,35},{4,36},{5,37},{6,38},{7,39},{8,40},{9,... | collective-permute-start | bytes 331784 | tf_op jit(solution)/shard_map/ppermute | solution.py:20
  69.8 3.9 %collective-permute-start.12 = (bf16[8,1,54,128]{3,0,2,1:T(8,128)(2,1)S(1)}, bf16[8,1,54,128]{3,0,2,1:T(8,128)(2,1)S(1)}, u32[]{:S(2)}, u32[]{:S(2)}) collective-permute-start(bf16[8,1,54,128]{3,0,2,1:T(8,128)(2,1)S(1)} %dynamic_update_slice.57), channel_id=1, source_target_pairs={{0,34},{1,35},{2,32},{3,33},{4,38},{5,39},{6,36},{7,37},{8,42},{9,... | collective-permute-start | bytes 331784 | tf_op jit(solution)/shard_map/ppermute | solution.py:20
  78.1 3.6 %collective-permute-done.13 = bf16[8,1,54,128]{3,0,2,1:T(8,128)(2,1)S(1)} collective-permute-done((bf16[8,1,54,128]{3,0,2,1:T(8,128)(2,1)S(1)}, bf16[8,1,54,128]{3,0,2,1:T(8,128)(2,1)S(1)}, u32[]{:S(2)}, u32[]{:S(2)}) %collective-permute-start.13) | collective-permute-done | bytes 110624 | tf_op jit(solution)/shard_map/ppermute | solution.py:20
  89.0 8.3 %collective-permute-done.14 = bf16[2,4,8,8,128]{4,0,3,2,1:T(2,128)(2,1)S(1)} collective-permute-done((bf16[2,4,8,8,128]{4,0,3,2,1:T(2,128)(2,1)S(1)}, bf16[2,4,8,8,128]{4,0,3,2,1:T(2,128)(2,1)S(1)}, u32[]{:S(2)}, u32[]{:S(2)}) %collective-permute-start.14) | collective-permute-done | bytes 131104 | tf_op jit(solution)/shard_map/ppermute | solution.py:15
  101.0 8.5 %collective-permute-done.15 = bf16[2,4,8,8,128]{4,0,3,2,1:T(2,128)(2,1)S(1)} collective-permute-done((bf16[2,4,8,8,128]{4,0,3,2,1:T(2,128)(2,1)S(1)}, bf16[2,4,8,8,128]{4,0,3,2,1:T(2,128)(2,1)S(1)}, u32[]{:S(2)}, u32[]{:S(2)}) %collective-permute-start.15) | collective-permute-done | bytes 131104 | tf_op jit(solution)/shard_map/ppermute | solution.py:15
  113.4 8.4 %collective-permute-done.16 = bf16[2,4,8,8,128]{4,0,3,2,1:T(2,128)(2,1)S(1)} collective-permute-done((bf16[2,4,8,8,128]{4,0,3,2,1:T(2,128)(2,1)S(1)}, bf16[2,4,8,8,128]{4,0,3,2,1:T(2,128)(2,1)S(1)}, u32[]{:S(2)}, u32[]{:S(2)}) %collective-permute-start.16) | collective-permute-done | bytes 131104 | tf_op jit(solution)/shard_map/ppermute | solution.py:15
  125.5 8.5 %collective-permute-done.17 = bf16[2,4,8,8,128]{4,0,3,2,1:T(2,128)(2,1)S(1)} collective-permute-done((bf16[2,4,8,8,128]{4,0,3,2,1:T(2,128)(2,1)S(1)}, bf16[2,4,8,8,128]{4,0,3,2,1:T(2,128)(2,1)S(1)}, u32[]{:S(2)}, u32[]{:S(2)}) %collective-permute-start.17) | collective-permute-done | bytes 131104 | tf_op jit(solution)/shard_map/ppermute | solution.py:15
  137.7 8.5 %collective-permute-done.18 = bf16[2,4,8,8,128]{4,0,3,2,1:T(2,128)(2,1)S(1)} collective-permute-done((bf16[2,4,8,8,128]{4,0,3,2,1:T(2,128)(2,1)S(1)}, bf16[2,4,8,8,128]{4,0,3,2,1:T(2,128)(2,1)S(1)}, u32[]{:S(2)}, u32[]{:S(2)}) %collective-permute-start.18) | collective-permute-done | bytes 131104 | tf_op jit(solution)/shard_map/ppermute | solution.py:15
  150.0 8.5 %collective-permute-done.19 = bf16[2,4,8,8,128]{4,0,3,2,1:T(2,128)(2,1)S(1)} collective-permute-done((bf16[2,4,8,8,128]{4,0,3,2,1:T(2,128)(2,1)S(1)}, bf16[2,4,8,8,128]{4,0,3,2,1:T(2,128)(2,1)S(1)}, u32[]{:S(2)}, u32[]{:S(2)}) %collective-permute-start.19) | collective-permute-done | bytes 131104 | tf_op jit(solution)/shard_map/ppermute | solution.py:15
  162.5 9.0 %collective-permute-done.20 = bf16[2,4,8,8,128]{4,0,3,2,1:T(2,128)(2,1)S(1)} collective-permute-done((bf16[2,4,8,8,128]{4,0,3,2,1:T(2,128)(2,1)S(1)}, bf16[2,4,8,8,128]{4,0,3,2,1:T(2,128)(2,1)S(1)}, u32[]{:S(2)}, u32[]{:S(2)}) %collective-permute-start.20) | collective-permute-done | bytes 131104 | tf_op jit(solution)/shard_map/ppermute | solution.py:15
  172.2 4.7 %fusion.24 = f32[3,3,3,128,128]{4,3,2,1,0:T(8,128)} fusion(pred[]{:T(512)S(6)} %eq.33, pred[]{:T(512)S(6)} %eq.35, pred[]{:T(512)S(6)} %eq.36, pred[]{:T(512)S(6)} %eq.37, pred[]{:T(512)S(6)} %eq.38, pred[]{:T(512)S(6)} %eq.39, pred[]{:T(512)S(6)} %eq.40, pred[]{:T(512)S(6)} %eq.34, bf16[2,4,8,8,128]{4,3,2,1,0:T(8,128)(2,1)S(1)} %bitcast.160, ...), kind=kOutput, calls=%fused_computation.73 | convolution fusion | flops 319815680 | bytes 3211272 | tf_op jit(solution)/shard_map/conv_general_dilated | solution.py:92
  183.0 4.1 %collective-permute-start.26 = (bf16[8,54,128]{2,0,1:T(8,128)(2,1)S(1)}, bf16[8,54,128]{2,0,1:T(8,128)(2,1)S(1)}, u32[]{:S(2)}, u32[]{:S(2)}) collective-permute-start(bf16[8,54,128]{2,0,1:T(8,128)(2,1)S(1)} %get-tuple-element.24), channel_id=1, source_target_pairs={{0,33},{1,32},{2,35},{3,34},{4,37},{5,36},{6,39},{7,38},{8,41},{9,... | collective-permute-start | bytes 331784 | tf_op jit(solution)/shard_map/ppermute | solution.py:20
  194.9 3.5 %collective-permute-start.22 = (bf16[8,54,128]{2,0,1:T(8,128)(2,1)S(1)}, bf16[8,54,128]{2,0,1:T(8,128)(2,1)S(1)}, u32[]{:S(2)}, u32[]{:S(2)}) collective-permute-start(bf16[8,54,128]{2,0,1:T(8,128)(2,1)S(1)} %get-tuple-element.28), channel_id=1, source_target_pairs={{0,32},{1,33},{2,34},{3,35},{4,36},{5,37},{6,38},{7,39},{8,40},{9,... | collective-permute-start | bytes 331784 | tf_op jit(solution)/shard_map/ppermute | solution.py:20
  208.2 6.9 %collective-permute-start.33 = (bf16[54,128]{1,0:T(8,128)(2,1)S(1)}, bf16[54,128]{1,0:T(8,128)(2,1)S(1)}, u32[]{:S(2)}, u32[]{:S(2)}) collective-permute-start(bf16[54,128]{1,0:T(8,128)(2,1)S(1)} %bitcast.152), channel_id=1, source_target_pairs={{0,12},{1,13},{2,14},{3,15},{4,8},{5,9},{6,10},{7,11},{8,4},{9,5},... | collective-permute-start | bytes 41480 | tf_op jit(solution)/shard_map/ppermute | solution.py:20
  219.1 9.1 %collective-permute-start.32 = (bf16[54,128]{1,0:T(8,128)(2,1)S(1)}, bf16[54,128]{1,0:T(8,128)(2,1)S(1)}, u32[]{:S(2)}, u32[]{:S(2)}) collective-permute-start(bf16[54,128]{1,0:T(8,128)(2,1)S(1)} %bitcast.154), channel_id=1, source_target_pairs={{0,20},{1,21},{2,22},{3,23},{4,16},{5,17},{6,18},{7,19},{8,28},{9,... | collective-permute-start | bytes 41480 | tf_op jit(solution)/shard_map/ppermute | solution.py:20
  230.2 5.2 %collective-permute-start.30 = (bf16[54,128]{1,0:T(8,128)(2,1)S(1)}, bf16[54,128]{1,0:T(8,128)(2,1)S(1)}, u32[]{:S(2)}, u32[]{:S(2)}) collective-permute-start(bf16[54,128]{1,0:T(8,128)(2,1)S(1)} %bitcast.156), channel_id=1, source_target_pairs={{0,24},{1,25},{2,26},{3,27},{4,28},{5,29},{6,30},{7,31},{8,16},{9,... | collective-permute-start | bytes 41480 | tf_op jit(solution)/shard_map/ppermute | solution.py:20
  235.4 4.0 %collective-permute-start.29 = (bf16[54,128]{1,0:T(8,128)(2,1)S(1)}, bf16[54,128]{1,0:T(8,128)(2,1)S(1)}, u32[]{:S(2)}, u32[]{:S(2)}) collective-permute-start(bf16[54,128]{1,0:T(8,128)(2,1)S(1)} %bitcast.158), channel_id=1, source_target_pairs={{0,8},{1,9},{2,10},{3,11},{4,12},{5,13},{6,14},{7,15},{8,0},{9,1},... | collective-permute-start | bytes 41480 | tf_op jit(solution)/shard_map/ppermute | solution.py:20
  239.4 7.8 %collective-permute-start.28 = (bf16[54,128]{1,0:T(8,128)(2,1)S(1)}, bf16[54,128]{1,0:T(8,128)(2,1)S(1)}, u32[]{:S(2)}, u32[]{:S(2)}) collective-permute-start(bf16[54,128]{1,0:T(8,128)(2,1)S(1)} %bitcast.157), channel_id=1, source_target_pairs={{0,16},{1,17},{2,18},{3,19},{4,20},{5,21},{6,22},{7,23},{8,24},{9,... | collective-permute-start | bytes 41480 | tf_op jit(solution)/shard_map/ppermute | solution.py:20
  247.3 6.4 %collective-permute-done.28 = bf16[54,128]{1,0:T(8,128)(2,1)S(1)} collective-permute-done((bf16[54,128]{1,0:T(8,128)(2,1)S(1)}, bf16[54,128]{1,0:T(8,128)(2,1)S(1)}, u32[]{:S(2)}, u32[]{:S(2)}) %collective-permute-start.28) | collective-permute-done | bytes 13856 | tf_op jit(solution)/shard_map/ppermute | solution.py:20
  (132 shorter events, 88.9 us)
Async XLA Ops:
  0.6 38.3 %collective-permute-start = (bf16[1,54,128]{2,1,0:T(8,128)(2,1)}, bf16[1,54,128]{2,1,0:T(8,128)(2,1)S(1)}, u32[]{:S(2)}, u32[]{:S(2)}) collective-permute-start(bf16[1,54,128]{2,1,0:T(8,128)(2,1)} %param.6), channel_id=1, source_target_pairs={{0,4},{1,5},{2,6},{3,7},{4,0},{5,1},{6,2},{7,3},{8,12},{9,13},{10,... | collective-permute-start | bytes 41480 | tf_op jit(solution)/shard_map/ppermute | solution.py:20
  5.8 41.9 %collective-permute-start.1 = (bf16[1,54,128]{2,1,0:T(8,128)(2,1)}, bf16[1,54,128]{2,1,0:T(8,128)(2,1)S(1)}, u32[]{:S(2)}, u32[]{:S(2)}) collective-permute-start(bf16[1,54,128]{2,1,0:T(8,128)(2,1)} %param.6), channel_id=1, source_target_pairs={{0,8},{1,9},{2,10},{3,11},{4,12},{5,13},{6,14},{7,15},{8,0},{9,1},... | collective-permute-start | bytes 41480 | tf_op jit(solution)/shard_map/ppermute | solution.py:20
  14.9 36.0 %collective-permute-start.2 = (bf16[1,54,128]{2,1,0:T(8,128)(2,1)}, bf16[1,54,128]{2,1,0:T(8,128)(2,1)S(1)}, u32[]{:S(2)}, u32[]{:S(2)}) collective-permute-start(bf16[1,54,128]{2,1,0:T(8,128)(2,1)} %param.6), channel_id=1, source_target_pairs={{0,12},{1,13},{2,14},{3,15},{4,8},{5,9},{6,10},{7,11},{8,4},{9,5},... | collective-permute-start | bytes 41480 | tf_op jit(solution)/shard_map/ppermute | solution.py:20
  16.9 34.1 %collective-permute-start.3 = (bf16[1,54,128]{2,1,0:T(8,128)(2,1)}, bf16[1,54,128]{2,1,0:T(8,128)(2,1)S(1)}, u32[]{:S(2)}, u32[]{:S(2)}) collective-permute-start(bf16[1,54,128]{2,1,0:T(8,128)(2,1)} %param.6), channel_id=1, source_target_pairs={{0,16},{1,17},{2,18},{3,19},{4,20},{5,21},{6,22},{7,23},{8,24},{9,... | collective-permute-start | bytes 41480 | tf_op jit(solution)/shard_map/ppermute | solution.py:20
  30.4 20.5 %collective-permute-start.4 = (bf16[1,54,128]{2,1,0:T(8,128)(2,1)}, bf16[1,54,128]{2,1,0:T(8,128)(2,1)S(1)}, u32[]{:S(2)}, u32[]{:S(2)}) collective-permute-start(bf16[1,54,128]{2,1,0:T(8,128)(2,1)} %param.6), channel_id=1, source_target_pairs={{0,20},{1,21},{2,22},{3,23},{4,16},{5,17},{6,18},{7,19},{8,28},{9,... | collective-permute-start | bytes 41480 | tf_op jit(solution)/shard_map/ppermute | solution.py:20
  39.0 12.0 %collective-permute-start.5 = (bf16[1,54,128]{2,1,0:T(8,128)(2,1)}, bf16[1,54,128]{2,1,0:T(8,128)(2,1)S(1)}, u32[]{:S(2)}, u32[]{:S(2)}) collective-permute-start(bf16[1,54,128]{2,1,0:T(8,128)(2,1)} %param.6), channel_id=1, source_target_pairs={{0,24},{1,25},{2,26},{3,27},{4,28},{5,29},{6,30},{7,31},{8,16},{9,... | collective-permute-start | bytes 41480 | tf_op jit(solution)/shard_map/ppermute | solution.py:20
  56.6 13.2 %collective-permute-start.7 = (bf16[8,1,54,128]{3,0,2,1:T(8,128)(2,1)S(1)}, bf16[8,1,54,128]{3,0,2,1:T(8,128)(2,1)S(1)}, u32[]{:S(2)}, u32[]{:S(2)}) collective-permute-start(bf16[8,1,54,128]{3,0,2,1:T(8,128)(2,1)S(1)} %dynamic_update_slice.57), channel_id=1, source_target_pairs={{0,1},{1,0},{2,3},{3,2},{4,5},{5,4},{6,7},{7,6},{8,9},{9,8},{10,11... | collective-permute-start | bytes 331784 | tf_op jit(solution)/shard_map/ppermute | solution.py:20
  58.5 15.3 %collective-permute-start.8 = (bf16[8,1,54,128]{3,0,2,1:T(8,128)(2,1)S(1)}, bf16[8,1,54,128]{3,0,2,1:T(8,128)(2,1)S(1)}, u32[]{:S(2)}, u32[]{:S(2)}) collective-permute-start(bf16[8,1,54,128]{3,0,2,1:T(8,128)(2,1)S(1)} %dynamic_update_slice.57), channel_id=1, source_target_pairs={{0,32},{1,33},{2,34},{3,35},{4,36},{5,37},{6,38},{7,39},{8,40},{9,... | collective-permute-start | bytes 331784 | tf_op jit(solution)/shard_map/ppermute | solution.py:20
  62.0 14.5 %collective-permute-start.9 = (bf16[8,1,54,128]{3,0,2,1:T(8,128)(2,1)S(1)}, bf16[8,1,54,128]{3,0,2,1:T(8,128)(2,1)S(1)}, u32[]{:S(2)}, u32[]{:S(2)}) collective-permute-start(bf16[8,1,54,128]{3,0,2,1:T(8,128)(2,1)S(1)} %dynamic_update_slice.57), channel_id=1, source_target_pairs={{0,33},{1,32},{2,35},{3,34},{4,37},{5,36},{6,39},{7,38},{8,41},{9,... | collective-permute-start | bytes 331784 | tf_op jit(solution)/shard_map/ppermute | solution.py:20
  64.2 12.3 %collective-permute-start.10 = (bf16[8,1,54,128]{3,0,2,1:T(8,128)(2,1)S(1)}, bf16[8,1,54,128]{3,0,2,1:T(8,128)(2,1)S(1)}, u32[]{:S(2)}, u32[]{:S(2)}) collective-permute-start(bf16[8,1,54,128]{3,0,2,1:T(8,128)(2,1)S(1)} %dynamic_update_slice.57), channel_id=1, source_target_pairs={{0,2},{1,3},{2,0},{3,1},{4,6},{5,7},{6,4},{7,5},{8,10},{9,11},{10,... | collective-permute-start | bytes 331784 | tf_op jit(solution)/shard_map/ppermute | solution.py:20
  86.2 11.0 %collective-permute-start.14 = (bf16[2,4,8,8,128]{4,0,3,2,1:T(2,128)(2,1)S(1)}, bf16[2,4,8,8,128]{4,0,3,2,1:T(2,128)(2,1)S(1)}, u32[]{:S(2)}, u32[]{:S(2)}) collective-permute-start(bf16[2,4,8,8,128]{4,0,3,2,1:T(2,128)(2,1)S(1)} %fusion), channel_id=1, source_target_pairs={{64,0},{128,64},{192,128},{256,192},{320,256},{384,320},{448,384},... | collective-permute-start | bytes 393224 | tf_op jit(solution)/shard_map/ppermute | solution.py:15
  111.3 10.5 %collective-permute-start.16 = (bf16[2,4,8,8,128]{4,0,3,2,1:T(2,128)(2,1)S(1)}, bf16[2,4,8,8,128]{4,0,3,2,1:T(2,128)(2,1)S(1)}, u32[]{:S(2)}, u32[]{:S(2)}) collective-permute-start(bf16[2,4,8,8,128]{4,0,3,2,1:T(2,128)(2,1)S(1)} %fusion.2), channel_id=1, source_target_pairs={{64,0},{128,64},{192,128},{256,192},{320,256},{384,320},{448,384},... | collective-permute-start | bytes 393224 | tf_op jit(solution)/shard_map/ppermute | solution.py:15
  160.3 11.2 %collective-permute-start.20 = (bf16[2,4,8,8,128]{4,0,3,2,1:T(2,128)(2,1)S(1)}, bf16[2,4,8,8,128]{4,0,3,2,1:T(2,128)(2,1)S(1)}, u32[]{:S(2)}, u32[]{:S(2)}) collective-permute-start(bf16[2,4,8,8,128]{4,0,3,2,1:T(2,128)(2,1)S(1)} %fusion.6), channel_id=1, source_target_pairs={{64,0},{128,64},{192,128},{256,192},{320,256},{384,320},{448,384},... | collective-permute-start | bytes 393224 | tf_op jit(solution)/shard_map/ppermute | solution.py:15
  181.1 13.8 %collective-permute-start.27 = (bf16[8,54,128]{2,0,1:T(8,128)(2,1)S(1)}, bf16[8,54,128]{2,0,1:T(8,128)(2,1)S(1)}, u32[]{:S(2)}, u32[]{:S(2)}) collective-permute-start(bf16[8,54,128]{2,0,1:T(8,128)(2,1)S(1)} %get-tuple-element.23), channel_id=1, source_target_pairs={{0,35},{1,34},{2,33},{3,32},{4,39},{5,38},{6,37},{7,36},{8,43},{9,... | collective-permute-start | bytes 331784 | tf_op jit(solution)/shard_map/ppermute | solution.py:20
  183.0 15.4 %collective-permute-start.26 = (bf16[8,54,128]{2,0,1:T(8,128)(2,1)S(1)}, bf16[8,54,128]{2,0,1:T(8,128)(2,1)S(1)}, u32[]{:S(2)}, u32[]{:S(2)}) collective-permute-start(bf16[8,54,128]{2,0,1:T(8,128)(2,1)S(1)} %get-tuple-element.24), channel_id=1, source_target_pairs={{0,33},{1,32},{2,35},{3,34},{4,37},{5,36},{6,39},{7,38},{8,41},{9,... | collective-permute-start | bytes 331784 | tf_op jit(solution)/shard_map/ppermute | solution.py:20
  187.1 14.3 %collective-permute-start.25 = (bf16[8,54,128]{2,0,1:T(8,128)(2,1)S(1)}, bf16[8,54,128]{2,0,1:T(8,128)(2,1)S(1)}, u32[]{:S(2)}, u32[]{:S(2)}) collective-permute-start(bf16[8,54,128]{2,0,1:T(8,128)(2,1)S(1)} %get-tuple-element.25), channel_id=1, source_target_pairs={{0,3},{1,2},{2,1},{3,0},{4,7},{5,6},{6,5},{7,4},{8,11},{9,10},{10,... | collective-permute-start | bytes 331784 | tf_op jit(solution)/shard_map/ppermute | solution.py:20
  189.1 12.3 %collective-permute-start.24 = (bf16[8,54,128]{2,0,1:T(8,128)(2,1)S(1)}, bf16[8,54,128]{2,0,1:T(8,128)(2,1)S(1)}, u32[]{:S(2)}, u32[]{:S(2)}) collective-permute-start(bf16[8,54,128]{2,0,1:T(8,128)(2,1)S(1)} %get-tuple-element.26), channel_id=1, source_target_pairs={{0,1},{1,0},{2,3},{3,2},{4,5},{5,4},{6,7},{7,6},{8,9},{9,8},{10,11... | collective-permute-start | bytes 331784 | tf_op jit(solution)/shard_map/ppermute | solution.py:20
  206.3 29.1 %collective-permute-start.34 = (bf16[54,128]{1,0:T(8,128)(2,1)S(1)}, bf16[54,128]{1,0:T(8,128)(2,1)S(1)}, u32[]{:S(2)}, u32[]{:S(2)}) collective-permute-start(bf16[54,128]{1,0:T(8,128)(2,1)S(1)} %bitcast.153), channel_id=1, source_target_pairs={{0,28},{1,29},{2,30},{3,31},{4,24},{5,25},{6,26},{7,27},{8,20},{9,... | collective-permute-start | bytes 41480 | tf_op jit(solution)/shard_map/ppermute | solution.py:20
  208.2 31.1 %collective-permute-start.33 = (bf16[54,128]{1,0:T(8,128)(2,1)S(1)}, bf16[54,128]{1,0:T(8,128)(2,1)S(1)}, u32[]{:S(2)}, u32[]{:S(2)}) collective-permute-start(bf16[54,128]{1,0:T(8,128)(2,1)S(1)} %bitcast.152), channel_id=1, source_target_pairs={{0,12},{1,13},{2,14},{3,15},{4,8},{5,9},{6,10},{7,11},{8,4},{9,5},... | collective-permute-start | bytes 41480 | tf_op jit(solution)/shard_map/ppermute | solution.py:20
  219.1 28.2 %collective-permute-start.32 = (bf16[54,128]{1,0:T(8,128)(2,1)S(1)}, bf16[54,128]{1,0:T(8,128)(2,1)S(1)}, u32[]{:S(2)}, u32[]{:S(2)}) collective-permute-start(bf16[54,128]{1,0:T(8,128)(2,1)S(1)} %bitcast.154), channel_id=1, source_target_pairs={{0,20},{1,21},{2,22},{3,23},{4,16},{5,17},{6,18},{7,19},{8,28},{9,... | collective-permute-start | bytes 41480 | tf_op jit(solution)/shard_map/ppermute | solution.py:20
  228.2 19.1 %collective-permute-start.31 = (bf16[54,128]{1,0:T(8,128)(2,1)S(1)}, bf16[54,128]{1,0:T(8,128)(2,1)S(1)}, u32[]{:S(2)}, u32[]{:S(2)}) collective-permute-start(bf16[54,128]{1,0:T(8,128)(2,1)S(1)} %bitcast.155), channel_id=1, source_target_pairs={{0,4},{1,5},{2,6},{3,7},{4,0},{5,1},{6,2},{7,3},{8,12},{9,13},{10,... | collective-permute-start | bytes 41480 | tf_op jit(solution)/shard_map/ppermute | solution.py:20
  230.2 17.2 %collective-permute-start.30 = (bf16[54,128]{1,0:T(8,128)(2,1)S(1)}, bf16[54,128]{1,0:T(8,128)(2,1)S(1)}, u32[]{:S(2)}, u32[]{:S(2)}) collective-permute-start(bf16[54,128]{1,0:T(8,128)(2,1)S(1)} %bitcast.156), channel_id=1, source_target_pairs={{0,24},{1,25},{2,26},{3,27},{4,28},{5,29},{6,30},{7,31},{8,16},{9,... | collective-permute-start | bytes 41480 | tf_op jit(solution)/shard_map/ppermute | solution.py:20
  235.4 11.9 %collective-permute-start.29 = (bf16[54,128]{1,0:T(8,128)(2,1)S(1)}, bf16[54,128]{1,0:T(8,128)(2,1)S(1)}, u32[]{:S(2)}, u32[]{:S(2)}) collective-permute-start(bf16[54,128]{1,0:T(8,128)(2,1)S(1)} %bitcast.158), channel_id=1, source_target_pairs={{0,8},{1,9},{2,10},{3,11},{4,12},{5,13},{6,14},{7,15},{8,0},{9,1},... | collective-permute-start | bytes 41480 | tf_op jit(solution)/shard_map/ppermute | solution.py:20
  239.4 14.3 %collective-permute-start.28 = (bf16[54,128]{1,0:T(8,128)(2,1)S(1)}, bf16[54,128]{1,0:T(8,128)(2,1)S(1)}, u32[]{:S(2)}, u32[]{:S(2)}) collective-permute-start(bf16[54,128]{1,0:T(8,128)(2,1)S(1)} %bitcast.157), channel_id=1, source_target_pairs={{0,16},{1,17},{2,18},{3,19},{4,20},{5,21},{6,22},{7,23},{8,24},{9,... | collective-permute-start | bytes 41480 | tf_op jit(solution)/shard_map/ppermute | solution.py:20
  (21 other events, 320.1 us)

commit v5 on v3

--- a/solution.py
+++ b/solution.py
@@ -123,7 +123,8 @@
         grads_held = jnp.where(mine, down_grad, grads_held)
         slope_held = jnp.where(mine, slope, slope_held)
         if tick + 1 < segments:
-            incoming = passed_along(down_grad, "segment", -1)
+            sender = segments - 1 - tick
+            incoming = lax.ppermute(down_grad, "segment", [(sender, sender - 1)])
 
     grad_term = conv_kernel_grad(fields, slope_held).reshape(dp_count, -1, channels)
     reduced = reduce_by_halves(grad_term, "dp", gather_order[::-1])

time: 209 us -> 177 us (0.85)
  the two profiles are of different devices: /device:TPU:14 before, /device:TPU:8 now
where the time goes in v5:
time: 177 us; the launch traced here: 176 us
  waiting for transfers between devices  83.6 us (47%)
  starting transfers between devices  57.1 us (32%)
  matrix products  22.2 us (13%)
  local copies, waits for them, and re-layouts  6.18 us (3%)
  other arithmetic  5.69 us (3%)
    ppermute x12, starting transfers between devices, exchanged(): return lax.ppermute(array, axis, [(i, i ^ mask) for i in range(length)])  51.6 us
    ppermute x12, waiting for transfers between devices, exchanged(): return lax.ppermute(array, axis, [(i, i ^ mask) for i in range(length)])  47 us
    ppermute x7, waiting for transfers between devices, local(): incoming = lax.ppermute(down_grad, 'segment', [(sender, sender - 1)])  36.5 us
    conv_general_dilated x8, matrix products, conv_transposed(): lax.conv_general_dilated(slope, flipped, (1, 1, 1), [(1, 1)] * 3, dimensi...  15.6 us
    ppermute x7, starting transfers between devices, local(): incoming = lax.ppermute(down_grad, 'segment', [(sender, sender - 1)])  5.49 us
    conv_general_dilated x1, matrix products, conv_kernel_grad(): lax.conv_general_dilated(field, slope, (1, 1, 1), [(1, 1)] * 3, dimension...  4.66 us
    sin x3, other arithmetic, position_term(): phases.append(jnp.sin(phase_val * (2.0 * math.pi / WAVE)))  3.93 us
  transfers between devices with their start and end apart: 19, of which 12 were waited for; matrix products, arithmetic and copies ran while one was open for 6% of the time, Pallas kernels for 0%

profile of v5, /device:TPU:8, one launch (start us, length us, event | category | flops | bytes accessed | tf_op | source)
XLA Modules:
  0.0 176.0 jit_solution(5170909504916443003)
XLA Ops:
  0.6 15.7 %collective-permute-start = (bf16[1,54,128]{2,1,0:T(8,128)(2,1)}, bf16[1,54,128]{2,1,0:T(8,128)(2,1)S(1)}, u32[]{:S(2)}, u32[]{:S(2)}) collective-permute-start(bf16[1,54,128]{2,1,0:T(8,128)(2,1)} %param.6), channel_id=1, source_target_pairs={{0,16},{1,17},{2,18},{3,19},{4,20},{5,21},{6,22},{7,23},{8,24},{9,... | collective-permute-start | bytes 41480 | tf_op jit(solution)/shard_map/ppermute | solution.py:20
  23.4 4.3 %collective-permute-start.1 = (bf16[2,1,54,128]{3,2,0,1:T(8,128)(2,1)S(1)}, bf16[2,1,54,128]{3,2,0,1:T(8,128)(2,1)S(1)}, u32[]{:S(2)}, u32[]{:S(2)}) collective-permute-start(bf16[2,1,54,128]{3,2,0,1:T(8,128)(2,1)S(1)} %fusion.38), channel_id=1, source_target_pairs={{0,8},{1,9},{2,10},{3,11},{4,12},{5,13},{6,14},{7,15},{8,0},{9,1},... | collective-permute-start | bytes 82952 | tf_op jit(solution)/shard_map/ppermute | solution.py:20
  27.7 5.9 %collective-permute-done.1 = bf16[2,1,54,128]{3,2,0,1:T(8,128)(2,1)S(1)} collective-permute-done((bf16[2,1,54,128]{3,2,0,1:T(8,128)(2,1)S(1)}, bf16[2,1,54,128]{3,2,0,1:T(8,128)(2,1)S(1)}, u32[]{:S(2)}, u32[]{:S(2)}) %collective-permute-start.1) | collective-permute-done | bytes 27680 | tf_op jit(solution)/shard_map/ppermute | solution.py:20
  33.7 2.8 %collective-permute-start.2 = (bf16[2,2,1,54,128]{4,3,1,0,2:T(8,128)(2,1)S(1)}, bf16[2,2,1,54,128]{4,3,1,0,2:T(8,128)(2,1)S(1)}, u32[]{:S(2)}, u32[]{:S(2)}) collective-permute-start(bf16[2,2,1,54,128]{4,3,1,0,2:T(8,128)(2,1)S(1)} %fusion.33), channel_id=1, source_target_pairs={{0,4},{1,5},{2,6},{3,7},{4,0},{5,1},{6,2},{7,3},{8,12},{9,13},{10,... | collective-permute-start | bytes 165896 | tf_op jit(solution)/shard_map/ppermute | solution.py:20
  36.5 4.6 %collective-permute-done.2 = bf16[2,2,1,54,128]{4,3,1,0,2:T(8,128)(2,1)S(1)} collective-permute-done((bf16[2,2,1,54,128]{4,3,1,0,2:T(8,128)(2,1)S(1)}, bf16[2,2,1,54,128]{4,3,1,0,2:T(8,128)(2,1)S(1)}, u32[]{:S(2)}, u32[]{:S(2)}) %collective-permute-start.2) | collective-permute-done | bytes 55328 | tf_op jit(solution)/shard_map/ppermute | solution.py:20
  41.2 1.9 %collective-permute-start.3 = (bf16[2,2,2,1,54,128]{5,4,2,1,0,3:T(8,128)(2,1)S(1)}, bf16[2,2,2,1,54,128]{5,4,2,1,0,3:T(8,128)(2,1)S(1)}, u32[]{:S(2)}, u32[]{:S(2)}) collective-permute-start(bf16[2,2,2,1,54,128]{5,4,2,1,0,3:T(8,128)(2,1)S(1)} %fusion.27), channel_id=1, source_target_pairs={{0,2},{1,3},{2,0},{3,1},{4,6},{5,7},{6,4},{7,5},{8,10},{9,11},{10,... | collective-permute-start | bytes 331784 | tf_op jit(solution)/shard_map/ppermute | solution.py:20
  43.2 4.7 %collective-permute-done.3 = bf16[2,2,2,1,54,128]{5,4,2,1,0,3:T(8,128)(2,1)S(1)} collective-permute-done((bf16[2,2,2,1,54,128]{5,4,2,1,0,3:T(8,128)(2,1)S(1)}, bf16[2,2,2,1,54,128]{5,4,2,1,0,3:T(8,128)(2,1)S(1)}, u32[]{:S(2)}, u32[]{:S(2)}) %collective-permute-start.3) | collective-permute-done | bytes 110624 | tf_op jit(solution)/shard_map/ppermute | solution.py:20
  48.0 2.4 %collective-permute-start.4 = (bf16[2,2,2,2,1,54,128]{6,5,3,2,1,0,4:T(8,128)(2,1)S(1)}, bf16[2,2,2,2,1,54,128]{6,5,3,2,1,0,4:T(8,128)(2,1)S(1)}, u32[]{:S(2)}, u32[]{:S(2)}) collective-permute-start(bf16[2,2,2,2,1,54,128]{6,5,3,2,1,0,4:T(8,128)(2,1)S(1)} %fusion.23), channel_id=1, source_target_pairs={{0,32},{1,33},{2,34},{3,35},{4,36},{5,37},{6,38},{7,39},{8,40},{9,... | collective-permute-start | bytes 663560 | tf_op jit(solution)/shard_map/ppermute | solution.py:20
  50.4 5.5 %collective-permute-done.4 = bf16[2,2,2,2,1,54,128]{6,5,3,2,1,0,4:T(8,128)(2,1)S(1)} collective-permute-done((bf16[2,2,2,2,1,54,128]{6,5,3,2,1,0,4:T(8,128)(2,1)S(1)}, bf16[2,2,2,2,1,54,128]{6,5,3,2,1,0,4:T(8,128)(2,1)S(1)}, u32[]{:S(2)}, u32[]{:S(2)}) %collective-permute-start.4) | collective-permute-done | bytes 221216 | tf_op jit(solution)/shard_map/ppermute | solution.py:20
  56.0 1.9 %collective-permute-start.5 = (bf16[2,2,2,2,2,1,54,128]{7,6,4,3,2,1,0,5:T(8,128)(2,1)S(1)}, bf16[2,2,2,2,2,1,54,128]{7,6,4,3,2,1,0,5:T(8,128)(2,1)S(1)}, u32[]{:S(2)}, u32[]{:S(2)}) collective-permute-start(bf16[2,2,2,2,2,1,54,128]{7,6,4,3,2,1,0,5:T(8,128)(2,1)S(1)} %fusion.12), channel_id=1, source_target_pairs={{0,1},{1,0},{2,3},{3,2},{4,5},{5,4},{6,7},{7,6},{8,9},{9,8},{10,11... | collective-permute-start | bytes 1327112 | tf_op jit(solution)/shard_map/ppermute | solution.py:20
  60.9 1.9 %add_multiply_fusion = f32[2,4,8,8,128]{4,0,3,2,1:T(2,128)S(1)} fusion(f32[1,4,8,8,128]{4,0,3,2,1:T(1,128)S(1)} %broadcast_add_fusion, f32[1,4,8,8,128]{4,0,3,2,1:T(1,128)S(1)} %broadcast_add_fusion.1, bf16[3,3,3,128,128]{4,3,2,1,0:T(8,128)(2,1)S(1)} %reshape_reshape.6, bf16[2,4,8,8,128]{4,3,2,1,0:T(8,128)(2,1)S(1)} %bitcast.140), kind=kOutput, calls=%fused_computation.47 | convolution fusion | flops 317784064 | bytes 1540096 | tf_op jit(solution)/shard_map/conv_general_dilated | solution.py:57
  80.9 36.5 %collective-permute-done.12 = bf16[2,4,8,8,128]{4,0,3,2,1:T(2,128)(2,1)S(1)} collective-permute-done((bf16[2,4,8,8,128]{4,0,3,2,1:T(2,128)(2,1)S(1)}, bf16[2,4,8,8,128]{4,0,3,2,1:T(2,128)(2,1)S(1)}, u32[]{:S(2)}, u32[]{:S(2)}) %collective-permute-start.12) | collective-permute-done | bytes 131104 | tf_op jit(solution)/shard_map/ppermute | solution.py:127
  117.4 4.7 %fusion.24 = f32[3,3,3,128,128]{4,3,2,1,0:T(8,128)} fusion(pred[]{:T(512)S(6)} %eq.51, pred[]{:T(512)S(6)} %eq.59, pred[]{:T(512)S(6)} %eq.60, pred[]{:T(512)S(6)} %eq.61, pred[]{:T(512)S(6)} %eq.62, pred[]{:T(512)S(6)} %eq.63, pred[]{:T(512)S(6)} %eq.64, pred[]{:T(512)S(6)} %eq.52, bf16[2,4,8,8,128]{4,3,2,1,0:T(8,128)(2,1)S(1)} %bitcast.141, ...), kind=kOutput, calls=%fused_computation.79 | convolution fusion | flops 319815680 | bytes 3211272 | tf_op jit(solution)/shard_map/conv_general_dilated | solution.py:74
  123.6 1.9 %collective-permute-start.13 = (bf16[2,2,2,2,2,54,128]{6,5,1,2,3,4,0:T(8,128)(2,1)S(1)}, bf16[2,2,2,2,2,54,128]{6,5,1,2,3,4,0:T(8,128)(2,1)S(1)}, u32[]{:S(2)}, u32[]{:S(2)}) collective-permute-start(bf16[2,2,2,2,2,54,128]{6,5,1,2,3,4,0:T(8,128)(2,1)S(1)} %fusion.11), channel_id=1, source_target_pairs={{0,1},{1,0},{2,3},{3,2},{4,5},{5,4},{6,7},{7,6},{8,9},{9,8},{10,11... | collective-permute-start | bytes 1327112 | tf_op jit(solution)/shard_map/ppermute | solution.py:20
  127.6 3.4 %collective-permute-start.14 = (bf16[2,2,2,2,54,128]{5,4,0,1,2,3:T(8,128)(2,1)S(1)}, bf16[2,2,2,2,54,128]{5,4,0,1,2,3:T(8,128)(2,1)S(1)}, u32[]{:S(2)}, u32[]{:S(2)}) collective-permute-start(bf16[2,2,2,2,54,128]{5,4,0,1,2,3:T(8,128)(2,1)S(1)} %fusion.22), channel_id=1, source_target_pairs={{0,32},{1,33},{2,34},{3,35},{4,36},{5,37},{6,38},{7,39},{8,40},{9,... | collective-permute-start | bytes 663560 | tf_op jit(solution)/shard_map/ppermute | solution.py:20
  131.0 6.3 %collective-permute-done.14 = bf16[2,2,2,2,54,128]{5,4,0,1,2,3:T(8,128)(2,1)S(1)} collective-permute-done((bf16[2,2,2,2,54,128]{5,4,0,1,2,3:T(8,128)(2,1)S(1)}, bf16[2,2,2,2,54,128]{5,4,0,1,2,3:T(8,128)(2,1)S(1)}, u32[]{:S(2)}, u32[]{:S(2)}) %collective-permute-start.14) | collective-permute-done | bytes 221216 | tf_op jit(solution)/shard_map/ppermute | solution.py:20
  137.3 1.9 %collective-permute-start.15 = (bf16[2,2,2,54,128]{4,3,0,1,2:T(8,128)(2,1)S(1)}, bf16[2,2,2,54,128]{4,3,0,1,2:T(8,128)(2,1)S(1)}, u32[]{:S(2)}, u32[]{:S(2)}) collective-permute-start(bf16[2,2,2,54,128]{4,3,0,1,2:T(8,128)(2,1)S(1)} %fusion.26), channel_id=1, source_target_pairs={{0,2},{1,3},{2,0},{3,1},{4,6},{5,7},{6,4},{7,5},{8,10},{9,11},{10,... | collective-permute-start | bytes 331784 | tf_op jit(solution)/shard_map/ppermute | solution.py:20
  139.2 4.8 %collective-permute-done.15 = bf16[2,2,2,54,128]{4,3,0,1,2:T(8,128)(2,1)S(1)} collective-permute-done((bf16[2,2,2,54,128]{4,3,0,1,2:T(8,128)(2,1)S(1)}, bf16[2,2,2,54,128]{4,3,0,1,2:T(8,128)(2,1)S(1)}, u32[]{:S(2)}, u32[]{:S(2)}) %collective-permute-start.15) | collective-permute-done | bytes 110624 | tf_op jit(solution)/shard_map/ppermute | solution.py:20
  144.1 2.4 %collective-permute-start.16 = (bf16[2,2,54,128]{3,2,0,1:T(8,128)(2,1)S(1)}, bf16[2,2,54,128]{3,2,0,1:T(8,128)(2,1)S(1)}, u32[]{:S(2)}, u32[]{:S(2)}) collective-permute-start(bf16[2,2,54,128]{3,2,0,1:T(8,128)(2,1)S(1)} %fusion.32), channel_id=1, source_target_pairs={{0,4},{1,5},{2,6},{3,7},{4,0},{5,1},{6,2},{7,3},{8,12},{9,13},{10,... | collective-permute-start | bytes 165896 | tf_op jit(solution)/shard_map/ppermute | solution.py:20
  146.5 4.6 %collective-permute-done.16 = bf16[2,2,54,128]{3,2,0,1:T(8,128)(2,1)S(1)} collective-permute-done((bf16[2,2,54,128]{3,2,0,1:T(8,128)(2,1)S(1)}, bf16[2,2,54,128]{3,2,0,1:T(8,128)(2,1)S(1)}, u32[]{:S(2)}, u32[]{:S(2)}) %collective-permute-start.16) | collective-permute-done | bytes 55328 | tf_op jit(solution)/shard_map/ppermute | solution.py:20
  151.1 4.3 %collective-permute-start.17 = (bf16[2,54,128]{2,1,0:T(8,128)(2,1)S(1)}, bf16[2,54,128]{2,1,0:T(8,128)(2,1)S(1)}, u32[]{:S(2)}, u32[]{:S(2)}) collective-permute-start(bf16[2,54,128]{2,1,0:T(8,128)(2,1)S(1)} %fusion.35), channel_id=1, source_target_pairs={{0,8},{1,9},{2,10},{3,11},{4,12},{5,13},{6,14},{7,15},{8,0},{9,1},... | collective-permute-start | bytes 82952 | tf_op jit(solution)/shard_map/ppermute | solution.py:20
  155.5 5.6 %collective-permute-done.17 = bf16[2,54,128]{2,1,0:T(8,128)(2,1)S(1)} collective-permute-done((bf16[2,54,128]{2,1,0:T(8,128)(2,1)S(1)}, bf16[2,54,128]{2,1,0:T(8,128)(2,1)S(1)}, u32[]{:S(2)}, u32[]{:S(2)}) %collective-permute-start.17) | collective-permute-done | bytes 27680 | tf_op jit(solution)/shard_map/ppermute | solution.py:20
  161.1 8.6 %collective-permute-start.18 = (bf16[54,128]{1,0:T(8,128)(2,1)S(1)}, bf16[54,128]{1,0:T(8,128)(2,1)S(1)}, u32[]{:S(2)}, u32[]{:S(2)}) collective-permute-start(bf16[54,128]{1,0:T(8,128)(2,1)S(1)} %fusion.39), channel_id=1, source_target_pairs={{0,16},{1,17},{2,18},{3,19},{4,20},{5,21},{6,22},{7,23},{8,24},{9,... | collective-permute-start | bytes 41480 | tf_op jit(solution)/shard_map/ppermute | solution.py:20
  169.7 3.3 %fusion.9 = bf16[1,2,4,8,8,128]{5,1,4,3,2,0:T(2,128)(2,1)S(1)} fusion(bf16[3,3,3,128,128]{4,3,2,1,0:T(8,128)(2,1)S(1)} %copy-done.1, pred[]{:T(512)S(6)} %eq.51, bf16[2,4,8,8,128]{4,0,3,2,1:T(2,128)(2,1)} %copy-done.13, pred[]{:T(512)S(6)} %eq.59, bf16[2,4,8,8,128]{4,0,3,2,1:T(2,128)(2,1)} %copy-done.12, pred[]{:T(512)S(6)} %eq.60, ...), kind=kOutput, calls=%fused_computation.18 | convolution fusion | flops 318242816 | bytes 2457608 | tf_op jit(solution)/shard_map/conv_general_dilated | solution.py:66
  (102 shorter events, 34.8 us)
Async XLA Ops:
  0.6 22.0 %collective-permute-start = (bf16[1,54,128]{2,1,0:T(8,128)(2,1)}, bf16[1,54,128]{2,1,0:T(8,128)(2,1)S(1)}, u32[]{:S(2)}, u32[]{:S(2)}) collective-permute-start(bf16[1,54,128]{2,1,0:T(8,128)(2,1)} %param.6), channel_id=1, source_target_pairs={{0,16},{1,17},{2,18},{3,19},{4,20},{5,21},{6,22},{7,23},{8,24},{9,... | collective-permute-start | bytes 41480 | tf_op jit(solution)/shard_map/ppermute | solution.py:20
  23.4 10.2 %collective-permute-start.1 = (bf16[2,1,54,128]{3,2,0,1:T(8,128)(2,1)S(1)}, bf16[2,1,54,128]{3,2,0,1:T(8,128)(2,1)S(1)}, u32[]{:S(2)}, u32[]{:S(2)}) collective-permute-start(bf16[2,1,54,128]{3,2,0,1:T(8,128)(2,1)S(1)} %fusion.38), channel_id=1, source_target_pairs={{0,8},{1,9},{2,10},{3,11},{4,12},{5,13},{6,14},{7,15},{8,0},{9,1},... | collective-permute-start | bytes 82952 | tf_op jit(solution)/shard_map/ppermute | solution.py:20
  33.7 7.5 %collective-permute-start.2 = (bf16[2,2,1,54,128]{4,3,1,0,2:T(8,128)(2,1)S(1)}, bf16[2,2,1,54,128]{4,3,1,0,2:T(8,128)(2,1)S(1)}, u32[]{:S(2)}, u32[]{:S(2)}) collective-permute-start(bf16[2,2,1,54,128]{4,3,1,0,2:T(8,128)(2,1)S(1)} %fusion.33), channel_id=1, source_target_pairs={{0,4},{1,5},{2,6},{3,7},{4,0},{5,1},{6,2},{7,3},{8,12},{9,13},{10,... | collective-permute-start | bytes 165896 | tf_op jit(solution)/shard_map/ppermute | solution.py:20
  41.2 6.7 %collective-permute-start.3 = (bf16[2,2,2,1,54,128]{5,4,2,1,0,3:T(8,128)(2,1)S(1)}, bf16[2,2,2,1,54,128]{5,4,2,1,0,3:T(8,128)(2,1)S(1)}, u32[]{:S(2)}, u32[]{:S(2)}) collective-permute-start(bf16[2,2,2,1,54,128]{5,4,2,1,0,3:T(8,128)(2,1)S(1)} %fusion.27), channel_id=1, source_target_pairs={{0,2},{1,3},{2,0},{3,1},{4,6},{5,7},{6,4},{7,5},{8,10},{9,11},{10,... | collective-permute-start | bytes 331784 | tf_op jit(solution)/shard_map/ppermute | solution.py:20
  48.0 7.9 %collective-permute-start.4 = (bf16[2,2,2,2,1,54,128]{6,5,3,2,1,0,4:T(8,128)(2,1)S(1)}, bf16[2,2,2,2,1,54,128]{6,5,3,2,1,0,4:T(8,128)(2,1)S(1)}, u32[]{:S(2)}, u32[]{:S(2)}) collective-permute-start(bf16[2,2,2,2,1,54,128]{6,5,3,2,1,0,4:T(8,128)(2,1)S(1)} %fusion.23), channel_id=1, source_target_pairs={{0,32},{1,33},{2,34},{3,35},{4,36},{5,37},{6,38},{7,39},{8,40},{9,... | collective-permute-start | bytes 663560 | tf_op jit(solution)/shard_map/ppermute | solution.py:20
  56.0 3.7 %collective-permute-start.5 = (bf16[2,2,2,2,2,1,54,128]{7,6,4,3,2,1,0,5:T(8,128)(2,1)S(1)}, bf16[2,2,2,2,2,1,54,128]{7,6,4,3,2,1,0,5:T(8,128)(2,1)S(1)}, u32[]{:S(2)}, u32[]{:S(2)}) collective-permute-start(bf16[2,2,2,2,2,1,54,128]{7,6,4,3,2,1,0,5:T(8,128)(2,1)S(1)} %fusion.12), channel_id=1, source_target_pairs={{0,1},{1,0},{2,3},{3,2},{4,5},{5,4},{6,7},{7,6},{8,9},{9,8},{10,11... | collective-permute-start | bytes 1327112 | tf_op jit(solution)/shard_map/ppermute | solution.py:20
  62.8 54.6 %copy-start.15 = (f32[2,4,8,8,128]{4,0,3,2,1:T(2,128)}, f32[2,4,8,8,128]{4,0,3,2,1:T(2,128)S(1)}, u32[]{:S(2)}) copy-start(f32[2,4,8,8,128]{4,0,3,2,1:T(2,128)S(1)} %add_multiply_fusion) | copy-start | bytes 786436
  64.5 0.7 collective-permute-start.6
  67.0 0.7 collective-permute-start.7
  69.4 0.7 collective-permute-start.8
  71.9 0.9 collective-permute-start.9
  74.6 0.7 collective-permute-start.10
  77.1 0.7 collective-permute-start.11
  79.5 42.5 %copy-start.13 = (bf16[2,4,8,8,128]{4,0,3,2,1:T(2,128)(2,1)}, bf16[2,4,8,8,128]{4,0,3,2,1:T(2,128)(2,1)S(1)}, u32[]{:S(2)}) copy-start(bf16[2,4,8,8,128]{4,0,3,2,1:T(2,128)(2,1)S(1)} %fusion.6) | copy-start | bytes 393220
  79.6 37.8 %collective-permute-start.12 = (bf16[2,4,8,8,128]{4,0,3,2,1:T(2,128)(2,1)S(1)}, bf16[2,4,8,8,128]{4,0,3,2,1:T(2,128)(2,1)S(1)}, u32[]{:S(2)}, u32[]{:S(2)}) collective-permute-start(bf16[2,4,8,8,128]{4,0,3,2,1:T(2,128)(2,1)S(1)} %fusion.6), channel_id=1, source_target_pairs={{64,0},{65,1},{66,2},{67,3},{68,4},{69,5},{70,6},{71,7},{72,8},{73... | collective-permute-start | bytes 393224 | tf_op jit(solution)/shard_map/ppermute | solution.py:127
  123.6 3.7 %collective-permute-start.13 = (bf16[2,2,2,2,2,54,128]{6,5,1,2,3,4,0:T(8,128)(2,1)S(1)}, bf16[2,2,2,2,2,54,128]{6,5,1,2,3,4,0:T(8,128)(2,1)S(1)}, u32[]{:S(2)}, u32[]{:S(2)}) collective-permute-start(bf16[2,2,2,2,2,54,128]{6,5,1,2,3,4,0:T(8,128)(2,1)S(1)} %fusion.11), channel_id=1, source_target_pairs={{0,1},{1,0},{2,3},{3,2},{4,5},{5,4},{6,7},{7,6},{8,9},{9,8},{10,11... | collective-permute-start | bytes 1327112 | tf_op jit(solution)/shard_map/ppermute | solution.py:20
  127.5 42.2 %copy-start.1 = (bf16[3,3,3,128,128]{4,3,2,1,0:T(8,128)(2,1)S(1)}, bf16[3,3,3,128,128]{4,3,2,1,0:T(8,128)(2,1)}, u32[]{:S(2)}) copy-start(bf16[3,3,3,128,128]{4,3,2,1,0:T(8,128)(2,1)} %copy-done) | copy-start | bytes 2654212
  127.5 42.2 %copy-start.5 = (bf16[2,4,8,8,128]{4,0,3,2,1:T(2,128)(2,1)S(1)}, bf16[2,4,8,8,128]{4,0,3,2,1:T(2,128)(2,1)}, u32[]{:S(2)}) copy-start(bf16[2,4,8,8,128]{4,0,3,2,1:T(2,128)(2,1)} %copy-done.4) | copy-start | bytes 393220
  127.5 42.2 %copy-start.7 = (bf16[2,4,8,8,128]{4,0,3,2,1:T(2,128)(2,1)S(1)}, bf16[2,4,8,8,128]{4,0,3,2,1:T(2,128)(2,1)}, u32[]{:S(2)}) copy-start(bf16[2,4,8,8,128]{4,0,3,2,1:T(2,128)(2,1)} %copy-done.6) | copy-start | bytes 393220
  127.6 9.7 %collective-permute-start.14 = (bf16[2,2,2,2,54,128]{5,4,0,1,2,3:T(8,128)(2,1)S(1)}, bf16[2,2,2,2,54,128]{5,4,0,1,2,3:T(8,128)(2,1)S(1)}, u32[]{:S(2)}, u32[]{:S(2)}) collective-permute-start(bf16[2,2,2,2,54,128]{5,4,0,1,2,3:T(8,128)(2,1)S(1)} %fusion.22), channel_id=1, source_target_pairs={{0,32},{1,33},{2,34},{3,35},{4,36},{5,37},{6,38},{7,39},{8,40},{9,... | collective-permute-start | bytes 663560 | tf_op jit(solution)/shard_map/ppermute | solution.py:20
  137.3 6.7 %collective-permute-start.15 = (bf16[2,2,2,54,128]{4,3,0,1,2:T(8,128)(2,1)S(1)}, bf16[2,2,2,54,128]{4,3,0,1,2:T(8,128)(2,1)S(1)}, u32[]{:S(2)}, u32[]{:S(2)}) collective-permute-start(bf16[2,2,2,54,128]{4,3,0,1,2:T(8,128)(2,1)S(1)} %fusion.26), channel_id=1, source_target_pairs={{0,2},{1,3},{2,0},{3,1},{4,6},{5,7},{6,4},{7,5},{8,10},{9,11},{10,... | collective-permute-start | bytes 331784 | tf_op jit(solution)/shard_map/ppermute | solution.py:20
  144.1 7.0 %collective-permute-start.16 = (bf16[2,2,54,128]{3,2,0,1:T(8,128)(2,1)S(1)}, bf16[2,2,54,128]{3,2,0,1:T(8,128)(2,1)S(1)}, u32[]{:S(2)}, u32[]{:S(2)}) collective-permute-start(bf16[2,2,54,128]{3,2,0,1:T(8,128)(2,1)S(1)} %fusion.32), channel_id=1, source_target_pairs={{0,4},{1,5},{2,6},{3,7},{4,0},{5,1},{6,2},{7,3},{8,12},{9,13},{10,... | collective-permute-start | bytes 165896 | tf_op jit(solution)/shard_map/ppermute | solution.py:20
  151.1 9.9 %collective-permute-start.17 = (bf16[2,54,128]{2,1,0:T(8,128)(2,1)S(1)}, bf16[2,54,128]{2,1,0:T(8,128)(2,1)S(1)}, u32[]{:S(2)}, u32[]{:S(2)}) collective-permute-start(bf16[2,54,128]{2,1,0:T(8,128)(2,1)S(1)} %fusion.35), channel_id=1, source_target_pairs={{0,8},{1,9},{2,10},{3,11},{4,12},{5,13},{6,14},{7,15},{8,0},{9,1},... | collective-permute-start | bytes 82952 | tf_op jit(solution)/shard_map/ppermute | solution.py:20
  161.1 14.3 %collective-permute-start.18 = (bf16[54,128]{1,0:T(8,128)(2,1)S(1)}, bf16[54,128]{1,0:T(8,128)(2,1)S(1)}, u32[]{:S(2)}, u32[]{:S(2)}) collective-permute-start(bf16[54,128]{1,0:T(8,128)(2,1)S(1)} %fusion.39), channel_id=1, source_target_pairs={{0,16},{1,17},{2,18},{3,19},{4,20},{5,21},{6,22},{7,23},{8,24},{9,... | collective-permute-start | bytes 41480 | tf_op jit(solution)/shard_map/ppermute | solution.py:20
  (11 other events, 159.8 us)

commit v6 on v5

--- a/solution.py
+++ b/solution.py
@@ -5,6 +5,7 @@
 from jax import lax
 from jax.sharding import PartitionSpec as P
 
+DP = ("y", "z", "core")
 STRIDE = 2
 WAVE = 64
 
@@ -39,18 +40,21 @@
     return held.reshape((-1,) + block.shape[1:])
 
 
-def reduce_by_halves(chunks, axis, order):
+def reduce_by_halves(chunks, axis, order, ring_axis):
     index = lax.axis_index(axis)
-    done = len(order)
+    done = bit_count(chunks.shape[0])
+    rest = [bit for bit in range(done - 1, -1, -1) if bit not in order]
     held = chunks.reshape((2,) * done + chunks.shape[1:])
-    held = jnp.transpose(held, [done - 1 - bit for bit in order] + list(range(done, held.ndim)))
+    held = jnp.transpose(held, [done - 1 - bit for bit in order + rest] + list(range(done, held.ndim)))
     for bit in order:
         mine = (index >> bit) & 1
         kept = lax.dynamic_index_in_dim(held, mine, 0, keepdims=False)
         sent = lax.dynamic_index_in_dim(held, 1 - mine, 0, keepdims=False)
         received = exchanged(sent.astype(jnp.bfloat16), axis, 1 << bit)
         held = kept + received.astype(jnp.float32)
-    return held.reshape((1,) + chunks.shape[1:])
+    held = held.reshape((-1,) + chunks.shape[1:]).astype(jnp.bfloat16)
+    received = lax.all_to_all(held, ring_axis, 0, 0, tiled=True)
+    return jnp.sum(received.astype(jnp.float32), axis=0, keepdims=True)
 
 
 def conv_forward(field, kernel):
@@ -93,12 +97,12 @@
 
 def local(acts, weights, pos_weight, anchors, top_grad):
     segments = lax.axis_size("segment")
-    dp_count = lax.axis_size("dp")
+    dp_count = lax.axis_size(DP)
     segment_index = lax.axis_index("segment")
     channels = weights.shape[2]
     bits = bit_count(dp_count)
     gather_order = list(range(bits - 2, 0, -1)) + [bits - 1, 0]
-    gathered = gather_by_halves(weights[0][None], "dp", gather_order)
+    gathered = gather_by_halves(weights[0][None], DP, gather_order)
     kernel = gathered.reshape(3, 3, 3, channels, channels)
     fields = acts[0]
     micro_count, size_x, size_y, size_z = fields.shape[:4]
@@ -126,23 +130,28 @@
             sender = segments - 1 - tick
             incoming = lax.ppermute(down_grad, "segment", [(sender, sender - 1)])
 
-    grad_term = conv_kernel_grad(fields, slope_held).reshape(dp_count, -1, channels)
-    reduced = reduce_by_halves(grad_term, "dp", gather_order[::-1])
     scale_factor = 1.0 / math.sqrt(dp_count * micro_count * cell_count)
-    return (grads_held[None], reduced * scale_factor)
+    grad_term = conv_kernel_grad(fields, slope_held) * scale_factor
+    grad_term = grad_term.reshape(dp_count, -1, channels)
+    reduced = reduce_by_halves(grad_term, DP, [0, bits - 1], "z")
+    return (grads_held[None], reduced)
 
 
 def solution(mesh):
+    segments, dp_count = mesh.devices.shape
+    fine = jax.sharding.Mesh(
+        mesh.devices.reshape(segments, 2, dp_count // 4, 2), ("segment",) + DP
+    )
     return jax.shard_map(
         local,
-        mesh=mesh,
+        mesh=fine,
         in_specs=(
-            P("segment", "dp", None, None, None, None),
-            P("segment", "dp", None),
+            P("segment", DP, None, None, None, None),
+            P("segment", DP, None),
             P("segment", None, None),
-            P("dp", None),
-            P("dp", None, None, None, None),
+            P(DP, None),
+            P(DP, None, None, None, None),
         ),
-        out_specs=(P("segment", "dp", None, None, None, None), P("segment", "dp", None)),
+        out_specs=(P("segment", DP, None, None, None, None), P("segment", DP, None)),
         check_vma=False,
     )

time: 177 us -> 165 us (0.932)
  the two profiles are of different devices: /device:TPU:8 before, /device:TPU:32 now
where the time goes in v6:
time: 165 us; the launch traced here: 164 us
  waiting for transfers between devices  76.3 us (46%)
  starting transfers between devices  51 us (31%)
  matrix products  22.5 us (14%)
  local copies, waits for them, and re-layouts  6.72 us (4%)
  other arithmetic  6.41 us (4%)
    ppermute x7, waiting for transfers between devices, local(): incoming = lax.ppermute(down_grad, 'segment', [(sender, sender - 1)])  37.4 us
    ppermute x8, starting transfers between devices, exchanged(): return lax.ppermute(array, axis, [(i, i ^ mask) for i in range(length)])  36.3 us
    ppermute x8, waiting for transfers between devices, exchanged(): return lax.ppermute(array, axis, [(i, i ^ mask) for i in range(length)])  26.4 us
    conv_general_dilated x8, matrix products, conv_transposed(): lax.conv_general_dilated(slope, flipped, (1, 1, 1), [(1, 1)] * 3, dimensi...  15.9 us
    all_to_all x1, waiting for transfers between devices, reduce_by_halves(): received = lax.all_to_all(held, ring_axis, 0, 0, tiled=True)  12.5 us
    all_to_all x1, starting transfers between devices, reduce_by_halves(): received = lax.all_to_all(held, ring_axis, 0, 0, tiled=True)  9.13 us
    ppermute x7, starting transfers between devices, local(): incoming = lax.ppermute(down_grad, 'segment', [(sender, sender - 1)])  5.49 us
    conv_general_dilated x1, matrix products, conv_kernel_grad(): lax.conv_general_dilated(field, slope, (1, 1, 1), [(1, 1)] * 3, dimension...  4.67 us
  transfers between devices with their start and end apart: 16, of which 9 were waited for; matrix products, arithmetic and copies ran while one was open for 7% of the time, Pallas kernels for 0%

profile of v6, /device:TPU:32, one launch (start us, length us, event | category | flops | bytes accessed | tf_op | source)
XLA Modules:
  0.0 164.1 jit_solution(1186884752763129693)
XLA Ops:
  0.6 14.8 %collective-permute-start = (bf16[1,54,128]{2,1,0:T(8,128)(2,1)}, bf16[1,54,128]{2,1,0:T(8,128)(2,1)S(1)}, u32[]{:S(2)}, u32[]{:S(2)}) collective-permute-start(bf16[1,54,128]{2,1,0:T(8,128)(2,1)} %param.6), channel_id=1, source_target_pairs={{0,16},{1,17},{2,18},{3,19},{4,20},{5,21},{6,22},{7,23},{8,24},{9,... | collective-permute-start | bytes 41480 | tf_op jit(solution)/shard_map/ppermute | solution.py:21
  22.5 4.3 %collective-permute-start.1 = (bf16[2,1,54,128]{3,2,0,1:T(8,128)(2,1)S(1)}, bf16[2,1,54,128]{3,2,0,1:T(8,128)(2,1)S(1)}, u32[]{:S(2)}, u32[]{:S(2)}) collective-permute-start(bf16[2,1,54,128]{3,2,0,1:T(8,128)(2,1)S(1)} %fusion.33), channel_id=1, source_target_pairs={{0,8},{1,9},{2,10},{3,11},{4,12},{5,13},{6,14},{7,15},{8,0},{9,1},... | collective-permute-start | bytes 82952 | tf_op jit(solution)/shard_map/ppermute | solution.py:21
  26.9 5.3 %collective-permute-done.1 = bf16[2,1,54,128]{3,2,0,1:T(8,128)(2,1)S(1)} collective-permute-done((bf16[2,1,54,128]{3,2,0,1:T(8,128)(2,1)S(1)}, bf16[2,1,54,128]{3,2,0,1:T(8,128)(2,1)S(1)}, u32[]{:S(2)}, u32[]{:S(2)}) %collective-permute-start.1) | collective-permute-done | bytes 27680 | tf_op jit(solution)/shard_map/ppermute | solution.py:21
  32.3 3.4 %collective-permute-start.2 = (bf16[2,2,1,54,128]{4,3,1,0,2:T(8,128)(2,1)S(1)}, bf16[2,2,1,54,128]{4,3,1,0,2:T(8,128)(2,1)S(1)}, u32[]{:S(2)}, u32[]{:S(2)}) collective-permute-start(bf16[2,2,1,54,128]{4,3,1,0,2:T(8,128)(2,1)S(1)} %fusion.31), channel_id=1, source_target_pairs={{0,4},{1,5},{2,6},{3,7},{4,0},{5,1},{6,2},{7,3},{8,12},{9,13},{10,... | collective-permute-start | bytes 165896 | tf_op jit(solution)/shard_map/ppermute | solution.py:21
  35.7 3.6 %collective-permute-done.2 = bf16[2,2,1,54,128]{4,3,1,0,2:T(8,128)(2,1)S(1)} collective-permute-done((bf16[2,2,1,54,128]{4,3,1,0,2:T(8,128)(2,1)S(1)}, bf16[2,2,1,54,128]{4,3,1,0,2:T(8,128)(2,1)S(1)}, u32[]{:S(2)}, u32[]{:S(2)}) %collective-permute-start.2) | collective-permute-done | bytes 55328 | tf_op jit(solution)/shard_map/ppermute | solution.py:21
  39.3 3.9 %collective-permute-start.3 = (bf16[2,2,2,1,54,128]{5,4,2,1,0,3:T(8,128)(2,1)S(1)}, bf16[2,2,2,1,54,128]{5,4,2,1,0,3:T(8,128)(2,1)S(1)}, u32[]{:S(2)}, u32[]{:S(2)}) collective-permute-start(bf16[2,2,2,1,54,128]{5,4,2,1,0,3:T(8,128)(2,1)S(1)} %fusion.26), channel_id=1, source_target_pairs={{0,2},{1,3},{2,0},{3,1},{4,6},{5,7},{6,4},{7,5},{8,10},{9,11},{10,... | collective-permute-start | bytes 331784 | tf_op jit(solution)/shard_map/ppermute | solution.py:21
  43.4 2.7 %collective-permute-done.3 = bf16[2,2,2,1,54,128]{5,4,2,1,0,3:T(8,128)(2,1)S(1)} collective-permute-done((bf16[2,2,2,1,54,128]{5,4,2,1,0,3:T(8,128)(2,1)S(1)}, bf16[2,2,2,1,54,128]{5,4,2,1,0,3:T(8,128)(2,1)S(1)}, u32[]{:S(2)}, u32[]{:S(2)}) %collective-permute-start.3) | collective-permute-done | bytes 110624 | tf_op jit(solution)/shard_map/ppermute | solution.py:21
  46.1 3.5 %collective-permute-start.4 = (bf16[2,2,2,2,1,54,128]{6,5,3,2,1,0,4:T(8,128)(2,1)S(1)}, bf16[2,2,2,2,1,54,128]{6,5,3,2,1,0,4:T(8,128)(2,1)S(1)}, u32[]{:S(2)}, u32[]{:S(2)}) collective-permute-start(bf16[2,2,2,2,1,54,128]{6,5,3,2,1,0,4:T(8,128)(2,1)S(1)} %fusion.24), channel_id=1, source_target_pairs={{0,32},{1,33},{2,34},{3,35},{4,36},{5,37},{6,38},{7,39},{8,40},{9,... | collective-permute-start | bytes 663560 | tf_op jit(solution)/shard_map/ppermute | solution.py:21
  49.7 4.3 %collective-permute-done.4 = bf16[2,2,2,2,1,54,128]{6,5,3,2,1,0,4:T(8,128)(2,1)S(1)} collective-permute-done((bf16[2,2,2,2,1,54,128]{6,5,3,2,1,0,4:T(8,128)(2,1)S(1)}, bf16[2,2,2,2,1,54,128]{6,5,3,2,1,0,4:T(8,128)(2,1)S(1)}, u32[]{:S(2)}, u32[]{:S(2)}) %collective-permute-start.4) | collective-permute-done | bytes 221216 | tf_op jit(solution)/shard_map/ppermute | solution.py:21
  54.2 1.9 %collective-permute-start.5 = (bf16[2,2,2,2,2,1,54,128]{7,6,4,3,2,1,0,5:T(8,128)(2,1)S(1)}, bf16[2,2,2,2,2,1,54,128]{7,6,4,3,2,1,0,5:T(8,128)(2,1)S(1)}, u32[]{:S(2)}, u32[]{:S(2)}) collective-permute-start(bf16[2,2,2,2,2,1,54,128]{7,6,4,3,2,1,0,5:T(8,128)(2,1)S(1)} %fusion.13), channel_id=1, source_target_pairs={{0,1},{1,0},{2,3},{3,2},{4,5},{5,4},{6,7},{7,6},{8,9},{9,8},{10,11... | collective-permute-start | bytes 1327112 | tf_op jit(solution)/shard_map/ppermute | solution.py:21
  59.0 1.9 %add_multiply_fusion = f32[2,4,8,8,128]{4,0,3,2,1:T(2,128)S(1)} fusion(f32[1,4,8,8,128]{4,0,3,2,1:T(1,128)S(1)} %broadcast_add_fusion, f32[1,4,8,8,128]{4,0,3,2,1:T(1,128)S(1)} %broadcast_add_fusion.1, bf16[3,3,3,128,128]{4,3,2,1,0:T(8,128)(2,1)S(1)} %reshape_reshape.6, bf16[2,4,8,8,128]{4,3,2,1,0:T(8,128)(2,1)S(1)} %bitcast.115), kind=kOutput, calls=%fused_computation.50 | convolution fusion | flops 317784064 | bytes 1540096 | tf_op jit(solution)/shard_map/conv_general_dilated | solution.py:61
  63.3 1.8 %fusion.1 = bf16[2,4,8,8,128]{4,0,3,2,1:T(2,128)(2,1)S(1)} fusion(bf16[3,3,3,128,128]{4,3,2,1,0:T(8,128)(2,1)S(1)} %reshape_reshape.6, f32[2,4,8,8,128]{4,0,3,2,1:T(2,128)S(1)} %add_multiply_fusion, bf16[2,4,8,8,128]{4,0,3,2,1:T(2,128)(2,1)S(1)} %collective-permute-done.6, pred[]{:T(512)S(6)} %eq.52, bf16[2,4,8,8,128]{4,3,2,1,0:T(8,128)(2,1)S(1)} %copy-done.2), kind=kOutput, calls=%fused_computation.11 | convolution fusion | flops 317718528 | bytes 1540097 | tf_op jit(solution)/shard_map/conv_general_dilated | solution.py:70
  65.8 1.8 %fusion.2 = bf16[2,4,8,8,128]{4,0,3,2,1:T(2,128)(2,1)S(1)} fusion(bf16[3,3,3,128,128]{4,3,2,1,0:T(8,128)(2,1)S(1)} %reshape_reshape.6, f32[2,4,8,8,128]{4,0,3,2,1:T(2,128)S(1)} %add_multiply_fusion, bf16[2,4,8,8,128]{4,0,3,2,1:T(2,128)(2,1)S(1)} %collective-permute-done.7, pred[]{:T(512)S(6)} %eq.52, bf16[2,4,8,8,128]{4,3,2,1,0:T(8,128)(2,1)S(1)} %copy-done.2), kind=kOutput, calls=%fused_computation.12 | convolution fusion | flops 317718528 | bytes 1540097 | tf_op jit(solution)/shard_map/conv_general_dilated | solution.py:70
  73.4 1.8 %fusion.5 = bf16[2,4,8,8,128]{4,0,3,2,1:T(2,128)(2,1)S(1)} fusion(bf16[3,3,3,128,128]{4,3,2,1,0:T(8,128)(2,1)S(1)} %reshape_reshape.6, f32[2,4,8,8,128]{4,0,3,2,1:T(2,128)S(1)} %add_multiply_fusion, bf16[2,4,8,8,128]{4,0,3,2,1:T(2,128)(2,1)S(1)} %collective-permute-done.10, pred[]{:T(512)S(6)} %eq.52, bf16[2,4,8,8,128]{4,3,2,1,0:T(8,128)(2,1)S(1)} %copy-done.2), kind=kOutput, calls=%fused_computation.15 | convolution fusion | flops 317718528 | bytes 1540097 | tf_op jit(solution)/shard_map/conv_general_dilated | solution.py:70
  75.9 1.8 %fusion.6 = bf16[2,4,8,8,128]{4,0,3,2,1:T(2,128)(2,1)S(1)} fusion(bf16[3,3,3,128,128]{4,3,2,1,0:T(8,128)(2,1)S(1)} %reshape_reshape.6, f32[2,4,8,8,128]{4,0,3,2,1:T(2,128)S(1)} %add_multiply_fusion, bf16[2,4,8,8,128]{4,0,3,2,1:T(2,128)(2,1)S(1)} %collective-permute-done.11, pred[]{:T(512)S(6)} %eq.52, bf16[2,4,8,8,128]{4,3,2,1,0:T(8,128)(2,1)S(1)} %copy-done.2), kind=kOutput, calls=%fused_computation.16 | convolution fusion | flops 317718528 | bytes 1540097 | tf_op jit(solution)/shard_map/conv_general_dilated | solution.py:70
  79.0 37.4 %collective-permute-done.12 = bf16[2,4,8,8,128]{4,0,3,2,1:T(2,128)(2,1)S(1)} collective-permute-done((bf16[2,4,8,8,128]{4,0,3,2,1:T(2,128)(2,1)S(1)}, bf16[2,4,8,8,128]{4,0,3,2,1:T(2,128)(2,1)S(1)}, u32[]{:S(2)}, u32[]{:S(2)}) %collective-permute-start.12) | collective-permute-done | bytes 131104 | tf_op jit(solution)/shard_map/ppermute | solution.py:131
  117.1 4.7 %convolution_multiply_fusion = f32[3,3,3,128,128]{4,3,2,1,0:T(8,128)} fusion(pred[]{:T(512)S(6)} %eq.51, pred[]{:T(512)S(6)} %eq.59, pred[]{:T(512)S(6)} %eq.60, pred[]{:T(512)S(6)} %eq.61, pred[]{:T(512)S(6)} %eq.62, pred[]{:T(512)S(6)} %eq.63, pred[]{:T(512)S(6)} %eq.64, pred[]{:T(512)S(6)} %eq.52, bf16[2,4,8,8,128]{4,3,2,1,0:T(8,128)(2,1)S(1)} %bitcast.116, ...), kind=kOutput, calls=%fused_computation | convolution fusion | flops 320258048 | bytes 3211272 | tf_op jit(solution)/shard_map/conv_general_dilated | solution.py:78
  123.4 1.9 %collective-permute-start.13 = (bf16[2,2,2,2,2,54,128]{6,5,4,3,2,1,0:T(8,128)(2,1)S(1)}, bf16[2,2,2,2,2,54,128]{6,5,4,3,2,1,0:T(8,128)(2,1)S(1)}, u32[]{:S(2)}, u32[]{:S(2)}) collective-permute-start(bf16[2,2,2,2,2,54,128]{6,5,4,3,2,1,0:T(8,128)(2,1)S(1)} %fusion.11), channel_id=1, source_target_pairs={{0,1},{1,0},{2,3},{3,2},{4,5},{5,4},{6,7},{7,6},{8,9},{9,8},{10,11... | collective-permute-start | bytes 1327112 | tf_op jit(solution)/shard_map/ppermute | solution.py:21
  125.3 1.8 %collective-permute-done.13 = bf16[2,2,2,2,2,54,128]{6,5,4,3,2,1,0:T(8,128)(2,1)S(1)} collective-permute-done((bf16[2,2,2,2,2,54,128]{6,5,4,3,2,1,0:T(8,128)(2,1)S(1)}, bf16[2,2,2,2,2,54,128]{6,5,4,3,2,1,0:T(8,128)(2,1)S(1)}, u32[]{:S(2)}, u32[]{:S(2)}) %collective-permute-start.13) | collective-permute-done | bytes 442400 | tf_op jit(solution)/shard_map/ppermute | solution.py:21
  127.2 2.6 %collective-permute-start.14 = (bf16[2,2,2,2,54,128]{5,4,3,2,1,0:T(8,128)(2,1)S(1)}, bf16[2,2,2,2,54,128]{5,4,3,2,1,0:T(8,128)(2,1)S(1)}, u32[]{:S(2)}, u32[]{:S(2)}) collective-permute-start(bf16[2,2,2,2,54,128]{5,4,3,2,1,0:T(8,128)(2,1)S(1)} %fusion.23), channel_id=1, source_target_pairs={{0,32},{1,33},{2,34},{3,35},{4,36},{5,37},{6,38},{7,39},{8,40},{9,... | collective-permute-start | bytes 663560 | tf_op jit(solution)/shard_map/ppermute | solution.py:21
  129.8 7.0 %collective-permute-done.14 = bf16[2,2,2,2,54,128]{5,4,3,2,1,0:T(8,128)(2,1)S(1)} collective-permute-done((bf16[2,2,2,2,54,128]{5,4,3,2,1,0:T(8,128)(2,1)S(1)}, bf16[2,2,2,2,54,128]{5,4,3,2,1,0:T(8,128)(2,1)S(1)}, u32[]{:S(2)}, u32[]{:S(2)}) %collective-permute-start.14) | collective-permute-done | bytes 221216 | tf_op jit(solution)/shard_map/ppermute | solution.py:21
  137.5 9.1 %all-to-all-start = ((bf16[16,54,128]{2,1,0:T(8,128)(2,1)}), bf16[16,54,128]{2,1,0:T(8,128)(2,1)S(1)}, u32[]{:S(2)}, u32[]{:S(2)}) async-start(bf16[16,54,128]{2,1,0:T(8,128)(2,1)} %bitcast.43), calls=%async_computation | async-start | bytes 458752 | tf_op jit(solution)/shard_map/all_to_all | solution.py:56
  146.6 3.6 %fusion.9 = bf16[1,2,4,8,8,128]{5,1,4,3,2,0:T(2,128)(2,1)S(1)} fusion(bf16[3,3,3,128,128]{4,3,2,1,0:T(8,128)(2,1)} %copy-done, pred[]{:T(512)S(6)} %eq.51, bf16[2,4,8,8,128]{4,0,3,2,1:T(2,128)(2,1)} %copy-done.8, pred[]{:T(512)S(6)} %eq.59, bf16[2,4,8,8,128]{4,0,3,2,1:T(2,128)(2,1)} %copy-done.7, pred[]{:T(512)S(6)} %eq.60, ...), kind=kOutput, calls=%fused_computation.19 | convolution fusion | flops 318242816 | bytes 2457608 | tf_op jit(solution)/shard_map/conv_general_dilated | solution.py:70
  150.9 12.5 %all-to-all-done = bf16[16,54,128]{2,1,0:T(8,128)(2,1)S(1)} async-done(((bf16[16,54,128]{2,1,0:T(8,128)(2,1)}), bf16[16,54,128]{2,1,0:T(8,128)(2,1)S(1)}, u32[]{:S(2)}, u32[]{:S(2)}) %all-to-all-start) | async-done | bytes 221216 | tf_op jit(solution)/shard_map/all_to_all | solution.py:56
  (79 shorter events, 25.6 us)
Async XLA Ops:
  0.6 21.2 %collective-permute-start = (bf16[1,54,128]{2,1,0:T(8,128)(2,1)}, bf16[1,54,128]{2,1,0:T(8,128)(2,1)S(1)}, u32[]{:S(2)}, u32[]{:S(2)}) collective-permute-start(bf16[1,54,128]{2,1,0:T(8,128)(2,1)} %param.6), channel_id=1, source_target_pairs={{0,16},{1,17},{2,18},{3,19},{4,20},{5,21},{6,22},{7,23},{8,24},{9,... | collective-permute-start | bytes 41480 | tf_op jit(solution)/shard_map/ppermute | solution.py:21
  22.5 9.7 %collective-permute-start.1 = (bf16[2,1,54,128]{3,2,0,1:T(8,128)(2,1)S(1)}, bf16[2,1,54,128]{3,2,0,1:T(8,128)(2,1)S(1)}, u32[]{:S(2)}, u32[]{:S(2)}) collective-permute-start(bf16[2,1,54,128]{3,2,0,1:T(8,128)(2,1)S(1)} %fusion.33), channel_id=1, source_target_pairs={{0,8},{1,9},{2,10},{3,11},{4,12},{5,13},{6,14},{7,15},{8,0},{9,1},... | collective-permute-start | bytes 82952 | tf_op jit(solution)/shard_map/ppermute | solution.py:21
  32.3 7.0 %collective-permute-start.2 = (bf16[2,2,1,54,128]{4,3,1,0,2:T(8,128)(2,1)S(1)}, bf16[2,2,1,54,128]{4,3,1,0,2:T(8,128)(2,1)S(1)}, u32[]{:S(2)}, u32[]{:S(2)}) collective-permute-start(bf16[2,2,1,54,128]{4,3,1,0,2:T(8,128)(2,1)S(1)} %fusion.31), channel_id=1, source_target_pairs={{0,4},{1,5},{2,6},{3,7},{4,0},{5,1},{6,2},{7,3},{8,12},{9,13},{10,... | collective-permute-start | bytes 165896 | tf_op jit(solution)/shard_map/ppermute | solution.py:21
  39.3 6.7 %collective-permute-start.3 = (bf16[2,2,2,1,54,128]{5,4,2,1,0,3:T(8,128)(2,1)S(1)}, bf16[2,2,2,1,54,128]{5,4,2,1,0,3:T(8,128)(2,1)S(1)}, u32[]{:S(2)}, u32[]{:S(2)}) collective-permute-start(bf16[2,2,2,1,54,128]{5,4,2,1,0,3:T(8,128)(2,1)S(1)} %fusion.26), channel_id=1, source_target_pairs={{0,2},{1,3},{2,0},{3,1},{4,6},{5,7},{6,4},{7,5},{8,10},{9,11},{10,... | collective-permute-start | bytes 331784 | tf_op jit(solution)/shard_map/ppermute | solution.py:21
  46.1 7.9 %collective-permute-start.4 = (bf16[2,2,2,2,1,54,128]{6,5,3,2,1,0,4:T(8,128)(2,1)S(1)}, bf16[2,2,2,2,1,54,128]{6,5,3,2,1,0,4:T(8,128)(2,1)S(1)}, u32[]{:S(2)}, u32[]{:S(2)}) collective-permute-start(bf16[2,2,2,2,1,54,128]{6,5,3,2,1,0,4:T(8,128)(2,1)S(1)} %fusion.24), channel_id=1, source_target_pairs={{0,32},{1,33},{2,34},{3,35},{4,36},{5,37},{6,38},{7,39},{8,40},{9,... | collective-permute-start | bytes 663560 | tf_op jit(solution)/shard_map/ppermute | solution.py:21
  54.2 3.7 %collective-permute-start.5 = (bf16[2,2,2,2,2,1,54,128]{7,6,4,3,2,1,0,5:T(8,128)(2,1)S(1)}, bf16[2,2,2,2,2,1,54,128]{7,6,4,3,2,1,0,5:T(8,128)(2,1)S(1)}, u32[]{:S(2)}, u32[]{:S(2)}) collective-permute-start(bf16[2,2,2,2,2,1,54,128]{7,6,4,3,2,1,0,5:T(8,128)(2,1)S(1)} %fusion.13), channel_id=1, source_target_pairs={{0,1},{1,0},{2,3},{3,2},{4,5},{5,4},{6,7},{7,6},{8,9},{9,8},{10,11... | collective-permute-start | bytes 1327112 | tf_op jit(solution)/shard_map/ppermute | solution.py:21
  58.4 17.5 %copy-start = (bf16[3,3,3,128,128]{4,3,2,1,0:T(8,128)(2,1)}, bf16[3,3,3,128,128]{4,3,2,1,0:T(8,128)(2,1)S(1)}, u32[]{:S(2)}) copy-start(bf16[3,3,3,128,128]{4,3,2,1,0:T(8,128)(2,1)S(1)} %reshape_reshape.6) | copy-start | bytes 2654212
  60.9 55.5 %copy-start.10 = (f32[2,4,8,8,128]{4,0,3,2,1:T(2,128)}, f32[2,4,8,8,128]{4,0,3,2,1:T(2,128)S(1)}, u32[]{:S(2)}) copy-start(f32[2,4,8,8,128]{4,0,3,2,1:T(2,128)S(1)} %add_multiply_fusion) | copy-start | bytes 786436
  62.6 0.7 collective-permute-start.6
  65.1 2.5 %copy-start.3 = (bf16[2,4,8,8,128]{4,0,3,2,1:T(2,128)(2,1)}, bf16[2,4,8,8,128]{4,0,3,2,1:T(2,128)(2,1)S(1)}, u32[]{:S(2)}) copy-start(bf16[2,4,8,8,128]{4,0,3,2,1:T(2,128)(2,1)S(1)} %fusion.1) | copy-start | bytes 393220
  65.1 0.7 collective-permute-start.7
  67.6 2.5 %copy-start.4 = (bf16[2,4,8,8,128]{4,0,3,2,1:T(2,128)(2,1)}, bf16[2,4,8,8,128]{4,0,3,2,1:T(2,128)(2,1)S(1)}, u32[]{:S(2)}) copy-start(bf16[2,4,8,8,128]{4,0,3,2,1:T(2,128)(2,1)S(1)} %fusion.2) | copy-start | bytes 393220
  67.6 0.7 collective-permute-start.8
  70.1 2.7 %copy-start.5 = (bf16[2,4,8,8,128]{4,0,3,2,1:T(2,128)(2,1)}, bf16[2,4,8,8,128]{4,0,3,2,1:T(2,128)(2,1)S(1)}, u32[]{:S(2)}) copy-start(bf16[2,4,8,8,128]{4,0,3,2,1:T(2,128)(2,1)S(1)} %fusion.3) | copy-start | bytes 393220
  70.1 0.9 collective-permute-start.9
  72.7 2.5 %copy-start.6 = (bf16[2,4,8,8,128]{4,0,3,2,1:T(2,128)(2,1)}, bf16[2,4,8,8,128]{4,0,3,2,1:T(2,128)(2,1)S(1)}, u32[]{:S(2)}) copy-start(bf16[2,4,8,8,128]{4,0,3,2,1:T(2,128)(2,1)S(1)} %fusion.4) | copy-start | bytes 393220
  72.7 0.7 collective-permute-start.10
  75.2 2.5 %copy-start.7 = (bf16[2,4,8,8,128]{4,0,3,2,1:T(2,128)(2,1)}, bf16[2,4,8,8,128]{4,0,3,2,1:T(2,128)(2,1)S(1)}, u32[]{:S(2)}) copy-start(bf16[2,4,8,8,128]{4,0,3,2,1:T(2,128)(2,1)S(1)} %fusion.5) | copy-start | bytes 393220
  75.2 0.7 collective-permute-start.11
  77.7 38.7 %copy-start.8 = (bf16[2,4,8,8,128]{4,0,3,2,1:T(2,128)(2,1)}, bf16[2,4,8,8,128]{4,0,3,2,1:T(2,128)(2,1)S(1)}, u32[]{:S(2)}) copy-start(bf16[2,4,8,8,128]{4,0,3,2,1:T(2,128)(2,1)S(1)} %fusion.6) | copy-start | bytes 393220
  77.7 38.7 %collective-permute-start.12 = (bf16[2,4,8,8,128]{4,0,3,2,1:T(2,128)(2,1)S(1)}, bf16[2,4,8,8,128]{4,0,3,2,1:T(2,128)(2,1)S(1)}, u32[]{:S(2)}, u32[]{:S(2)}) collective-permute-start(bf16[2,4,8,8,128]{4,0,3,2,1:T(2,128)(2,1)S(1)} %fusion.6), channel_id=1, source_target_pairs={{64,0},{65,1},{66,2},{67,3},{68,4},{69,5},{70,6},{71,7},{72,8},{73... | collective-permute-start | bytes 393224 | tf_op jit(solution)/shard_map/ppermute | solution.py:131
  123.4 3.7 %collective-permute-start.13 = (bf16[2,2,2,2,2,54,128]{6,5,4,3,2,1,0:T(8,128)(2,1)S(1)}, bf16[2,2,2,2,2,54,128]{6,5,4,3,2,1,0:T(8,128)(2,1)S(1)}, u32[]{:S(2)}, u32[]{:S(2)}) collective-permute-start(bf16[2,2,2,2,2,54,128]{6,5,4,3,2,1,0:T(8,128)(2,1)S(1)} %fusion.11), channel_id=1, source_target_pairs={{0,1},{1,0},{2,3},{3,2},{4,5},{5,4},{6,7},{7,6},{8,9},{9,8},{10,11... | collective-permute-start | bytes 1327112 | tf_op jit(solution)/shard_map/ppermute | solution.py:21
  127.2 9.5 %collective-permute-start.14 = (bf16[2,2,2,2,54,128]{5,4,3,2,1,0:T(8,128)(2,1)S(1)}, bf16[2,2,2,2,54,128]{5,4,3,2,1,0:T(8,128)(2,1)S(1)}, u32[]{:S(2)}, u32[]{:S(2)}) collective-permute-start(bf16[2,2,2,2,54,128]{5,4,3,2,1,0:T(8,128)(2,1)S(1)} %fusion.23), channel_id=1, source_target_pairs={{0,32},{1,33},{2,34},{3,35},{4,36},{5,37},{6,38},{7,39},{8,40},{9,... | collective-permute-start | bytes 663560 | tf_op jit(solution)/shard_map/ppermute | solution.py:21
  137.5 25.9 %all-to-all-start = ((bf16[16,54,128]{2,1,0:T(8,128)(2,1)}), bf16[16,54,128]{2,1,0:T(8,128)(2,1)S(1)}, u32[]{:S(2)}, u32[]{:S(2)}) async-start(bf16[16,54,128]{2,1,0:T(8,128)(2,1)} %bitcast.43), calls=%async_computation | async-start | bytes 458752 | tf_op jit(solution)/shard_map/all_to_all | solution.py:56
  (3 other events, 3.5 us)

commit v7 on v6

--- a/solution.py
+++ b/solution.py
@@ -25,18 +25,17 @@
     return length.bit_length() - 1
 
 
-def gather_by_halves(block, axis, order):
+def gather_by_halves(block, axis, order, ring_axis):
     index = lax.axis_index(axis)
-    held = block
+    ring = lax.axis_size(ring_axis)
+    held = lax.all_to_all(jnp.broadcast_to(block, (ring,) + block.shape), ring_axis, 0, 0, tiled=True)
     for bit in order:
         upper = ((index >> bit) & 1) == 1
         received = exchanged(held, axis, 1 << bit)
         low = jnp.where(upper, received, held)
         high = jnp.where(upper, held, received)
         held = jnp.stack([low, high])
-    done = len(order)
-    natural = [done - 1 - order.index(bit) for bit in range(done - 1, -1, -1)]
-    held = jnp.transpose(held, natural + list(range(done, held.ndim)))
+    held = jnp.moveaxis(held, 0, len(order))
     return held.reshape((-1,) + block.shape[1:])
 
 
@@ -82,16 +81,14 @@
     )
 
 
-def position_term(anchor, pos_gain, size_x, size_y, size_z):
-    phases = []
-    for axis_num, axis_len in enumerate((size_x, size_y, size_z)):
-        coords = anchor[axis_num] + STRIDE * jnp.arange(axis_len, dtype=jnp.int32)
-        phase_val = (coords % WAVE).astype(jnp.float32)
-        phases.append(jnp.sin(phase_val * (2.0 * math.pi / WAVE)))
+def position_terms(anchors, pos_gain, size_x, size_y, size_z):
+    longest = max(size_x, size_y, size_z)
+    coords = anchors[:, :, None] + STRIDE * jnp.arange(longest, dtype=jnp.int32)
+    phases = jnp.sin((coords % WAVE).astype(jnp.float32) * (2.0 * math.pi / WAVE))
     return (
-        phases[0][:, None, None, None] * pos_gain[0]
-        + phases[1][None, :, None, None] * pos_gain[1]
-        + phases[2][None, None, :, None] * pos_gain[2]
+        phases[:, 0, :size_x, None, None, None] * pos_gain[0]
+        + phases[:, 1, None, :size_y, None, None] * pos_gain[1]
+        + phases[:, 2, None, None, :size_z, None] * pos_gain[2]
     )
 
 
@@ -101,16 +98,13 @@
     segment_index = lax.axis_index("segment")
     channels = weights.shape[2]
     bits = bit_count(dp_count)
-    gather_order = list(range(bits - 2, 0, -1)) + [bits - 1, 0]
-    gathered = gather_by_halves(weights[0][None], DP, gather_order)
+    gathered = gather_by_halves(weights[0], DP, [bits - 1, 0], "z")
     kernel = gathered.reshape(3, 3, 3, channels, channels)
     fields = acts[0]
     micro_count, size_x, size_y, size_z = fields.shape[:4]
     cell_count = size_x * size_y * size_z
     pos_gain = pos_weight[0]
-    position_all = jnp.stack(
-        [position_term(anchors[m], pos_gain, size_x, size_y, size_z) for m in range(micro_count)]
-    )
+    position_all = position_terms(anchors, pos_gain, size_x, size_y, size_z)
     pre_act = conv_forward(fields, kernel) + position_all
     sigmoid_h = jax.nn.sigmoid(pre_act)
     silu_slope = sigmoid_h * (1.0 + pre_act * (1.0 - sigmoid_h))

time: 165 us -> 150 us (0.909)
  starting transfers between devices: 51 us -> 36.9 us
  other arithmetic: 6.41 us -> 1.44 us
  waiting for transfers between devices: 76.3 us -> 80.5 us
    ppermute x8 -> x4, starting transfers between devices: 36.3 us -> 9.9 us  [exchanged(): return lax.ppermute(array, axis, [(i, i ^ mask) for i in range(length)])]
    all_to_all x0 -> x1, starting transfers between devices: none -> 15.2 us  [gather_by_halves(): lax.all_to_all(jnp.broadcast_to(block, (ring,) + block.shape), ring_axis,...]
    all_to_all x0 -> x1, waiting for transfers between devices: none -> 15 us  [gather_by_halves(): lax.all_to_all(jnp.broadcast_to(block, (ring,) + block.shape), ring_axis,...]
    ppermute x8 -> x4, waiting for transfers between devices: 26.4 us -> 15.6 us  [exchanged(): return lax.ppermute(array, axis, [(i, i ^ mask) for i in range(length)])]
    sin x3 -> x1, other arithmetic: 3.98 us -> 0.13 us  [position_terms(): jnp.sin((coords % WAVE).astype(jnp.float32) * (2.0 * math.pi / WAVE))]
    all_to_all x1, starting transfers between devices: 9.13 us -> 6.31 us  [reduce_by_halves(): received = lax.all_to_all(held, ring_axis, 0, 0, tiled=True)]
  transfers between devices with their start and end apart: 16 -> 13, of which waited for: 9 -> 7; matrix products, arithmetic and copies ran while one was open for 7% -> 4% of each run, Pallas kernels for 0% -> 0%
where the time goes in v7:
time: 150 us
  waiting for transfers between devices  80.5 us (54%)
  starting transfers between devices  36.9 us (25%)
  matrix products  22.4 us (15%)
  local copies, waits for them, and re-layouts  7.56 us (5%)
    ppermute x7, waiting for transfers between devices, local(): incoming = lax.ppermute(down_grad, 'segment', [(sender, sender - 1)])  37.4 us
    conv_general_dilated x8, matrix products, conv_transposed(): lax.conv_general_dilated(slope, flipped, (1, 1, 1), [(1, 1)] * 3, dimensi...  15.9 us
    ppermute x4, waiting for transfers between devices, exchanged(): return lax.ppermute(array, axis, [(i, i ^ mask) for i in range(length)])  15.6 us
    all_to_all x1, starting transfers between devices, gather_by_halves(): lax.all_to_all(jnp.broadcast_to(block, (ring,) + block.shape), ring_axis,...  15.2 us
    all_to_all x1, waiting for transfers between devices, gather_by_halves(): lax.all_to_all(jnp.broadcast_to(block, (ring,) + block.shape), ring_axis,...  15 us
    all_to_all x1, waiting for transfers between devices, reduce_by_halves(): received = lax.all_to_all(held, ring_axis, 0, 0, tiled=True)  12.5 us
    ppermute x4, starting transfers between devices, exchanged(): return lax.ppermute(array, axis, [(i, i ^ mask) for i in range(length)])  9.9 us
    all_to_all x1, starting transfers between devices, reduce_by_halves(): received = lax.all_to_all(held, ring_axis, 0, 0, tiled=True)  6.31 us
  transfers between devices with their start and end apart: 13, of which 7 were waited for; matrix products, arithmetic and copies ran while one was open for 4% of the time, Pallas kernels for 0%

profile of v7, /device:TPU:32, one launch (start us, length us, event | category | flops | bytes accessed | tf_op | source)
XLA Modules:
  0.0 149.9 jit_solution(17503432322952283095)
XLA Ops:
  2.1 15.2 %all-to-all-start = ((bf16[16,54,128]{2,1,0:T(8,128)(2,1)}), bf16[16,54,128]{2,1,0:T(8,128)(2,1)S(1)}, u32[]{:S(2)}, u32[]{:S(2)}) async-start(bf16[16,54,128]{2,1,0:T(8,128)(2,1)} %broadcast_in_dim.11), calls=%async_computation | async-start | bytes 458752 | tf_op jit(solution)/shard_map/all_to_all | solution.py:31
  19.2 15.0 %all-to-all-done = bf16[16,54,128]{2,1,0:T(8,128)(2,1)S(1)} async-done(((bf16[16,54,128]{2,1,0:T(8,128)(2,1)}), bf16[16,54,128]{2,1,0:T(8,128)(2,1)S(1)}, u32[]{:S(2)}, u32[]{:S(2)}) %all-to-all-start) | async-done | bytes 221216 | tf_op jit(solution)/shard_map/all_to_all | solution.py:31
  34.2 3.5 %collective-permute-start = (bf16[16,54,128]{2,1,0:T(8,128)(2,1)S(1)}, bf16[16,54,128]{2,1,0:T(8,128)(2,1)S(1)}, u32[]{:S(2)}, u32[]{:S(2)}) collective-permute-start(bf16[16,54,128]{2,1,0:T(8,128)(2,1)S(1)} %all-to-all-done), channel_id=1, source_target_pairs={{0,32},{1,33},{2,34},{3,35},{4,36},{5,37},{6,38},{7,39},{8,40},{9,... | collective-permute-start | bytes 663560 | tf_op jit(solution)/shard_map/ppermute | solution.py:21
  37.8 5.2 %collective-permute-done = bf16[16,54,128]{2,1,0:T(8,128)(2,1)S(1)} collective-permute-done((bf16[16,54,128]{2,1,0:T(8,128)(2,1)S(1)}, bf16[16,54,128]{2,1,0:T(8,128)(2,1)S(1)}, u32[]{:S(2)}, u32[]{:S(2)}) %collective-permute-start) | collective-permute-done | bytes 221216 | tf_op jit(solution)/shard_map/ppermute | solution.py:21
  43.0 1.9 %collective-permute-start.1 = (bf16[2,16,54,128]{3,2,1,0:T(8,128)(2,1)S(1)}, bf16[2,16,54,128]{3,2,1,0:T(8,128)(2,1)S(1)}, u32[]{:S(2)}, u32[]{:S(2)}) collective-permute-start(bf16[2,16,54,128]{3,2,1,0:T(8,128)(2,1)S(1)} %pad_maximum_fusion), channel_id=1, source_target_pairs={{0,1},{1,0},{2,3},{3,2},{4,5},{5,4},{6,7},{7,6},{8,9},{9,8},{10,11... | collective-permute-start | bytes 1327112 | tf_op jit(solution)/shard_map/ppermute | solution.py:21
  45.1 1.7 %collective-permute-done.1 = bf16[2,16,54,128]{3,2,1,0:T(8,128)(2,1)S(1)} collective-permute-done((bf16[2,16,54,128]{3,2,1,0:T(8,128)(2,1)S(1)}, bf16[2,16,54,128]{3,2,1,0:T(8,128)(2,1)S(1)}, u32[]{:S(2)}, u32[]{:S(2)}) %collective-permute-start.1) | collective-permute-done | bytes 442400 | tf_op jit(solution)/shard_map/ppermute | solution.py:21
  47.7 1.8 %add_multiply_fusion = f32[2,4,8,8,128]{4,0,3,2,1:T(2,128)S(1)} fusion(bf16[3,3,3,128,128]{4,3,2,1,0:T(8,128)(2,1)S(1)} %reshape_reshape.6, f32[2,8,128]{2,0,1:T(2,128)S(1)} %get-tuple-element.15, f32[2,4,8,128]{3,0,2,1:T(2,128)S(1)} %broadcast_add_fusion, bf16[2,4,8,8,128]{4,3,2,1,0:T(8,128)(2,1)S(1)} %bitcast.51), kind=kOutput, calls=%fused_computation.47 | convolution fusion | flops 317784064 | bytes 1318912 | tf_op jit(solution)/shard_map/conv_general_dilated | solution.py:60
  49.5 1.7 %fusion = bf16[2,4,8,8,128]{4,0,3,2,1:T(2,128)(2,1)S(1)} fusion(bf16[3,3,3,128,128]{4,3,2,1,0:T(8,128)(2,1)S(1)} %reshape_reshape.6, pred[]{:T(512)S(6)} %eq.34, f32[2,4,8,8,128]{4,0,3,2,1:T(2,128)S(1)} %add_multiply_fusion, bf16[2,4,8,8,128]{4,3,2,1,0:T(8,128)(2,1)S(1)} %copy-done.2), kind=kOutput, calls=%fused_computation.10 | convolution fusion | flops 317718528 | bytes 1409025 | tf_op jit(solution)/shard_map/conv_general_dilated | solution.py:69
  51.9 1.8 %fusion.1 = bf16[2,4,8,8,128]{4,0,3,2,1:T(2,128)(2,1)S(1)} fusion(bf16[3,3,3,128,128]{4,3,2,1,0:T(8,128)(2,1)S(1)} %reshape_reshape.6, f32[2,4,8,8,128]{4,0,3,2,1:T(2,128)S(1)} %add_multiply_fusion, bf16[2,4,8,8,128]{4,0,3,2,1:T(2,128)(2,1)S(1)} %collective-permute-done.2, pred[]{:T(512)S(6)} %eq.34, bf16[2,4,8,8,128]{4,3,2,1,0:T(8,128)(2,1)S(1)} %copy-done.2), kind=kOutput, calls=%fused_computation.11 | convolution fusion | flops 317718528 | bytes 1540097 | tf_op jit(solution)/shard_map/conv_general_dilated | solution.py:69
  54.4 1.8 %fusion.2 = bf16[2,4,8,8,128]{4,0,3,2,1:T(2,128)(2,1)S(1)} fusion(bf16[3,3,3,128,128]{4,3,2,1,0:T(8,128)(2,1)S(1)} %reshape_reshape.6, f32[2,4,8,8,128]{4,0,3,2,1:T(2,128)S(1)} %add_multiply_fusion, bf16[2,4,8,8,128]{4,0,3,2,1:T(2,128)(2,1)S(1)} %collective-permute-done.3, pred[]{:T(512)S(6)} %eq.34, bf16[2,4,8,8,128]{4,3,2,1,0:T(8,128)(2,1)S(1)} %copy-done.2), kind=kOutput, calls=%fused_computation.12 | convolution fusion | flops 317718528 | bytes 1540097 | tf_op jit(solution)/shard_map/conv_general_dilated | solution.py:69
  56.9 1.8 %fusion.3 = bf16[2,4,8,8,128]{4,0,3,2,1:T(2,128)(2,1)S(1)} fusion(bf16[3,3,3,128,128]{4,3,2,1,0:T(8,128)(2,1)S(1)} %reshape_reshape.6, f32[2,4,8,8,128]{4,0,3,2,1:T(2,128)S(1)} %add_multiply_fusion, bf16[2,4,8,8,128]{4,0,3,2,1:T(2,128)(2,1)S(1)} %collective-permute-done.4, pred[]{:T(512)S(6)} %eq.34, bf16[2,4,8,8,128]{4,3,2,1,0:T(8,128)(2,1)S(1)} %copy-done.2), kind=kOutput, calls=%fused_computation.13 | convolution fusion | flops 317718528 | bytes 1540097 | tf_op jit(solution)/shard_map/conv_general_dilated | solution.py:69
  59.5 1.8 %fusion.4 = bf16[2,4,8,8,128]{4,0,3,2,1:T(2,128)(2,1)S(1)} fusion(bf16[3,3,3,128,128]{4,3,2,1,0:T(8,128)(2,1)S(1)} %reshape_reshape.6, f32[2,4,8,8,128]{4,0,3,2,1:T(2,128)S(1)} %add_multiply_fusion, bf16[2,4,8,8,128]{4,0,3,2,1:T(2,128)(2,1)S(1)} %collective-permute-done.5, pred[]{:T(512)S(6)} %eq.34, bf16[2,4,8,8,128]{4,3,2,1,0:T(8,128)(2,1)S(1)} %copy-done.2), kind=kOutput, calls=%fused_computation.14 | convolution fusion | flops 317718528 | bytes 1540097 | tf_op jit(solution)/shard_map/conv_general_dilated | solution.py:69
  62.0 1.8 %fusion.5 = bf16[2,4,8,8,128]{4,0,3,2,1:T(2,128)(2,1)S(1)} fusion(bf16[3,3,3,128,128]{4,3,2,1,0:T(8,128)(2,1)S(1)} %reshape_reshape.6, f32[2,4,8,8,128]{4,0,3,2,1:T(2,128)S(1)} %add_multiply_fusion, bf16[2,4,8,8,128]{4,0,3,2,1:T(2,128)(2,1)S(1)} %collective-permute-done.6, pred[]{:T(512)S(6)} %eq.34, bf16[2,4,8,8,128]{4,3,2,1,0:T(8,128)(2,1)S(1)} %copy-done.2), kind=kOutput, calls=%fused_computation.15 | convolution fusion | flops 317718528 | bytes 1540097 | tf_op jit(solution)/shard_map/conv_general_dilated | solution.py:69
  64.5 1.8 %fusion.6 = bf16[2,4,8,8,128]{4,0,3,2,1:T(2,128)(2,1)S(1)} fusion(bf16[3,3,3,128,128]{4,3,2,1,0:T(8,128)(2,1)S(1)} %reshape_reshape.6, f32[2,4,8,8,128]{4,0,3,2,1:T(2,128)S(1)} %add_multiply_fusion, bf16[2,4,8,8,128]{4,0,3,2,1:T(2,128)(2,1)S(1)} %collective-permute-done.7, pred[]{:T(512)S(6)} %eq.34, bf16[2,4,8,8,128]{4,3,2,1,0:T(8,128)(2,1)S(1)} %copy-done.2), kind=kOutput, calls=%fused_computation.16 | convolution fusion | flops 317718528 | bytes 1540097 | tf_op jit(solution)/shard_map/conv_general_dilated | solution.py:69
  67.6 37.4 %collective-permute-done.8 = bf16[2,4,8,8,128]{4,0,3,2,1:T(2,128)(2,1)S(1)} collective-permute-done((bf16[2,4,8,8,128]{4,0,3,2,1:T(2,128)(2,1)S(1)}, bf16[2,4,8,8,128]{4,0,3,2,1:T(2,128)(2,1)S(1)}, u32[]{:S(2)}, u32[]{:S(2)}) %collective-permute-start.8) | collective-permute-done | bytes 131104 | tf_op jit(solution)/shard_map/ppermute | solution.py:125
  105.7 4.7 %convolution_multiply_fusion = f32[3,3,3,128,128]{4,3,2,1,0:T(8,128)} fusion(pred[]{:T(512)S(6)} %eq.33, pred[]{:T(512)S(6)} %eq.37, pred[]{:T(512)S(6)} %eq.38, pred[]{:T(512)S(6)} %eq.39, pred[]{:T(512)S(6)} %eq.40, pred[]{:T(512)S(6)} %eq.41, pred[]{:T(512)S(6)} %eq.42, pred[]{:T(512)S(6)} %eq.34, bf16[2,4,8,8,128]{4,3,2,1,0:T(8,128)(2,1)S(1)} %bitcast.52, ...), kind=kOutput, calls=%fused_computation | convolution fusion | flops 320258048 | bytes 3211272 | tf_op jit(solution)/shard_map/conv_general_dilated | solution.py:77
  110.4 1.5 reshape_reshape.7
  112.0 1.9 %collective-permute-start.9 = (bf16[2,2,2,2,2,54,128]{6,5,4,3,2,1,0:T(8,128)(2,1)S(1)}, bf16[2,2,2,2,2,54,128]{6,5,4,3,2,1,0:T(8,128)(2,1)S(1)}, u32[]{:S(2)}, u32[]{:S(2)}) collective-permute-start(bf16[2,2,2,2,2,54,128]{6,5,4,3,2,1,0:T(8,128)(2,1)S(1)} %fusion.10), channel_id=1, source_target_pairs={{0,1},{1,0},{2,3},{3,2},{4,5},{5,4},{6,7},{7,6},{8,9},{9,8},{10,11... | collective-permute-start | bytes 1327112 | tf_op jit(solution)/shard_map/ppermute | solution.py:21
  113.9 1.8 %collective-permute-done.9 = bf16[2,2,2,2,2,54,128]{6,5,4,3,2,1,0:T(8,128)(2,1)S(1)} collective-permute-done((bf16[2,2,2,2,2,54,128]{6,5,4,3,2,1,0:T(8,128)(2,1)S(1)}, bf16[2,2,2,2,2,54,128]{6,5,4,3,2,1,0:T(8,128)(2,1)S(1)}, u32[]{:S(2)}, u32[]{:S(2)}) %collective-permute-start.9) | collective-permute-done | bytes 442400 | tf_op jit(solution)/shard_map/ppermute | solution.py:21
  115.8 2.6 %collective-permute-start.10 = (bf16[2,2,2,2,54,128]{5,4,3,2,1,0:T(8,128)(2,1)S(1)}, bf16[2,2,2,2,54,128]{5,4,3,2,1,0:T(8,128)(2,1)S(1)}, u32[]{:S(2)}, u32[]{:S(2)}) collective-permute-start(bf16[2,2,2,2,54,128]{5,4,3,2,1,0:T(8,128)(2,1)S(1)} %fusion.20), channel_id=1, source_target_pairs={{0,32},{1,33},{2,34},{3,35},{4,36},{5,37},{6,38},{7,39},{8,40},{9,... | collective-permute-start | bytes 663560 | tf_op jit(solution)/shard_map/ppermute | solution.py:21
  118.4 7.0 %collective-permute-done.10 = bf16[2,2,2,2,54,128]{5,4,3,2,1,0:T(8,128)(2,1)S(1)} collective-permute-done((bf16[2,2,2,2,54,128]{5,4,3,2,1,0:T(8,128)(2,1)S(1)}, bf16[2,2,2,2,54,128]{5,4,3,2,1,0:T(8,128)(2,1)S(1)}, u32[]{:S(2)}, u32[]{:S(2)}) %collective-permute-start.10) | collective-permute-done | bytes 221216 | tf_op jit(solution)/shard_map/ppermute | solution.py:21
  126.1 6.3 %all-to-all-start.1 = ((bf16[16,54,128]{2,1,0:T(8,128)(2,1)}), bf16[16,54,128]{2,1,0:T(8,128)(2,1)S(1)}, u32[]{:S(2)}, u32[]{:S(2)}) async-start(bf16[16,54,128]{2,1,0:T(8,128)(2,1)} %bitcast.19), calls=%async_computation.1 | async-start | bytes 458752 | tf_op jit(solution)/shard_map/all_to_all | solution.py:55
  132.4 3.6 %fusion.9 = bf16[1,2,4,8,8,128]{5,1,4,3,2,0:T(2,128)(2,1)S(1)} fusion(bf16[3,3,3,128,128]{4,3,2,1,0:T(8,128)(2,1)} %copy-done, pred[]{:T(512)S(6)} %eq.33, bf16[2,4,8,8,128]{4,0,3,2,1:T(2,128)(2,1)} %copy-done.8, pred[]{:T(512)S(6)} %eq.37, bf16[2,4,8,8,128]{4,0,3,2,1:T(2,128)(2,1)} %copy-done.7, pred[]{:T(512)S(6)} %eq.38, ...), kind=kOutput, calls=%fused_computation.19 | convolution fusion | flops 318242816 | bytes 2457608 | tf_op jit(solution)/shard_map/conv_general_dilated | solution.py:69
  136.7 12.5 %all-to-all-done.1 = bf16[16,54,128]{2,1,0:T(8,128)(2,1)S(1)} async-done(((bf16[16,54,128]{2,1,0:T(8,128)(2,1)}), bf16[16,54,128]{2,1,0:T(8,128)(2,1)S(1)}, u32[]{:S(2)}, u32[]{:S(2)}) %all-to-all-start.1) | async-done | bytes 221216 | tf_op jit(solution)/shard_map/all_to_all | solution.py:55
  (60 shorter events, 13.0 us)
Async XLA Ops:
  2.1 32.1 %all-to-all-start = ((bf16[16,54,128]{2,1,0:T(8,128)(2,1)}), bf16[16,54,128]{2,1,0:T(8,128)(2,1)S(1)}, u32[]{:S(2)}, u32[]{:S(2)}) async-start(bf16[16,54,128]{2,1,0:T(8,128)(2,1)} %broadcast_in_dim.11), calls=%async_computation | async-start | bytes 458752 | tf_op jit(solution)/shard_map/all_to_all | solution.py:31
  34.2 8.7 %collective-permute-start = (bf16[16,54,128]{2,1,0:T(8,128)(2,1)S(1)}, bf16[16,54,128]{2,1,0:T(8,128)(2,1)S(1)}, u32[]{:S(2)}, u32[]{:S(2)}) collective-permute-start(bf16[16,54,128]{2,1,0:T(8,128)(2,1)S(1)} %all-to-all-done), channel_id=1, source_target_pairs={{0,32},{1,33},{2,34},{3,35},{4,36},{5,37},{6,38},{7,39},{8,40},{9,... | collective-permute-start | bytes 663560 | tf_op jit(solution)/shard_map/ppermute | solution.py:21
  43.0 3.7 %collective-permute-start.1 = (bf16[2,16,54,128]{3,2,1,0:T(8,128)(2,1)S(1)}, bf16[2,16,54,128]{3,2,1,0:T(8,128)(2,1)S(1)}, u32[]{:S(2)}, u32[]{:S(2)}) collective-permute-start(bf16[2,16,54,128]{3,2,1,0:T(8,128)(2,1)S(1)} %pad_maximum_fusion), channel_id=1, source_target_pairs={{0,1},{1,0},{2,3},{3,2},{4,5},{5,4},{6,7},{7,6},{8,9},{9,8},{10,11... | collective-permute-start | bytes 1327112 | tf_op jit(solution)/shard_map/ppermute | solution.py:21
  46.8 0.9 copy-start.1
  47.2 17.3 %copy-start = (bf16[3,3,3,128,128]{4,3,2,1,0:T(8,128)(2,1)}, bf16[3,3,3,128,128]{4,3,2,1,0:T(8,128)(2,1)S(1)}, u32[]{:S(2)}) copy-start(bf16[3,3,3,128,128]{4,3,2,1,0:T(8,128)(2,1)S(1)} %reshape_reshape.6) | copy-start | bytes 2654212
  47.7 1.8 %copy-start.2 = (bf16[2,4,8,8,128]{4,3,2,1,0:T(8,128)(2,1)S(1)}, bf16[2,4,8,8,128]{4,3,2,1,0:T(8,128)(2,1)}, u32[]{:S(2)}) copy-start(bf16[2,4,8,8,128]{4,3,2,1,0:T(8,128)(2,1)} %param.9) | copy-start | bytes 393220
  49.5 55.5 %copy-start.10 = (f32[2,4,8,8,128]{4,0,3,2,1:T(2,128)}, f32[2,4,8,8,128]{4,0,3,2,1:T(2,128)S(1)}, u32[]{:S(2)}) copy-start(f32[2,4,8,8,128]{4,0,3,2,1:T(2,128)S(1)} %add_multiply_fusion) | copy-start | bytes 786436
  51.2 0.7 collective-permute-start.2
  53.7 2.5 %copy-start.3 = (bf16[2,4,8,8,128]{4,0,3,2,1:T(2,128)(2,1)}, bf16[2,4,8,8,128]{4,0,3,2,1:T(2,128)(2,1)S(1)}, u32[]{:S(2)}) copy-start(bf16[2,4,8,8,128]{4,0,3,2,1:T(2,128)(2,1)S(1)} %fusion.1) | copy-start | bytes 393220
  53.7 0.7 collective-permute-start.3
  56.2 2.5 %copy-start.4 = (bf16[2,4,8,8,128]{4,0,3,2,1:T(2,128)(2,1)}, bf16[2,4,8,8,128]{4,0,3,2,1:T(2,128)(2,1)S(1)}, u32[]{:S(2)}) copy-start(bf16[2,4,8,8,128]{4,0,3,2,1:T(2,128)(2,1)S(1)} %fusion.2) | copy-start | bytes 393220
  56.2 0.7 collective-permute-start.4
  58.7 2.7 %copy-start.5 = (bf16[2,4,8,8,128]{4,0,3,2,1:T(2,128)(2,1)}, bf16[2,4,8,8,128]{4,0,3,2,1:T(2,128)(2,1)S(1)}, u32[]{:S(2)}) copy-start(bf16[2,4,8,8,128]{4,0,3,2,1:T(2,128)(2,1)S(1)} %fusion.3) | copy-start | bytes 393220
  58.7 0.9 collective-permute-start.5
  61.3 2.5 %copy-start.6 = (bf16[2,4,8,8,128]{4,0,3,2,1:T(2,128)(2,1)}, bf16[2,4,8,8,128]{4,0,3,2,1:T(2,128)(2,1)S(1)}, u32[]{:S(2)}) copy-start(bf16[2,4,8,8,128]{4,0,3,2,1:T(2,128)(2,1)S(1)} %fusion.4) | copy-start | bytes 393220
  61.3 0.7 collective-permute-start.6
  63.8 2.5 %copy-start.7 = (bf16[2,4,8,8,128]{4,0,3,2,1:T(2,128)(2,1)}, bf16[2,4,8,8,128]{4,0,3,2,1:T(2,128)(2,1)S(1)}, u32[]{:S(2)}) copy-start(bf16[2,4,8,8,128]{4,0,3,2,1:T(2,128)(2,1)S(1)} %fusion.5) | copy-start | bytes 393220
  63.8 0.7 collective-permute-start.7
  66.3 38.7 %copy-start.8 = (bf16[2,4,8,8,128]{4,0,3,2,1:T(2,128)(2,1)}, bf16[2,4,8,8,128]{4,0,3,2,1:T(2,128)(2,1)S(1)}, u32[]{:S(2)}) copy-start(bf16[2,4,8,8,128]{4,0,3,2,1:T(2,128)(2,1)S(1)} %fusion.6) | copy-start | bytes 393220
  66.3 38.7 %collective-permute-start.8 = (bf16[2,4,8,8,128]{4,0,3,2,1:T(2,128)(2,1)S(1)}, bf16[2,4,8,8,128]{4,0,3,2,1:T(2,128)(2,1)S(1)}, u32[]{:S(2)}, u32[]{:S(2)}) collective-permute-start(bf16[2,4,8,8,128]{4,0,3,2,1:T(2,128)(2,1)S(1)} %fusion.6), channel_id=1, source_target_pairs={{64,0},{65,1},{66,2},{67,3},{68,4},{69,5},{70,6},{71,7},{72,8},{73... | collective-permute-start | bytes 393224 | tf_op jit(solution)/shard_map/ppermute | solution.py:125
  105.0 0.7 copy-start.9
  112.0 3.7 %collective-permute-start.9 = (bf16[2,2,2,2,2,54,128]{6,5,4,3,2,1,0:T(8,128)(2,1)S(1)}, bf16[2,2,2,2,2,54,128]{6,5,4,3,2,1,0:T(8,128)(2,1)S(1)}, u32[]{:S(2)}, u32[]{:S(2)}) collective-permute-start(bf16[2,2,2,2,2,54,128]{6,5,4,3,2,1,0:T(8,128)(2,1)S(1)} %fusion.10), channel_id=1, source_target_pairs={{0,1},{1,0},{2,3},{3,2},{4,5},{5,4},{6,7},{7,6},{8,9},{9,8},{10,11... | collective-permute-start | bytes 1327112 | tf_op jit(solution)/shard_map/ppermute | solution.py:21
  115.8 9.5 %collective-permute-start.10 = (bf16[2,2,2,2,54,128]{5,4,3,2,1,0:T(8,128)(2,1)S(1)}, bf16[2,2,2,2,54,128]{5,4,3,2,1,0:T(8,128)(2,1)S(1)}, u32[]{:S(2)}, u32[]{:S(2)}) collective-permute-start(bf16[2,2,2,2,54,128]{5,4,3,2,1,0:T(8,128)(2,1)S(1)} %fusion.20), channel_id=1, source_target_pairs={{0,32},{1,33},{2,34},{3,35},{4,36},{5,37},{6,38},{7,39},{8,40},{9,... | collective-permute-start | bytes 663560 | tf_op jit(solution)/shard_map/ppermute | solution.py:21
  126.1 23.1 %all-to-all-start.1 = ((bf16[16,54,128]{2,1,0:T(8,128)(2,1)}), bf16[16,54,128]{2,1,0:T(8,128)(2,1)S(1)}, u32[]{:S(2)}, u32[]{:S(2)}) async-start(bf16[16,54,128]{2,1,0:T(8,128)(2,1)} %bitcast.19), calls=%async_computation.1 | async-start | bytes 458752 | tf_op jit(solution)/shard_map/all_to_all | solution.py:55

commit v8 on v7

--- a/solution.py
+++ b/solution.py
@@ -92,37 +92,73 @@
     )
 
 
+def silu_slopes(field, kernel, anchors, pos_gain):
+    size_x, size_y, size_z = field.shape[1:4]
+    pre_act = conv_forward(field, kernel) + position_terms(anchors, pos_gain, size_x, size_y, size_z)
+    sigmoid_h = jax.nn.sigmoid(pre_act)
+    return sigmoid_h * (1.0 + pre_act * (1.0 - sigmoid_h))
+
+
+def section_step(cotangent, silu_slope, kernel):
+    slope = (cotangent * silu_slope).astype(jnp.bfloat16)
+    down_grad = (cotangent + conv_transposed(slope, kernel)).astype(jnp.bfloat16)
+    return slope, down_grad
+
+
+def split_exact(values):
+    high = values.astype(jnp.bfloat16)
+    rest = values - high.astype(jnp.float32)
+    middle = rest.astype(jnp.bfloat16)
+    low = (rest - middle.astype(jnp.float32)).astype(jnp.bfloat16)
+    return [high, middle, low]
+
+
 def local(acts, weights, pos_weight, anchors, top_grad):
     segments = lax.axis_size("segment")
     dp_count = lax.axis_size(DP)
     segment_index = lax.axis_index("segment")
     channels = weights.shape[2]
+    rows = weights.shape[1]
     bits = bit_count(dp_count)
-    gathered = gather_by_halves(weights[0], DP, [bits - 1, 0], "z")
-    kernel = gathered.reshape(3, 3, 3, channels, channels)
     fields = acts[0]
     micro_count, size_x, size_y, size_z = fields.shape[:4]
     cell_count = size_x * size_y * size_z
-    pos_gain = pos_weight[0]
-    position_all = position_terms(anchors, pos_gain, size_x, size_y, size_z)
-    pre_act = conv_forward(fields, kernel) + position_all
-    sigmoid_h = jax.nn.sigmoid(pre_act)
-    silu_slope = sigmoid_h * (1.0 + pre_act * (1.0 - sigmoid_h))
+    gain_rows = pos_weight.shape[1]
 
-    is_top = segment_index == segments - 1
-    incoming = jnp.zeros(top_grad.shape, jnp.bfloat16)
+    packed = jnp.concatenate(
+        [weights[0], fields.reshape(-1, channels)] + split_exact(pos_weight[0]), axis=0
+    )
+    upper = lax.ppermute(packed, "segment", [(i + 1, i) for i in range(segments - 1)])
+    weights_up = upper[:rows]
+    fields_up = upper[rows : rows + micro_count * cell_count].reshape(fields.shape)
+    gain_parts = upper[rows + micro_count * cell_count :].astype(jnp.float32)
+    gain_up = (
+        gain_parts[:gain_rows] + gain_parts[gain_rows : 2 * gain_rows]
+    ) + gain_parts[2 * gain_rows :]
+
+    both = jnp.concatenate([weights[0], weights_up], axis=1)
+    gathered = gather_by_halves(both, DP, [bits - 1, 0], "z")
+    kernel = gathered[:, :channels].reshape(3, 3, 3, channels, channels)
+    kernel_up = gathered[:, channels:].reshape(3, 3, 3, channels, channels)
+    silu_own = silu_slopes(fields, kernel, anchors, pos_weight[0])
+    silu_up = silu_slopes(fields_up, kernel_up, anchors, gain_up)
+
+    received = jnp.zeros(top_grad.shape, jnp.bfloat16)
     grads_held = jnp.zeros(top_grad.shape, jnp.bfloat16)
     slope_held = jnp.zeros(top_grad.shape, jnp.bfloat16)
-    for tick in range(segments):
-        cotangent = jnp.where(is_top, top_grad, incoming).astype(jnp.float32)
-        slope = (cotangent * silu_slope).astype(jnp.bfloat16)
-        down_grad = (cotangent + conv_transposed(slope, kernel)).astype(jnp.bfloat16)
-        mine = segment_index == segments - 1 - tick
+    stages = (segments + 1) // 2
+    for stage in range(stages):
+        high = segments - 1 - 2 * stage
+        cotangent = jnp.where(segment_index == segments - 2, top_grad, received)
+        _, above = section_step(cotangent.astype(jnp.float32), silu_up, kernel_up)
+        cotangent = jnp.where(segment_index == segments - 1, top_grad, above)
+        slope, down_grad = section_step(cotangent.astype(jnp.float32), silu_own, kernel)
+        mine = (segment_index == high) | (segment_index == high - 1)
         grads_held = jnp.where(mine, down_grad, grads_held)
         slope_held = jnp.where(mine, slope, slope_held)
-        if tick + 1 < segments:
-            sender = segments - 1 - tick
-            incoming = lax.ppermute(down_grad, "segment", [(sender, sender - 1)])
+        pairs = [(source, source - 2) for source in (high, high - 1) if source - 2 >= 0]
+        if pairs:
+            received = lax.ppermute(down_grad, "segment", pairs)
 
     scale_factor = 1.0 / math.sqrt(dp_count * micro_count * cell_count)
     grad_term = conv_kernel_grad(fields, slope_held) * scale_factor

time: 150 us -> 160 us (1.067)
  local copies, waits for them, and re-layouts: 7.56 us -> 10.8 us
  starting transfers between devices: 36.9 us -> 40 us
  other arithmetic: 1.44 us -> 3.28 us
    ppermute x7 -> x4, waiting for transfers between devices: 37.4 us -> 27.1 us  [the longest x3 20.9 us: local(): received = lax.ppermute(down_grad, 'segment', pairs)]
    all_to_all x1, waiting for transfers between devices: 15 us -> 24.5 us  [gather_by_halves(): lax.all_to_all(jnp.broadcast_to(block, (ring,) + block.shape), ring_axis,...]
    all_to_all x1, starting transfers between devices: 6.31 us -> 10.1 us  [reduce_by_halves(): received = lax.all_to_all(held, ring_axis, 0, 0, tiled=True)]
    conv_general_dilated x1 -> x2, matrix products: 1.76 us -> 3.67 us  [conv_forward(): lax.conv_general_dilated(field, kernel, (1, 1, 1), [(1, 1)] * 3, dimensio...]
    concatenate x0 -> x1, local copies, waits for them, and re-layouts: none -> 1.85 us  [local(): jnp.concatenate([weights[0], fields.reshape(-1, channels)] + split_exact(...]
    ppermute x7 -> x4, starting transfers between devices: 5.49 us -> 4.09 us  [the longest x3 2.81 us: local(): received = lax.ppermute(down_grad, 'segment', pairs)]
  transfers between devices with their start and end apart: 13 -> 10, of which waited for: 7 -> 8; matrix products, arithmetic and copies ran while one was open for 4% -> 3% of each run, Pallas kernels for 0% -> 0%
where the time goes in v8:
time: 160 us
  waiting for transfers between devices  81.6 us (51%)
  starting transfers between devices  40 us (25%)
  matrix products  22.9 us (14%)
  local copies, waits for them, and re-layouts  10.8 us (7%)
  other arithmetic  3.28 us (2%)
    all_to_all x1, waiting for transfers between devices, gather_by_halves(): lax.all_to_all(jnp.broadcast_to(block, (ring,) + block.shape), ring_axis,...  24.5 us
    ppermute x3, waiting for transfers between devices, local(): received = lax.ppermute(down_grad, 'segment', pairs)  20.9 us
    ppermute x4, waiting for transfers between devices, exchanged(): return lax.ppermute(array, axis, [(i, i ^ mask) for i in range(length)])  17 us
    conv_general_dilated x8, matrix products, conv_transposed(): lax.conv_general_dilated(slope, flipped, (1, 1, 1), [(1, 1)] * 3, dimensi...  15.5 us
    all_to_all x1, starting transfers between devices, gather_by_halves(): lax.all_to_all(jnp.broadcast_to(block, (ring,) + block.shape), ring_axis,...  15.2 us
    all_to_all x1, waiting for transfers between devices, reduce_by_halves(): received = lax.all_to_all(held, ring_axis, 0, 0, tiled=True)  12.9 us
    ppermute x4, starting transfers between devices, exchanged(): return lax.ppermute(array, axis, [(i, i ^ mask) for i in range(length)])  10.6 us
    all_to_all x1, starting transfers between devices, reduce_by_halves(): received = lax.all_to_all(held, ring_axis, 0, 0, tiled=True)  10.1 us
  transfers between devices with their start and end apart: 10, of which 8 were waited for; matrix products, arithmetic and copies ran while one was open for 3% of the time, Pallas kernels for 0%

profile of v8, /device:TPU:32, one launch (start us, length us, event | category | flops | bytes accessed | tf_op | source)
XLA Modules:
  0.0 159.7 jit_solution(15593797602615095295)
XLA Ops:
  2.1 1.8 %concatenate.6 = bf16[575,128]{1,0:T(8,128)(2,1)S(1)} concatenate(bf16[54,128]{1,0:T(8,128)(2,1)} %bitcast.87, bf16[512,128]{1,0:T(8,128)(2,1)} %bitcast.83, bf16[3,128]{1,0:T(4,128)(2,1)S(1)} %bitcast.89, bf16[3,128]{1,0:T(4,128)(2,1)S(1)} %get-tuple-element.31, bf16[3,128]{1,0:T(4,128)(2,1)S(1)} %get-tuple-element.30), dimensions={0} | concatenate | bytes 294400 | tf_op jit(solution)/shard_map/concatenate | solution.py:128
  5.2 6.2 %collective-permute-done = bf16[575,128]{1,0:T(8,128)(2,1)S(1)} collective-permute-done((bf16[575,128]{1,0:T(8,128)(2,1)S(1)}, bf16[575,128]{1,0:T(8,128)(2,1)S(1)}, u32[]{:S(2)}, u32[]{:S(2)}) %collective-permute-start) | collective-permute-done | bytes 147232 | tf_op jit(solution)/shard_map/ppermute | solution.py:131
  12.9 15.2 %all-to-all-start = ((bf16[16,54,256]{2,1,0:T(8,128)(2,1)}), bf16[16,54,256]{2,1,0:T(8,128)(2,1)S(1)}, u32[]{:S(2)}, u32[]{:S(2)}) async-start(bf16[16,54,256]{2,1,0:T(8,128)(2,1)} %broadcast_in_dim.6), calls=%async_computation | async-start | bytes 917504 | tf_op jit(solution)/shard_map/all_to_all | solution.py:31
  28.7 24.5 %all-to-all-done = bf16[16,54,256]{2,1,0:T(8,128)(2,1)S(1)} async-done(((bf16[16,54,256]{2,1,0:T(8,128)(2,1)}), bf16[16,54,256]{2,1,0:T(8,128)(2,1)S(1)}, u32[]{:S(2)}, u32[]{:S(2)}) %all-to-all-start) | async-done | bytes 442400 | tf_op jit(solution)/shard_map/all_to_all | solution.py:31
  53.2 3.5 %collective-permute-start.1 = (bf16[16,54,256]{2,1,0:T(8,128)(2,1)S(1)}, bf16[16,54,256]{2,1,0:T(8,128)(2,1)S(1)}, u32[]{:S(2)}, u32[]{:S(2)}) collective-permute-start(bf16[16,54,256]{2,1,0:T(8,128)(2,1)S(1)} %all-to-all-done), channel_id=1, source_target_pairs={{0,32},{1,33},{2,34},{3,35},{4,36},{5,37},{6,38},{7,39},{8,40},{9,... | collective-permute-start | bytes 1327112 | tf_op jit(solution)/shard_map/ppermute | solution.py:21
  56.7 6.9 %collective-permute-done.1 = bf16[16,54,256]{2,1,0:T(8,128)(2,1)S(1)} collective-permute-done((bf16[16,54,256]{2,1,0:T(8,128)(2,1)S(1)}, bf16[16,54,256]{2,1,0:T(8,128)(2,1)S(1)}, u32[]{:S(2)}, u32[]{:S(2)}) %collective-permute-start.1) | collective-permute-done | bytes 442400 | tf_op jit(solution)/shard_map/ppermute | solution.py:21
  63.9 1.9 %collective-permute-start.2 = (bf16[2,16,54,256]{3,1,2,0:T(8,128)(2,1)S(1)}, bf16[2,16,54,256]{3,1,2,0:T(8,128)(2,1)S(1)}, u32[]{:S(2)}, u32[]{:S(2)}) collective-permute-start(bf16[2,16,54,256]{3,1,2,0:T(8,128)(2,1)S(1)} %copy.58), channel_id=1, source_target_pairs={{0,1},{1,0},{2,3},{3,2},{4,5},{5,4},{6,7},{7,6},{8,9},{9,8},{10,11... | collective-permute-start | bytes 2654216 | tf_op jit(solution)/shard_map/ppermute | solution.py:21
  66.1 2.2 %collective-permute-done.2 = bf16[2,16,54,256]{3,1,2,0:T(8,128)(2,1)S(1)} collective-permute-done((bf16[2,16,54,256]{3,1,2,0:T(8,128)(2,1)S(1)}, bf16[2,16,54,256]{3,1,2,0:T(8,128)(2,1)S(1)}, u32[]{:S(2)}, u32[]{:S(2)}) %collective-permute-start.2) | collective-permute-done | bytes 884768 | tf_op jit(solution)/shard_map/ppermute | solution.py:21
  72.0 1.8 %add_multiply_fusion.1 = f32[2,4,8,8,128]{4,0,3,2,1:T(2,128)S(1)} fusion(bf16[3,3,3,128,128]{4,3,2,1,0:T(8,128)(2,1)S(1)} %bitcast.78, bf16[2,4,8,8,128]{4,3,2,1,0:T(8,128)(2,1)S(1)} %bitcast.86, f32[2,8,128]{2,0,1:T(2,128)S(1)} %get-tuple-element.19, f32[2,4,8,128]{3,0,2,1:T(2,128)S(1)} %broadcast_add_fusion.1), kind=kOutput, calls=%fused_computation.55 | convolution fusion | flops 317784064 | bytes 1318912 | tf_op jit(solution)/shard_map/conv_general_dilated | solution.py:60
  73.9 1.8 %fusion.17 = f32[2,4,8,8,128]{4,0,3,2,1:T(2,128)S(1)} fusion(bf16[3,3,3,128,128]{4,3,2,1,0:T(8,128)(2,1)S(1)} %bitcast.79, pred[]{:T(512)S(6)} %eq.43, f32[2,4,8,8,128]{4,0,3,2,1:T(2,128)S(1)} %add_multiply_fusion.1, pred[]{:T(512)S(6)} %eq.44, bf16[2,4,8,8,128]{4,3,2,1,0:T(8,128)(2,1)S(1)} %copy-done.4), kind=kOutput, calls=%fused_computation.29 | convolution fusion | flops 317849600 | bytes 1540098 | tf_op jit(solution)/shard_map/conv_general_dilated | solution.py:69
  75.7 1.8 %add_multiply_fusion = f32[2,4,8,8,128]{4,0,3,2,1:T(2,128)S(1)} fusion(bf16[3,3,3,128,128]{4,3,2,1,0:T(8,128)(2,1)S(1)} %bitcast.73, f32[2,8,128]{2,0,1:T(2,128)S(1)} %get-tuple-element.18, f32[2,4,8,128]{3,0,2,1:T(2,128)S(1)} %broadcast_add_fusion, bf16[2,4,8,8,128]{4,3,2,1,0:T(8,128)(2,1)S(1)} %bitcast.84), kind=kOutput, calls=%fused_computation.54 | convolution fusion | flops 317784064 | bytes 1318912 | tf_op jit(solution)/shard_map/conv_general_dilated | solution.py:60
  77.5 1.7 %fusion.1 = bf16[2,4,8,8,128]{4,0,3,2,1:T(2,128)(2,1)S(1)} fusion(f32[2,4,8,8,128]{4,0,3,2,1:T(2,128)S(1)} %fusion.17, bf16[3,3,3,128,128]{4,3,2,1,0:T(8,128)(2,1)S(1)} %bitcast.74, f32[2,4,8,8,128]{4,0,3,2,1:T(2,128)S(1)} %add_multiply_fusion), kind=kOutput, calls=%fused_computation.13 | convolution fusion | flops 317456384 | bytes 1540096 | tf_op jit(solution)/shard_map/conv_general_dilated | solution.py:69
  80.0 1.8 %fusion.15 = f32[2,4,8,8,128]{4,0,3,2,1:T(2,128)S(1)} fusion(bf16[3,3,3,128,128]{4,3,2,1,0:T(8,128)(2,1)S(1)} %bitcast.80, pred[]{:T(512)S(6)} %eq.43, f32[2,4,8,8,128]{4,0,3,2,1:T(2,128)S(1)} %add_multiply_fusion.1, bf16[2,4,8,8,128]{4,0,3,2,1:T(2,128)(2,1)S(1)} %collective-permute-done.3, pred[]{:T(512)S(6)} %eq.44, ...), kind=kOutput, calls=%fused_computation.27 | convolution fusion | flops 317849600 | bytes 1671170 | tf_op jit(solution)/shard_map/conv_general_dilated | solution.py:69
  84.2 1.8 %fusion.13 = f32[2,4,8,8,128]{4,0,3,2,1:T(2,128)S(1)} fusion(bf16[3,3,3,128,128]{4,3,2,1,0:T(8,128)(2,1)S(1)} %bitcast.81, pred[]{:T(512)S(6)} %eq.43, f32[2,4,8,8,128]{4,0,3,2,1:T(2,128)S(1)} %add_multiply_fusion.1, bf16[2,4,8,8,128]{4,0,3,2,1:T(2,128)(2,1)S(1)} %collective-permute-done.4, pred[]{:T(512)S(6)} %eq.44, ...), kind=kOutput, calls=%fused_computation.25 | convolution fusion | flops 317849600 | bytes 1671170 | tf_op jit(solution)/shard_map/conv_general_dilated | solution.py:69
  89.1 20.9 %collective-permute-done.5 = bf16[2,4,8,8,128]{4,0,3,2,1:T(2,128)(2,1)S(1)} collective-permute-done((bf16[2,4,8,8,128]{4,0,3,2,1:T(2,128)(2,1)S(1)}, bf16[2,4,8,8,128]{4,0,3,2,1:T(2,128)(2,1)S(1)}, u32[]{:S(2)}, u32[]{:S(2)}) %collective-permute-start.5) | collective-permute-done | bytes 131104 | tf_op jit(solution)/shard_map/ppermute | solution.py:161
  110.0 1.9 %fusion.11 = f32[2,4,8,8,128]{4,0,3,2,1:T(2,128)S(1)} fusion(bf16[3,3,3,128,128]{4,3,2,1,0:T(8,128)(2,1)S(1)} %bitcast.82, pred[]{:T(512)S(6)} %eq.43, f32[2,4,8,8,128]{4,0,3,2,1:T(2,128)S(1)} %add_multiply_fusion.1, bf16[2,4,8,8,128]{4,0,3,2,1:T(2,128)(2,1)S(1)} %collective-permute-done.5, pred[]{:T(512)S(6)} %eq.44, ...), kind=kOutput, calls=%fused_computation.23 | convolution fusion | flops 317849600 | bytes 1671170 | tf_op jit(solution)/shard_map/conv_general_dilated | solution.py:69
  112.7 3.8 %convolution_multiply_fusion = f32[3,3,3,128,128]{4,3,2,1,0:T(8,128)} fusion(pred[]{:T(512)S(6)} %or.12, pred[]{:T(512)S(6)} %or.13, pred[]{:T(512)S(6)} %or.14, pred[]{:T(512)S(6)} %or.15, bf16[2,4,8,8,128]{4,3,2,1,0:T(8,128)(2,1)S(1)} %bitcast.85, f32[2,4,8,8,128]{4,0,3,2,1:T(2,128)S(1)} %fusion.17, f32[2,4,8,8,128]{4,0,3,2,1:T(2,128)S(1)} %add_multiply_fusion, ...), kind=kOutput, calls=%fused_computation.1 | convolution fusion | flops 318423040 | bytes 3211268 | tf_op jit(solution)/shard_map/conv_general_dilated | solution.py:77
  118.0 1.9 %collective-permute-start.6 = (bf16[2,2,2,2,2,54,128]{6,5,4,3,2,1,0:T(8,128)(2,1)S(1)}, bf16[2,2,2,2,2,54,128]{6,5,4,3,2,1,0:T(8,128)(2,1)S(1)}, u32[]{:S(2)}, u32[]{:S(2)}) collective-permute-start(bf16[2,2,2,2,2,54,128]{6,5,4,3,2,1,0:T(8,128)(2,1)S(1)} %fusion.18), channel_id=1, source_target_pairs={{0,1},{1,0},{2,3},{3,2},{4,5},{5,4},{6,7},{7,6},{8,9},{9,8},{10,11... | collective-permute-start | bytes 1327112 | tf_op jit(solution)/shard_map/ppermute | solution.py:21
  119.9 1.8 %collective-permute-done.6 = bf16[2,2,2,2,2,54,128]{6,5,4,3,2,1,0:T(8,128)(2,1)S(1)} collective-permute-done((bf16[2,2,2,2,2,54,128]{6,5,4,3,2,1,0:T(8,128)(2,1)S(1)}, bf16[2,2,2,2,2,54,128]{6,5,4,3,2,1,0:T(8,128)(2,1)S(1)}, u32[]{:S(2)}, u32[]{:S(2)}) %collective-permute-start.6) | collective-permute-done | bytes 442400 | tf_op jit(solution)/shard_map/ppermute | solution.py:21
  121.9 3.3 %collective-permute-start.7 = (bf16[2,2,2,2,54,128]{5,4,3,2,1,0:T(8,128)(2,1)S(1)}, bf16[2,2,2,2,54,128]{5,4,3,2,1,0:T(8,128)(2,1)S(1)}, u32[]{:S(2)}, u32[]{:S(2)}) collective-permute-start(bf16[2,2,2,2,54,128]{5,4,3,2,1,0:T(8,128)(2,1)S(1)} %fusion.24), channel_id=1, source_target_pairs={{0,32},{1,33},{2,34},{3,35},{4,36},{5,37},{6,38},{7,39},{8,40},{9,... | collective-permute-start | bytes 663560 | tf_op jit(solution)/shard_map/ppermute | solution.py:21
  125.2 6.2 %collective-permute-done.7 = bf16[2,2,2,2,54,128]{5,4,3,2,1,0:T(8,128)(2,1)S(1)} collective-permute-done((bf16[2,2,2,2,54,128]{5,4,3,2,1,0:T(8,128)(2,1)S(1)}, bf16[2,2,2,2,54,128]{5,4,3,2,1,0:T(8,128)(2,1)S(1)}, u32[]{:S(2)}, u32[]{:S(2)}) %collective-permute-start.7) | collective-permute-done | bytes 221216 | tf_op jit(solution)/shard_map/ppermute | solution.py:21
  132.2 10.1 %all-to-all-start.1 = ((bf16[16,54,128]{2,1,0:T(8,128)(2,1)}), bf16[16,54,128]{2,1,0:T(8,128)(2,1)S(1)}, u32[]{:S(2)}, u32[]{:S(2)}) async-start(bf16[16,54,128]{2,1,0:T(8,128)(2,1)} %bitcast.25), calls=%async_computation.1 | async-start | bytes 458752 | tf_op jit(solution)/shard_map/all_to_all | solution.py:55
  142.2 3.2 %fusion.9 = bf16[1,2,4,8,8,128]{5,1,4,3,2,0:T(2,128)(2,1)S(1)} fusion(f32[2,4,8,8,128]{4,0,3,2,1:T(2,128)} %copy-done.7, bf16[3,3,3,128,128]{4,3,2,1,0:T(8,128)(2,1)} %bitcast.77, pred[]{:T(512)S(6)} %or.12, bf16[2,4,8,8,128]{4,0,3,2,1:T(2,128)(2,1)} %copy-done.5, pred[]{:T(512)S(6)} %or.13, bf16[2,4,8,8,128]{4,0,3,2,1:T(2,128)(2,1)S(1)} %fusion.3, ...), kind=kOutput, calls=%fused_computation.21 | convolution fusion | flops 317718528 | bytes 1933316 | tf_op jit(solution)/shard_map/conv_general_dilated | solution.py:69
  146.1 12.9 %all-to-all-done.1 = bf16[16,54,128]{2,1,0:T(8,128)(2,1)S(1)} async-done(((bf16[16,54,128]{2,1,0:T(8,128)(2,1)}), bf16[16,54,128]{2,1,0:T(8,128)(2,1)S(1)}, u32[]{:S(2)}, u32[]{:S(2)}) %all-to-all-start.1) | async-done | bytes 221216 | tf_op jit(solution)/shard_map/all_to_all | solution.py:55
  (62 shorter events, 19.7 us)
Async XLA Ops:
  0.6 28.0 %copy-start.2 = (f32[1,3,128]{2,0,1:T(1,128)S(1)}, f32[1,3,128]{2,0,1:T(1,128)}, u32[]{:S(2)}) copy-start(f32[1,3,128]{2,0,1:T(1,128)} %param.7) | copy-start | bytes 4612
  0.6 27.5 %copy-start.3 = (s32[2,3]{1,0:T(2,128)S(1)}, s32[2,3]{1,0:T(2,128)}, u32[]{:S(2)}) copy-start(s32[2,3]{1,0:T(2,128)} %param.8) | copy-start | bytes 76
  3.9 7.5 %collective-permute-start = (bf16[575,128]{1,0:T(8,128)(2,1)S(1)}, bf16[575,128]{1,0:T(8,128)(2,1)S(1)}, u32[]{:S(2)}, u32[]{:S(2)}) collective-permute-start(bf16[575,128]{1,0:T(8,128)(2,1)S(1)} %concatenate.6), channel_id=1, source_target_pairs={{64,0},{128,64},{192,128},{256,192},{320,256},{384,320},{448,384},... | collective-permute-start | bytes 441608 | tf_op jit(solution)/shard_map/ppermute | solution.py:131
  12.9 40.3 %all-to-all-start = ((bf16[16,54,256]{2,1,0:T(8,128)(2,1)}), bf16[16,54,256]{2,1,0:T(8,128)(2,1)S(1)}, u32[]{:S(2)}, u32[]{:S(2)}) async-start(bf16[16,54,256]{2,1,0:T(8,128)(2,1)} %broadcast_in_dim.6), calls=%async_computation | async-start | bytes 917504 | tf_op jit(solution)/shard_map/all_to_all | solution.py:31
  53.2 10.4 %collective-permute-start.1 = (bf16[16,54,256]{2,1,0:T(8,128)(2,1)S(1)}, bf16[16,54,256]{2,1,0:T(8,128)(2,1)S(1)}, u32[]{:S(2)}, u32[]{:S(2)}) collective-permute-start(bf16[16,54,256]{2,1,0:T(8,128)(2,1)S(1)} %all-to-all-done), channel_id=1, source_target_pairs={{0,32},{1,33},{2,34},{3,35},{4,36},{5,37},{6,38},{7,39},{8,40},{9,... | collective-permute-start | bytes 1327112 | tf_op jit(solution)/shard_map/ppermute | solution.py:21
  63.9 4.3 %collective-permute-start.2 = (bf16[2,16,54,256]{3,1,2,0:T(8,128)(2,1)S(1)}, bf16[2,16,54,256]{3,1,2,0:T(8,128)(2,1)S(1)}, u32[]{:S(2)}, u32[]{:S(2)}) collective-permute-start(bf16[2,16,54,256]{3,1,2,0:T(8,128)(2,1)S(1)} %copy.58), channel_id=1, source_target_pairs={{0,1},{1,0},{2,3},{3,2},{4,5},{5,4},{6,7},{7,6},{8,9},{9,8},{10,11... | collective-permute-start | bytes 2654216 | tf_op jit(solution)/shard_map/ppermute | solution.py:21
  72.0 14.1 %copy-start = (bf16[3456,128]{1,0:T(8,128)(2,1)}, bf16[3456,128]{1,0:T(8,128)(2,1)S(1)}, u32[]{:S(2)}) copy-start(bf16[3456,128]{1,0:T(8,128)(2,1)S(1)} %get-tuple-element.12) | copy-start | bytes 2654212
  72.0 1.9 %copy-start.4 = (bf16[2,4,8,8,128]{4,3,2,1,0:T(8,128)(2,1)S(1)}, bf16[2,4,8,8,128]{4,3,2,1,0:T(8,128)(2,1)}, u32[]{:S(2)}) copy-start(bf16[2,4,8,8,128]{4,3,2,1,0:T(8,128)(2,1)} %param.9) | copy-start | bytes 393220
  73.9 1.8 %copy-start.1 = (bf16[1,2,4,8,8,128]{5,4,3,2,1,0:T(8,128)(2,1)S(1)}, bf16[1,2,4,8,8,128]{5,4,3,2,1,0:T(8,128)(2,1)}, u32[]{:S(2)}) copy-start(bf16[1,2,4,8,8,128]{5,4,3,2,1,0:T(8,128)(2,1)} %param.5) | copy-start | bytes 393220
  77.5 34.4 %copy-start.6 = (f32[2,4,8,8,128]{4,0,3,2,1:T(2,128)}, f32[2,4,8,8,128]{4,0,3,2,1:T(2,128)S(1)}, u32[]{:S(2)}) copy-start(f32[2,4,8,8,128]{4,0,3,2,1:T(2,128)S(1)} %add_multiply_fusion) | copy-start | bytes 786436
  79.2 0.9 collective-permute-start.3
  83.6 0.7 collective-permute-start.4
  87.8 24.1 %copy-start.5 = (bf16[2,4,8,8,128]{4,0,3,2,1:T(2,128)(2,1)}, bf16[2,4,8,8,128]{4,0,3,2,1:T(2,128)(2,1)S(1)}, u32[]{:S(2)}) copy-start(bf16[2,4,8,8,128]{4,0,3,2,1:T(2,128)(2,1)S(1)} %fusion.5) | copy-start | bytes 393220
  87.8 22.2 %collective-permute-start.5 = (bf16[2,4,8,8,128]{4,0,3,2,1:T(2,128)(2,1)S(1)}, bf16[2,4,8,8,128]{4,0,3,2,1:T(2,128)(2,1)S(1)}, u32[]{:S(2)}, u32[]{:S(2)}) collective-permute-start(bf16[2,4,8,8,128]{4,0,3,2,1:T(2,128)(2,1)S(1)} %fusion.5), channel_id=1, source_target_pairs={{192,64},{128,0},{193,65},{129,1},{194,66},{130,2},{195,67},{131,3... | collective-permute-start | bytes 393224 | tf_op jit(solution)/shard_map/ppermute | solution.py:161
  111.9 0.7 copy-start.7
  118.0 3.7 %collective-permute-start.6 = (bf16[2,2,2,2,2,54,128]{6,5,4,3,2,1,0:T(8,128)(2,1)S(1)}, bf16[2,2,2,2,2,54,128]{6,5,4,3,2,1,0:T(8,128)(2,1)S(1)}, u32[]{:S(2)}, u32[]{:S(2)}) collective-permute-start(bf16[2,2,2,2,2,54,128]{6,5,4,3,2,1,0:T(8,128)(2,1)S(1)} %fusion.18), channel_id=1, source_target_pairs={{0,1},{1,0},{2,3},{3,2},{4,5},{5,4},{6,7},{7,6},{8,9},{9,8},{10,11... | collective-permute-start | bytes 1327112 | tf_op jit(solution)/shard_map/ppermute | solution.py:21
  121.9 9.5 %collective-permute-start.7 = (bf16[2,2,2,2,54,128]{5,4,3,2,1,0:T(8,128)(2,1)S(1)}, bf16[2,2,2,2,54,128]{5,4,3,2,1,0:T(8,128)(2,1)S(1)}, u32[]{:S(2)}, u32[]{:S(2)}) collective-permute-start(bf16[2,2,2,2,54,128]{5,4,3,2,1,0:T(8,128)(2,1)S(1)} %fusion.24), channel_id=1, source_target_pairs={{0,32},{1,33},{2,34},{3,35},{4,36},{5,37},{6,38},{7,39},{8,40},{9,... | collective-permute-start | bytes 663560 | tf_op jit(solution)/shard_map/ppermute | solution.py:21
  132.2 26.8 %all-to-all-start.1 = ((bf16[16,54,128]{2,1,0:T(8,128)(2,1)}), bf16[16,54,128]{2,1,0:T(8,128)(2,1)S(1)}, u32[]{:S(2)}, u32[]{:S(2)}) async-start(bf16[16,54,128]{2,1,0:T(8,128)(2,1)} %bitcast.25), calls=%async_computation.1 | async-start | bytes 458752 | tf_op jit(solution)/shard_map/all_to_all | solution.py:55

commit v9 on v7

--- a/solution.py
+++ b/solution.py
@@ -39,19 +39,21 @@
     return held.reshape((-1,) + block.shape[1:])
 
 
-def reduce_by_halves(chunks, axis, order, ring_axis):
+def reduce_by_halves(chunks, axis, ring_axis):
     index = lax.axis_index(axis)
-    done = bit_count(chunks.shape[0])
-    rest = [bit for bit in range(done - 1, -1, -1) if bit not in order]
-    held = chunks.reshape((2,) * done + chunks.shape[1:])
-    held = jnp.transpose(held, [done - 1 - bit for bit in order + rest] + list(range(done, held.ndim)))
-    for bit in order:
-        mine = (index >> bit) & 1
-        kept = lax.dynamic_index_in_dim(held, mine, 0, keepdims=False)
-        sent = lax.dynamic_index_in_dim(held, 1 - mine, 0, keepdims=False)
-        received = exchanged(sent.astype(jnp.bfloat16), axis, 1 << bit)
-        held = kept + received.astype(jnp.float32)
-    held = held.reshape((-1,) + chunks.shape[1:]).astype(jnp.bfloat16)
+    ring = lax.axis_size(ring_axis)
+    held = chunks.reshape((2, ring, 2) + chunks.shape[1:])
+    mine = index & 1
+    kept = lax.dynamic_index_in_dim(held, mine, 2, keepdims=False)
+    sent = lax.dynamic_index_in_dim(held, 1 - mine, 2, keepdims=False)
+    received = exchanged(sent.astype(jnp.bfloat16), axis, 1)
+    held = kept + received.astype(jnp.float32)
+    top = bit_count(lax.axis_size(axis)) - 1
+    mine = (index >> top) & 1
+    kept = lax.dynamic_index_in_dim(held, mine, 0, keepdims=False)
+    sent = lax.dynamic_index_in_dim(held, 1 - mine, 0, keepdims=False)
+    received = exchanged(sent.astype(jnp.bfloat16), axis, 1 << top)
+    held = (kept + received.astype(jnp.float32)).astype(jnp.bfloat16)
     received = lax.all_to_all(held, ring_axis, 0, 0, tiled=True)
     return jnp.sum(received.astype(jnp.float32), axis=0, keepdims=True)
 
@@ -127,7 +129,7 @@
     scale_factor = 1.0 / math.sqrt(dp_count * micro_count * cell_count)
     grad_term = conv_kernel_grad(fields, slope_held) * scale_factor
     grad_term = grad_term.reshape(dp_count, -1, channels)
-    reduced = reduce_by_halves(grad_term, DP, [0, bits - 1], "z")
+    reduced = reduce_by_halves(grad_term, DP, "z")
     return (grads_held[None], reduced)
 
 

time: 150 us -> 150 us (level)
  no operation moved by 1% of the time
where the time goes in v9:
time: 150 us
  waiting for transfers between devices  80.5 us (54%)
  starting transfers between devices  36.9 us (25%)
  matrix products  22.4 us (15%)
  local copies, waits for them, and re-layouts  7.56 us (5%)
    ppermute x7, waiting for transfers between devices, local(): incoming = lax.ppermute(down_grad, 'segment', [(sender, sender - 1)])  37.4 us
    conv_general_dilated x8, matrix products, conv_transposed(): lax.conv_general_dilated(slope, flipped, (1, 1, 1), [(1, 1)] * 3, dimensi...  15.9 us
    ppermute x4, waiting for transfers between devices, exchanged(): return lax.ppermute(array, axis, [(i, i ^ mask) for i in range(length)])  15.6 us
    all_to_all x1, starting transfers between devices, gather_by_halves(): lax.all_to_all(jnp.broadcast_to(block, (ring,) + block.shape), ring_axis,...  15.2 us
    all_to_all x1, waiting for transfers between devices, gather_by_halves(): lax.all_to_all(jnp.broadcast_to(block, (ring,) + block.shape), ring_axis,...  15 us
    all_to_all x1, waiting for transfers between devices, reduce_by_halves(): received = lax.all_to_all(held, ring_axis, 0, 0, tiled=True)  12.5 us
    ppermute x4, starting transfers between devices, exchanged(): return lax.ppermute(array, axis, [(i, i ^ mask) for i in range(length)])  9.9 us
    all_to_all x1, starting transfers between devices, reduce_by_halves(): received = lax.all_to_all(held, ring_axis, 0, 0, tiled=True)  6.31 us
  transfers between devices with their start and end apart: 13, of which 7 were waited for; matrix products, arithmetic and copies ran while one was open for 4% of the time, Pallas kernels for 0%

profile of v9, /device:TPU:32, one launch (start us, length us, event | category | flops | bytes accessed | tf_op | source)
XLA Modules:
  0.0 149.9 jit_solution(11476848654809974335)
XLA Ops:
  2.1 15.2 %all-to-all-start = ((bf16[16,54,128]{2,1,0:T(8,128)(2,1)}), bf16[16,54,128]{2,1,0:T(8,128)(2,1)S(1)}, u32[]{:S(2)}, u32[]{:S(2)}) async-start(bf16[16,54,128]{2,1,0:T(8,128)(2,1)} %broadcast_in_dim.11), calls=%async_computation | async-start | bytes 458752 | tf_op jit(solution)/shard_map/all_to_all | solution.py:31
  19.2 15.0 %all-to-all-done = bf16[16,54,128]{2,1,0:T(8,128)(2,1)S(1)} async-done(((bf16[16,54,128]{2,1,0:T(8,128)(2,1)}), bf16[16,54,128]{2,1,0:T(8,128)(2,1)S(1)}, u32[]{:S(2)}, u32[]{:S(2)}) %all-to-all-start) | async-done | bytes 221216 | tf_op jit(solution)/shard_map/all_to_all | solution.py:31
  34.2 3.5 %collective-permute-start = (bf16[16,54,128]{2,1,0:T(8,128)(2,1)S(1)}, bf16[16,54,128]{2,1,0:T(8,128)(2,1)S(1)}, u32[]{:S(2)}, u32[]{:S(2)}) collective-permute-start(bf16[16,54,128]{2,1,0:T(8,128)(2,1)S(1)} %all-to-all-done), channel_id=1, source_target_pairs={{0,32},{1,33},{2,34},{3,35},{4,36},{5,37},{6,38},{7,39},{8,40},{9,... | collective-permute-start | bytes 663560 | tf_op jit(solution)/shard_map/ppermute | solution.py:21
  37.8 5.2 %collective-permute-done = bf16[16,54,128]{2,1,0:T(8,128)(2,1)S(1)} collective-permute-done((bf16[16,54,128]{2,1,0:T(8,128)(2,1)S(1)}, bf16[16,54,128]{2,1,0:T(8,128)(2,1)S(1)}, u32[]{:S(2)}, u32[]{:S(2)}) %collective-permute-start) | collective-permute-done | bytes 221216 | tf_op jit(solution)/shard_map/ppermute | solution.py:21
  43.0 1.9 %collective-permute-start.1 = (bf16[2,16,54,128]{3,2,1,0:T(8,128)(2,1)S(1)}, bf16[2,16,54,128]{3,2,1,0:T(8,128)(2,1)S(1)}, u32[]{:S(2)}, u32[]{:S(2)}) collective-permute-start(bf16[2,16,54,128]{3,2,1,0:T(8,128)(2,1)S(1)} %pad_maximum_fusion), channel_id=1, source_target_pairs={{0,1},{1,0},{2,3},{3,2},{4,5},{5,4},{6,7},{7,6},{8,9},{9,8},{10,11... | collective-permute-start | bytes 1327112 | tf_op jit(solution)/shard_map/ppermute | solution.py:21
  45.1 1.7 %collective-permute-done.1 = bf16[2,16,54,128]{3,2,1,0:T(8,128)(2,1)S(1)} collective-permute-done((bf16[2,16,54,128]{3,2,1,0:T(8,128)(2,1)S(1)}, bf16[2,16,54,128]{3,2,1,0:T(8,128)(2,1)S(1)}, u32[]{:S(2)}, u32[]{:S(2)}) %collective-permute-start.1) | collective-permute-done | bytes 442400 | tf_op jit(solution)/shard_map/ppermute | solution.py:21
  47.7 1.8 %add_multiply_fusion = f32[2,4,8,8,128]{4,0,3,2,1:T(2,128)S(1)} fusion(bf16[3,3,3,128,128]{4,3,2,1,0:T(8,128)(2,1)S(1)} %reshape_reshape.6, f32[2,8,128]{2,0,1:T(2,128)S(1)} %get-tuple-element.15, f32[2,4,8,128]{3,0,2,1:T(2,128)S(1)} %broadcast_add_fusion, bf16[2,4,8,8,128]{4,3,2,1,0:T(8,128)(2,1)S(1)} %bitcast.50), kind=kOutput, calls=%fused_computation.47 | convolution fusion | flops 317784064 | bytes 1318912 | tf_op jit(solution)/shard_map/conv_general_dilated | solution.py:62
  49.5 1.7 %fusion = bf16[2,4,8,8,128]{4,0,3,2,1:T(2,128)(2,1)S(1)} fusion(bf16[3,3,3,128,128]{4,3,2,1,0:T(8,128)(2,1)S(1)} %reshape_reshape.6, pred[]{:T(512)S(6)} %eq.34, f32[2,4,8,8,128]{4,0,3,2,1:T(2,128)S(1)} %add_multiply_fusion, bf16[2,4,8,8,128]{4,3,2,1,0:T(8,128)(2,1)S(1)} %copy-done.2), kind=kOutput, calls=%fused_computation.10 | convolution fusion | flops 317718528 | bytes 1409025 | tf_op jit(solution)/shard_map/conv_general_dilated | solution.py:71
  51.9 1.8 %fusion.1 = bf16[2,4,8,8,128]{4,0,3,2,1:T(2,128)(2,1)S(1)} fusion(bf16[3,3,3,128,128]{4,3,2,1,0:T(8,128)(2,1)S(1)} %reshape_reshape.6, f32[2,4,8,8,128]{4,0,3,2,1:T(2,128)S(1)} %add_multiply_fusion, bf16[2,4,8,8,128]{4,0,3,2,1:T(2,128)(2,1)S(1)} %collective-permute-done.2, pred[]{:T(512)S(6)} %eq.34, bf16[2,4,8,8,128]{4,3,2,1,0:T(8,128)(2,1)S(1)} %copy-done.2), kind=kOutput, calls=%fused_computation.11 | convolution fusion | flops 317718528 | bytes 1540097 | tf_op jit(solution)/shard_map/conv_general_dilated | solution.py:71
  54.4 1.8 %fusion.2 = bf16[2,4,8,8,128]{4,0,3,2,1:T(2,128)(2,1)S(1)} fusion(bf16[3,3,3,128,128]{4,3,2,1,0:T(8,128)(2,1)S(1)} %reshape_reshape.6, f32[2,4,8,8,128]{4,0,3,2,1:T(2,128)S(1)} %add_multiply_fusion, bf16[2,4,8,8,128]{4,0,3,2,1:T(2,128)(2,1)S(1)} %collective-permute-done.3, pred[]{:T(512)S(6)} %eq.34, bf16[2,4,8,8,128]{4,3,2,1,0:T(8,128)(2,1)S(1)} %copy-done.2), kind=kOutput, calls=%fused_computation.12 | convolution fusion | flops 317718528 | bytes 1540097 | tf_op jit(solution)/shard_map/conv_general_dilated | solution.py:71
  56.9 1.8 %fusion.3 = bf16[2,4,8,8,128]{4,0,3,2,1:T(2,128)(2,1)S(1)} fusion(bf16[3,3,3,128,128]{4,3,2,1,0:T(8,128)(2,1)S(1)} %reshape_reshape.6, f32[2,4,8,8,128]{4,0,3,2,1:T(2,128)S(1)} %add_multiply_fusion, bf16[2,4,8,8,128]{4,0,3,2,1:T(2,128)(2,1)S(1)} %collective-permute-done.4, pred[]{:T(512)S(6)} %eq.34, bf16[2,4,8,8,128]{4,3,2,1,0:T(8,128)(2,1)S(1)} %copy-done.2), kind=kOutput, calls=%fused_computation.13 | convolution fusion | flops 317718528 | bytes 1540097 | tf_op jit(solution)/shard_map/conv_general_dilated | solution.py:71
  59.5 1.8 %fusion.4 = bf16[2,4,8,8,128]{4,0,3,2,1:T(2,128)(2,1)S(1)} fusion(bf16[3,3,3,128,128]{4,3,2,1,0:T(8,128)(2,1)S(1)} %reshape_reshape.6, f32[2,4,8,8,128]{4,0,3,2,1:T(2,128)S(1)} %add_multiply_fusion, bf16[2,4,8,8,128]{4,0,3,2,1:T(2,128)(2,1)S(1)} %collective-permute-done.5, pred[]{:T(512)S(6)} %eq.34, bf16[2,4,8,8,128]{4,3,2,1,0:T(8,128)(2,1)S(1)} %copy-done.2), kind=kOutput, calls=%fused_computation.14 | convolution fusion | flops 317718528 | bytes 1540097 | tf_op jit(solution)/shard_map/conv_general_dilated | solution.py:71
  62.0 1.8 %fusion.5 = bf16[2,4,8,8,128]{4,0,3,2,1:T(2,128)(2,1)S(1)} fusion(bf16[3,3,3,128,128]{4,3,2,1,0:T(8,128)(2,1)S(1)} %reshape_reshape.6, f32[2,4,8,8,128]{4,0,3,2,1:T(2,128)S(1)} %add_multiply_fusion, bf16[2,4,8,8,128]{4,0,3,2,1:T(2,128)(2,1)S(1)} %collective-permute-done.6, pred[]{:T(512)S(6)} %eq.34, bf16[2,4,8,8,128]{4,3,2,1,0:T(8,128)(2,1)S(1)} %copy-done.2), kind=kOutput, calls=%fused_computation.15 | convolution fusion | flops 317718528 | bytes 1540097 | tf_op jit(solution)/shard_map/conv_general_dilated | solution.py:71
  64.5 1.8 %fusion.6 = bf16[2,4,8,8,128]{4,0,3,2,1:T(2,128)(2,1)S(1)} fusion(bf16[3,3,3,128,128]{4,3,2,1,0:T(8,128)(2,1)S(1)} %reshape_reshape.6, f32[2,4,8,8,128]{4,0,3,2,1:T(2,128)S(1)} %add_multiply_fusion, bf16[2,4,8,8,128]{4,0,3,2,1:T(2,128)(2,1)S(1)} %collective-permute-done.7, pred[]{:T(512)S(6)} %eq.34, bf16[2,4,8,8,128]{4,3,2,1,0:T(8,128)(2,1)S(1)} %copy-done.2), kind=kOutput, calls=%fused_computation.16 | convolution fusion | flops 317718528 | bytes 1540097 | tf_op jit(solution)/shard_map/conv_general_dilated | solution.py:71
  67.6 37.4 %collective-permute-done.8 = bf16[2,4,8,8,128]{4,0,3,2,1:T(2,128)(2,1)S(1)} collective-permute-done((bf16[2,4,8,8,128]{4,0,3,2,1:T(2,128)(2,1)S(1)}, bf16[2,4,8,8,128]{4,0,3,2,1:T(2,128)(2,1)S(1)}, u32[]{:S(2)}, u32[]{:S(2)}) %collective-permute-start.8) | collective-permute-done | bytes 131104 | tf_op jit(solution)/shard_map/ppermute | solution.py:127
  105.7 4.7 %convolution_multiply_fusion = f32[3,3,3,128,128]{4,3,2,1,0:T(8,128)} fusion(pred[]{:T(512)S(6)} %eq.33, pred[]{:T(512)S(6)} %eq.37, pred[]{:T(512)S(6)} %eq.38, pred[]{:T(512)S(6)} %eq.39, pred[]{:T(512)S(6)} %eq.40, pred[]{:T(512)S(6)} %eq.41, pred[]{:T(512)S(6)} %eq.42, pred[]{:T(512)S(6)} %eq.34, bf16[2,4,8,8,128]{4,3,2,1,0:T(8,128)(2,1)S(1)} %bitcast.51, ...), kind=kOutput, calls=%fused_computation | convolution fusion | flops 320258048 | bytes 3211272 | tf_op jit(solution)/shard_map/conv_general_dilated | solution.py:79
  110.4 1.5 reshape_reshape.7
  112.0 1.9 %collective-permute-start.9 = (bf16[2,16,54,128]{3,2,1,0:T(8,128)(2,1)S(1)}, bf16[2,16,54,128]{3,2,1,0:T(8,128)(2,1)S(1)}, u32[]{:S(2)}, u32[]{:S(2)}) collective-permute-start(bf16[2,16,54,128]{3,2,1,0:T(8,128)(2,1)S(1)} %fusion.10), channel_id=1, source_target_pairs={{0,1},{1,0},{2,3},{3,2},{4,5},{5,4},{6,7},{7,6},{8,9},{9,8},{10,11... | collective-permute-start | bytes 1327112 | tf_op jit(solution)/shard_map/ppermute | solution.py:21
  113.9 1.8 %collective-permute-done.9 = bf16[2,16,54,128]{3,2,1,0:T(8,128)(2,1)S(1)} collective-permute-done((bf16[2,16,54,128]{3,2,1,0:T(8,128)(2,1)S(1)}, bf16[2,16,54,128]{3,2,1,0:T(8,128)(2,1)S(1)}, u32[]{:S(2)}, u32[]{:S(2)}) %collective-permute-start.9) | collective-permute-done | bytes 442400 | tf_op jit(solution)/shard_map/ppermute | solution.py:21
  115.8 2.6 %collective-permute-start.10 = (bf16[16,54,128]{2,1,0:T(8,128)(2,1)S(1)}, bf16[16,54,128]{2,1,0:T(8,128)(2,1)S(1)}, u32[]{:S(2)}, u32[]{:S(2)}) collective-permute-start(bf16[16,54,128]{2,1,0:T(8,128)(2,1)S(1)} %fusion.20), channel_id=1, source_target_pairs={{0,32},{1,33},{2,34},{3,35},{4,36},{5,37},{6,38},{7,39},{8,40},{9,... | collective-permute-start | bytes 663560 | tf_op jit(solution)/shard_map/ppermute | solution.py:21
  118.4 7.0 %collective-permute-done.10 = bf16[16,54,128]{2,1,0:T(8,128)(2,1)S(1)} collective-permute-done((bf16[16,54,128]{2,1,0:T(8,128)(2,1)S(1)}, bf16[16,54,128]{2,1,0:T(8,128)(2,1)S(1)}, u32[]{:S(2)}, u32[]{:S(2)}) %collective-permute-start.10) | collective-permute-done | bytes 221216 | tf_op jit(solution)/shard_map/ppermute | solution.py:21
  126.1 6.3 %all-to-all-start.1 = ((bf16[16,54,128]{2,1,0:T(8,128)(2,1)}), bf16[16,54,128]{2,1,0:T(8,128)(2,1)S(1)}, u32[]{:S(2)}, u32[]{:S(2)}) async-start(bf16[16,54,128]{2,1,0:T(8,128)(2,1)} %fusion.11), calls=%async_computation.1 | async-start | bytes 458752 | tf_op jit(solution)/shard_map/all_to_all | solution.py:57
  132.4 3.6 %fusion.9 = bf16[1,2,4,8,8,128]{5,1,4,3,2,0:T(2,128)(2,1)S(1)} fusion(bf16[3,3,3,128,128]{4,3,2,1,0:T(8,128)(2,1)} %copy-done, pred[]{:T(512)S(6)} %eq.33, bf16[2,4,8,8,128]{4,0,3,2,1:T(2,128)(2,1)} %copy-done.8, pred[]{:T(512)S(6)} %eq.37, bf16[2,4,8,8,128]{4,0,3,2,1:T(2,128)(2,1)} %copy-done.7, pred[]{:T(512)S(6)} %eq.38, ...), kind=kOutput, calls=%fused_computation.19 | convolution fusion | flops 318242816 | bytes 2457608 | tf_op jit(solution)/shard_map/conv_general_dilated | solution.py:71
  136.7 12.5 %all-to-all-done.1 = bf16[16,54,128]{2,1,0:T(8,128)(2,1)S(1)} async-done(((bf16[16,54,128]{2,1,0:T(8,128)(2,1)}), bf16[16,54,128]{2,1,0:T(8,128)(2,1)S(1)}, u32[]{:S(2)}, u32[]{:S(2)}) %all-to-all-start.1) | async-done | bytes 221216 | tf_op jit(solution)/shard_map/all_to_all | solution.py:57
  (60 shorter events, 13.0 us)
Async XLA Ops:
  2.1 32.1 %all-to-all-start = ((bf16[16,54,128]{2,1,0:T(8,128)(2,1)}), bf16[16,54,128]{2,1,0:T(8,128)(2,1)S(1)}, u32[]{:S(2)}, u32[]{:S(2)}) async-start(bf16[16,54,128]{2,1,0:T(8,128)(2,1)} %broadcast_in_dim.11), calls=%async_computation | async-start | bytes 458752 | tf_op jit(solution)/shard_map/all_to_all | solution.py:31
  34.2 8.7 %collective-permute-start = (bf16[16,54,128]{2,1,0:T(8,128)(2,1)S(1)}, bf16[16,54,128]{2,1,0:T(8,128)(2,1)S(1)}, u32[]{:S(2)}, u32[]{:S(2)}) collective-permute-start(bf16[16,54,128]{2,1,0:T(8,128)(2,1)S(1)} %all-to-all-done), channel_id=1, source_target_pairs={{0,32},{1,33},{2,34},{3,35},{4,36},{5,37},{6,38},{7,39},{8,40},{9,... | collective-permute-start | bytes 663560 | tf_op jit(solution)/shard_map/ppermute | solution.py:21
  43.0 3.7 %collective-permute-start.1 = (bf16[2,16,54,128]{3,2,1,0:T(8,128)(2,1)S(1)}, bf16[2,16,54,128]{3,2,1,0:T(8,128)(2,1)S(1)}, u32[]{:S(2)}, u32[]{:S(2)}) collective-permute-start(bf16[2,16,54,128]{3,2,1,0:T(8,128)(2,1)S(1)} %pad_maximum_fusion), channel_id=1, source_target_pairs={{0,1},{1,0},{2,3},{3,2},{4,5},{5,4},{6,7},{7,6},{8,9},{9,8},{10,11... | collective-permute-start | bytes 1327112 | tf_op jit(solution)/shard_map/ppermute | solution.py:21
  46.8 0.9 copy-start.1
  47.2 17.3 %copy-start = (bf16[3,3,3,128,128]{4,3,2,1,0:T(8,128)(2,1)}, bf16[3,3,3,128,128]{4,3,2,1,0:T(8,128)(2,1)S(1)}, u32[]{:S(2)}) copy-start(bf16[3,3,3,128,128]{4,3,2,1,0:T(8,128)(2,1)S(1)} %reshape_reshape.6) | copy-start | bytes 2654212
  47.7 1.8 %copy-start.2 = (bf16[2,4,8,8,128]{4,3,2,1,0:T(8,128)(2,1)S(1)}, bf16[2,4,8,8,128]{4,3,2,1,0:T(8,128)(2,1)}, u32[]{:S(2)}) copy-start(bf16[2,4,8,8,128]{4,3,2,1,0:T(8,128)(2,1)} %param.9) | copy-start | bytes 393220
  49.5 55.5 %copy-start.10 = (f32[2,4,8,8,128]{4,0,3,2,1:T(2,128)}, f32[2,4,8,8,128]{4,0,3,2,1:T(2,128)S(1)}, u32[]{:S(2)}) copy-start(f32[2,4,8,8,128]{4,0,3,2,1:T(2,128)S(1)} %add_multiply_fusion) | copy-start | bytes 786436
  51.2 0.7 collective-permute-start.2
  53.7 2.5 %copy-start.3 = (bf16[2,4,8,8,128]{4,0,3,2,1:T(2,128)(2,1)}, bf16[2,4,8,8,128]{4,0,3,2,1:T(2,128)(2,1)S(1)}, u32[]{:S(2)}) copy-start(bf16[2,4,8,8,128]{4,0,3,2,1:T(2,128)(2,1)S(1)} %fusion.1) | copy-start | bytes 393220
  53.7 0.7 collective-permute-start.3
  56.2 2.5 %copy-start.4 = (bf16[2,4,8,8,128]{4,0,3,2,1:T(2,128)(2,1)}, bf16[2,4,8,8,128]{4,0,3,2,1:T(2,128)(2,1)S(1)}, u32[]{:S(2)}) copy-start(bf16[2,4,8,8,128]{4,0,3,2,1:T(2,128)(2,1)S(1)} %fusion.2) | copy-start | bytes 393220
  56.2 0.7 collective-permute-start.4
  58.7 2.7 %copy-start.5 = (bf16[2,4,8,8,128]{4,0,3,2,1:T(2,128)(2,1)}, bf16[2,4,8,8,128]{4,0,3,2,1:T(2,128)(2,1)S(1)}, u32[]{:S(2)}) copy-start(bf16[2,4,8,8,128]{4,0,3,2,1:T(2,128)(2,1)S(1)} %fusion.3) | copy-start | bytes 393220
  58.7 0.9 collective-permute-start.5
  61.3 2.5 %copy-start.6 = (bf16[2,4,8,8,128]{4,0,3,2,1:T(2,128)(2,1)}, bf16[2,4,8,8,128]{4,0,3,2,1:T(2,128)(2,1)S(1)}, u32[]{:S(2)}) copy-start(bf16[2,4,8,8,128]{4,0,3,2,1:T(2,128)(2,1)S(1)} %fusion.4) | copy-start | bytes 393220
  61.3 0.7 collective-permute-start.6
  63.8 2.5 %copy-start.7 = (bf16[2,4,8,8,128]{4,0,3,2,1:T(2,128)(2,1)}, bf16[2,4,8,8,128]{4,0,3,2,1:T(2,128)(2,1)S(1)}, u32[]{:S(2)}) copy-start(bf16[2,4,8,8,128]{4,0,3,2,1:T(2,128)(2,1)S(1)} %fusion.5) | copy-start | bytes 393220
  63.8 0.7 collective-permute-start.7
  66.3 38.7 %copy-start.8 = (bf16[2,4,8,8,128]{4,0,3,2,1:T(2,128)(2,1)}, bf16[2,4,8,8,128]{4,0,3,2,1:T(2,128)(2,1)S(1)}, u32[]{:S(2)}) copy-start(bf16[2,4,8,8,128]{4,0,3,2,1:T(2,128)(2,1)S(1)} %fusion.6) | copy-start | bytes 393220
  66.3 38.7 %collective-permute-start.8 = (bf16[2,4,8,8,128]{4,0,3,2,1:T(2,128)(2,1)S(1)}, bf16[2,4,8,8,128]{4,0,3,2,1:T(2,128)(2,1)S(1)}, u32[]{:S(2)}, u32[]{:S(2)}) collective-permute-start(bf16[2,4,8,8,128]{4,0,3,2,1:T(2,128)(2,1)S(1)} %fusion.6), channel_id=1, source_target_pairs={{64,0},{65,1},{66,2},{67,3},{68,4},{69,5},{70,6},{71,7},{72,8},{73... | collective-permute-start | bytes 393224 | tf_op jit(solution)/shard_map/ppermute | solution.py:127
  105.0 0.7 copy-start.9
  112.0 3.7 %collective-permute-start.9 = (bf16[2,16,54,128]{3,2,1,0:T(8,128)(2,1)S(1)}, bf16[2,16,54,128]{3,2,1,0:T(8,128)(2,1)S(1)}, u32[]{:S(2)}, u32[]{:S(2)}) collective-permute-start(bf16[2,16,54,128]{3,2,1,0:T(8,128)(2,1)S(1)} %fusion.10), channel_id=1, source_target_pairs={{0,1},{1,0},{2,3},{3,2},{4,5},{5,4},{6,7},{7,6},{8,9},{9,8},{10,11... | collective-permute-start | bytes 1327112 | tf_op jit(solution)/shard_map/ppermute | solution.py:21
  115.8 9.6 %collective-permute-start.10 = (bf16[16,54,128]{2,1,0:T(8,128)(2,1)S(1)}, bf16[16,54,128]{2,1,0:T(8,128)(2,1)S(1)}, u32[]{:S(2)}, u32[]{:S(2)}) collective-permute-start(bf16[16,54,128]{2,1,0:T(8,128)(2,1)S(1)} %fusion.20), channel_id=1, source_target_pairs={{0,32},{1,33},{2,34},{3,35},{4,36},{5,37},{6,38},{7,39},{8,40},{9,... | collective-permute-start | bytes 663560 | tf_op jit(solution)/shard_map/ppermute | solution.py:21
  126.1 23.1 %all-to-all-start.1 = ((bf16[16,54,128]{2,1,0:T(8,128)(2,1)}), bf16[16,54,128]{2,1,0:T(8,128)(2,1)S(1)}, u32[]{:S(2)}, u32[]{:S(2)}) async-start(bf16[16,54,128]{2,1,0:T(8,128)(2,1)} %fusion.11), calls=%async_computation.1 | async-start | bytes 458752 | tf_op jit(solution)/shard_map/all_to_all | solution.py:57

commit v10 on v7

--- a/solution.py
+++ b/solution.py
@@ -110,6 +110,16 @@
     silu_slope = sigmoid_h * (1.0 + pre_act * (1.0 - sigmoid_h))
 
     is_top = segment_index == segments - 1
+    pair_axes = ("segment", "y")
+    crossed = segments // 2 - 1
+    is_crossed = segment_index == crossed
+    swap_pairs = [(2 * crossed, 2 * crossed + 1), (2 * crossed + 1, 2 * crossed)]
+    partner = lax.ppermute(
+        jnp.stack([fields.astype(jnp.float32), silu_slope]), pair_axes, swap_pairs
+    )
+    silu_slope = jnp.where(is_crossed, partner[1], silu_slope)
+    fields_used = jnp.where(is_crossed, partner[0].astype(jnp.bfloat16), fields)
+
     incoming = jnp.zeros(top_grad.shape, jnp.bfloat16)
     grads_held = jnp.zeros(top_grad.shape, jnp.bfloat16)
     slope_held = jnp.zeros(top_grad.shape, jnp.bfloat16)
@@ -122,10 +132,16 @@
         slope_held = jnp.where(mine, slope, slope_held)
         if tick + 1 < segments:
             sender = segments - 1 - tick
-            incoming = lax.ppermute(down_grad, "segment", [(sender, sender - 1)])
+            if sender in (crossed + 1, crossed):
+                pairs = [(2 * sender + y, 2 * (sender - 1) + 1 - y) for y in range(2)]
+                incoming = lax.ppermute(down_grad, pair_axes, pairs)
+            else:
+                incoming = lax.ppermute(down_grad, "segment", [(sender, sender - 1)])
+    returned = lax.ppermute(grads_held, pair_axes, swap_pairs)
+    grads_held = jnp.where(is_crossed, returned, grads_held)
 
     scale_factor = 1.0 / math.sqrt(dp_count * micro_count * cell_count)
-    grad_term = conv_kernel_grad(fields, slope_held) * scale_factor
+    grad_term = conv_kernel_grad(fields_used, slope_held) * scale_factor
     grad_term = grad_term.reshape(dp_count, -1, channels)
     reduced = reduce_by_halves(grad_term, DP, [0, bits - 1], "z")
     return (grads_held[None], reduced)

time: 150 us -> 151 us (level)
  the two profiles are of different devices: /device:TPU:32 before, /device:TPU:8 now
where the time goes in v10:
time: 151 us; the launch traced here: 150 us
  waiting for transfers between devices  81.7 us (54%)
  starting transfers between devices  37.2 us (25%)
  matrix products  16.2 us (11%)
  local copies, waits for them, and re-layouts  7.03 us (5%)
  other arithmetic  6.87 us (5%)
    ppermute x5, waiting for transfers between devices, local(): incoming = lax.ppermute(down_grad, 'segment', [(sender, sender - 1)])  37.5 us
    ppermute x4, waiting for transfers between devices, exchanged(): return lax.ppermute(array, axis, [(i, i ^ mask) for i in range(length)])  16.2 us
    all_to_all x1, starting transfers between devices, gather_by_halves(): lax.all_to_all(jnp.broadcast_to(block, (ring,) + block.shape), ring_axis,...  15.2 us
    all_to_all x1, waiting for transfers between devices, gather_by_halves(): lax.all_to_all(jnp.broadcast_to(block, (ring,) + block.shape), ring_axis,...  14.8 us
    all_to_all x1, waiting for transfers between devices, reduce_by_halves(): received = lax.all_to_all(held, ring_axis, 0, 0, tiled=True)  13.2 us
    conv_general_dilated x8, matrix products, conv_transposed(): lax.conv_general_dilated(slope, flipped, (1, 1, 1), [(1, 1)] * 3, dimensi...  12.6 us
    ppermute x4, starting transfers between devices, exchanged(): return lax.ppermute(array, axis, [(i, i ^ mask) for i in range(length)])  8.46 us
    all_to_all x1, starting transfers between devices, reduce_by_halves(): received = lax.all_to_all(held, ring_axis, 0, 0, tiled=True)  6.66 us
  transfers between devices with their start and end apart: 15, of which 7 were waited for; matrix products, arithmetic and copies ran while one was open for 4% of the time, Pallas kernels for 0%

profile of v10, /device:TPU:8, one launch (start us, length us, event | category | flops | bytes accessed | tf_op | source)
XLA Modules:
  0.0 150.2 jit_solution(7523999237577428952)
XLA Ops:
  0.6 1.4 broadcast_in_dim.11
  2.1 15.2 %all-to-all-start = ((bf16[16,54,128]{2,1,0:T(8,128)(2,1)}), bf16[16,54,128]{2,1,0:T(8,128)(2,1)S(1)}, u32[]{:S(2)}, u32[]{:S(2)}) async-start(bf16[16,54,128]{2,1,0:T(8,128)(2,1)} %broadcast_in_dim.11), calls=%async_computation | async-start | bytes 458752 | tf_op jit(solution)/shard_map/all_to_all | solution.py:31
  19.9 14.8 %all-to-all-done = bf16[16,54,128]{2,1,0:T(8,128)(2,1)S(1)} async-done(((bf16[16,54,128]{2,1,0:T(8,128)(2,1)}), bf16[16,54,128]{2,1,0:T(8,128)(2,1)S(1)}, u32[]{:S(2)}, u32[]{:S(2)}) %all-to-all-start) | async-done | bytes 221216 | tf_op jit(solution)/shard_map/all_to_all | solution.py:31
  34.7 2.3 %collective-permute-start = (bf16[16,54,128]{2,1,0:T(8,128)(2,1)S(1)}, bf16[16,54,128]{2,1,0:T(8,128)(2,1)S(1)}, u32[]{:S(2)}, u32[]{:S(2)}) collective-permute-start(bf16[16,54,128]{2,1,0:T(8,128)(2,1)S(1)} %all-to-all-done), channel_id=1, source_target_pairs={{0,32},{1,33},{2,34},{3,35},{4,36},{5,37},{6,38},{7,39},{8,40},{9,... | collective-permute-start | bytes 663560 | tf_op jit(solution)/shard_map/ppermute | solution.py:21
  37.0 5.5 %collective-permute-done = bf16[16,54,128]{2,1,0:T(8,128)(2,1)S(1)} collective-permute-done((bf16[16,54,128]{2,1,0:T(8,128)(2,1)S(1)}, bf16[16,54,128]{2,1,0:T(8,128)(2,1)S(1)}, u32[]{:S(2)}, u32[]{:S(2)}) %collective-permute-start) | collective-permute-done | bytes 221216 | tf_op jit(solution)/shard_map/ppermute | solution.py:21
  42.6 1.9 %collective-permute-start.1 = (bf16[2,16,54,128]{3,2,1,0:T(8,128)(2,1)S(1)}, bf16[2,16,54,128]{3,2,1,0:T(8,128)(2,1)S(1)}, u32[]{:S(2)}, u32[]{:S(2)}) collective-permute-start(bf16[2,16,54,128]{3,2,1,0:T(8,128)(2,1)S(1)} %pad_maximum_fusion.1), channel_id=1, source_target_pairs={{0,1},{1,0},{2,3},{3,2},{4,5},{5,4},{6,7},{7,6},{8,9},{9,8},{10,11... | collective-permute-start | bytes 1327112 | tf_op jit(solution)/shard_map/ppermute | solution.py:21
  44.7 1.7 %collective-permute-done.1 = bf16[2,16,54,128]{3,2,1,0:T(8,128)(2,1)S(1)} collective-permute-done((bf16[2,16,54,128]{3,2,1,0:T(8,128)(2,1)S(1)}, bf16[2,16,54,128]{3,2,1,0:T(8,128)(2,1)S(1)}, u32[]{:S(2)}, u32[]{:S(2)}) %collective-permute-start.1) | collective-permute-done | bytes 442400 | tf_op jit(solution)/shard_map/ppermute | solution.py:21
  47.3 1.5 fusion.41
  49.9 1.5 fusion.39
  52.1 1.5 fusion.37
  54.4 1.5 fusion.35
  56.7 1.5 fusion.33
  59.0 1.5 fusion.31
  61.5 1.5 fusion.29
  63.8 1.5 fusion.27
  67.6 37.5 %collective-permute-done.9 = bf16[2,4,8,8,128]{4,3,2,1,0:T(8,128)(2,1)S(1)} collective-permute-done((bf16[2,4,8,8,128]{4,3,2,1,0:T(8,128)(2,1)S(1)}, bf16[2,4,8,8,128]{4,3,2,1,0:T(8,128)(2,1)S(1)}, u32[]{:S(2)}, u32[]{:S(2)}) %collective-permute-start.9) | collective-permute-done | bytes 131104 | tf_op jit(solution)/shard_map/ppermute | solution.py:139
  105.8 2.2 %convolution_multiply_fusion = f32[3,3,3,128,128]{4,3,2,1,0:T(8,128)S(1)} fusion(bf16[2,4,8,8,128]{4,3,2,1,0:T(8,128)(2,1)S(1)} %get-tuple-element.6, bf16[2,4,8,8,128]{4,3,2,1,0:T(8,128)(2,1)S(1)} %fusion.21), kind=kOutput, calls=%fused_computation | convolution fusion | flops 317636608 | bytes 2031616 | tf_op jit(solution)/shard_map/conv_general_dilated | solution.py:77
  110.6 1.9 %collective-permute-start.11 = (bf16[2,2,2,2,2,54,128]{6,5,4,3,2,1,0:T(8,128)(2,1)S(1)}, bf16[2,2,2,2,2,54,128]{6,5,4,3,2,1,0:T(8,128)(2,1)S(1)}, u32[]{:S(2)}, u32[]{:S(2)}) collective-permute-start(bf16[2,2,2,2,2,54,128]{6,5,4,3,2,1,0:T(8,128)(2,1)S(1)} %fusion), channel_id=1, source_target_pairs={{0,1},{1,0},{2,3},{3,2},{4,5},{5,4},{6,7},{7,6},{8,9},{9,8},{10,11... | collective-permute-start | bytes 1327112 | tf_op jit(solution)/shard_map/ppermute | solution.py:21
  112.5 1.8 %collective-permute-done.11 = bf16[2,2,2,2,2,54,128]{6,5,4,3,2,1,0:T(8,128)(2,1)S(1)} collective-permute-done((bf16[2,2,2,2,2,54,128]{6,5,4,3,2,1,0:T(8,128)(2,1)S(1)}, bf16[2,2,2,2,2,54,128]{6,5,4,3,2,1,0:T(8,128)(2,1)S(1)}, u32[]{:S(2)}, u32[]{:S(2)}) %collective-permute-start.11) | collective-permute-done | bytes 442400 | tf_op jit(solution)/shard_map/ppermute | solution.py:21
  115.6 2.3 %collective-permute-start.12 = (bf16[2,2,2,2,54,128]{5,4,3,2,1,0:T(8,128)(2,1)S(1)}, bf16[2,2,2,2,54,128]{5,4,3,2,1,0:T(8,128)(2,1)S(1)}, u32[]{:S(2)}, u32[]{:S(2)}) collective-permute-start(bf16[2,2,2,2,54,128]{5,4,3,2,1,0:T(8,128)(2,1)S(1)} %fusion.19), channel_id=1, source_target_pairs={{0,32},{1,33},{2,34},{3,35},{4,36},{5,37},{6,38},{7,39},{8,40},{9,... | collective-permute-start | bytes 663560 | tf_op jit(solution)/shard_map/ppermute | solution.py:21
  118.0 7.2 %collective-permute-done.12 = bf16[2,2,2,2,54,128]{5,4,3,2,1,0:T(8,128)(2,1)S(1)} collective-permute-done((bf16[2,2,2,2,54,128]{5,4,3,2,1,0:T(8,128)(2,1)S(1)}, bf16[2,2,2,2,54,128]{5,4,3,2,1,0:T(8,128)(2,1)S(1)}, u32[]{:S(2)}, u32[]{:S(2)}) %collective-permute-start.12) | collective-permute-done | bytes 221216 | tf_op jit(solution)/shard_map/ppermute | solution.py:21
  125.9 6.7 %all-to-all-start.1 = ((bf16[16,54,128]{2,1,0:T(8,128)(2,1)}), bf16[16,54,128]{2,1,0:T(8,128)(2,1)S(1)}, u32[]{:S(2)}, u32[]{:S(2)}) async-start(bf16[16,54,128]{2,1,0:T(8,128)(2,1)} %bitcast.22), calls=%async_computation.1 | async-start | bytes 458752 | tf_op jit(solution)/shard_map/all_to_all | solution.py:55
  132.6 2.3 %fusion.25 = f32[2,4,8,8,128]{4,0,3,2,1:T(2,128)S(1)} fusion(bf16[3,3,3,128,128]{4,3,2,1,0:T(8,128)(2,1)S(1)} %reshape_reshape.6, bf16[2,4,8,8,128]{4,3,2,1,0:T(8,128)(2,1)} %get-tuple-element.7), kind=kOutput, calls=%fused_computation.58 | convolution fusion | flops 317194240 | bytes 1277952 | tf_op jit(solution)/shard_map/conv_general_dilated | solution.py:69
  136.4 13.2 %all-to-all-done.1 = bf16[16,54,128]{2,1,0:T(8,128)(2,1)S(1)} async-done(((bf16[16,54,128]{2,1,0:T(8,128)(2,1)}), bf16[16,54,128]{2,1,0:T(8,128)(2,1)S(1)}, u32[]{:S(2)}, u32[]{:S(2)}) %all-to-all-start.1) | async-done | bytes 221216 | tf_op jit(solution)/shard_map/all_to_all | solution.py:55
  (77 shorter events, 19.3 us)
Async XLA Ops:
  2.1 32.6 %all-to-all-start = ((bf16[16,54,128]{2,1,0:T(8,128)(2,1)}), bf16[16,54,128]{2,1,0:T(8,128)(2,1)S(1)}, u32[]{:S(2)}, u32[]{:S(2)}) async-start(bf16[16,54,128]{2,1,0:T(8,128)(2,1)} %broadcast_in_dim.11), calls=%async_computation | async-start | bytes 458752 | tf_op jit(solution)/shard_map/all_to_all | solution.py:31
  34.7 7.9 %collective-permute-start = (bf16[16,54,128]{2,1,0:T(8,128)(2,1)S(1)}, bf16[16,54,128]{2,1,0:T(8,128)(2,1)S(1)}, u32[]{:S(2)}, u32[]{:S(2)}) collective-permute-start(bf16[16,54,128]{2,1,0:T(8,128)(2,1)S(1)} %all-to-all-done), channel_id=1, source_target_pairs={{0,32},{1,33},{2,34},{3,35},{4,36},{5,37},{6,38},{7,39},{8,40},{9,... | collective-permute-start | bytes 663560 | tf_op jit(solution)/shard_map/ppermute | solution.py:21
  42.6 3.7 %collective-permute-start.1 = (bf16[2,16,54,128]{3,2,1,0:T(8,128)(2,1)S(1)}, bf16[2,16,54,128]{3,2,1,0:T(8,128)(2,1)S(1)}, u32[]{:S(2)}, u32[]{:S(2)}) collective-permute-start(bf16[2,16,54,128]{3,2,1,0:T(8,128)(2,1)S(1)} %pad_maximum_fusion.1), channel_id=1, source_target_pairs={{0,1},{1,0},{2,3},{3,2},{4,5},{5,4},{6,7},{7,6},{8,9},{9,8},{10,11... | collective-permute-start | bytes 1327112 | tf_op jit(solution)/shard_map/ppermute | solution.py:21
  46.4 0.9 copy-start.1
  47.3 2.3 %copy-start = (bf16[2,4,8,8,128]{4,3,2,1,0:T(8,128)(2,1)S(1)}, bf16[2,4,8,8,128]{4,3,2,1,0:T(8,128)(2,1)}, u32[]{:S(2)}) copy-start(bf16[2,4,8,8,128]{4,3,2,1,0:T(8,128)(2,1)} %param.9) | copy-start | bytes 393220
  49.0 0.7 collective-permute-start.2
  49.7 1.7 %copy-start.8 = (f32[2,2,4,8,8,128]{5,4,3,2,1,0:T(8,128)}, f32[2,2,4,8,8,128]{5,4,3,2,1,0:T(8,128)S(1)}, u32[]{:S(2)}) copy-start(f32[2,2,4,8,8,128]{5,4,3,2,1,0:T(8,128)S(1)} %collective-permute-done.2) | copy-start | bytes 1572868
  51.4 0.7 collective-permute-start.3
  53.7 0.7 collective-permute-start.4
  56.0 0.7 collective-permute-start.5
  58.2 0.7 collective-permute-start.6
  60.5 0.9 collective-permute-start.7
  63.0 2.3 %copy-start.2 = (bf16[2,4,8,8,128]{4,3,2,1,0:T(8,128)(2,1)}, bf16[2,4,8,8,128]{4,3,2,1,0:T(8,128)(2,1)S(1)}, u32[]{:S(2)}) copy-start(bf16[2,4,8,8,128]{4,3,2,1,0:T(8,128)(2,1)S(1)} %fusion.13) | copy-start | bytes 393220
  63.0 0.7 collective-permute-start.8
  65.3 40.5 %copy-start.4 = (bf16[2,4,8,8,128]{4,3,2,1,0:T(8,128)(2,1)}, bf16[2,4,8,8,128]{4,3,2,1,0:T(8,128)(2,1)S(1)}, u32[]{:S(2)}) copy-start(bf16[2,4,8,8,128]{4,3,2,1,0:T(8,128)(2,1)S(1)} %fusion.15) | copy-start | bytes 393220
  65.3 39.8 %collective-permute-start.9 = (bf16[2,4,8,8,128]{4,3,2,1,0:T(8,128)(2,1)S(1)}, bf16[2,4,8,8,128]{4,3,2,1,0:T(8,128)(2,1)S(1)}, u32[]{:S(2)}, u32[]{:S(2)}) collective-permute-start(bf16[2,4,8,8,128]{4,3,2,1,0:T(8,128)(2,1)S(1)} %fusion.15), channel_id=1, source_target_pairs={{64,0},{65,1},{66,2},{67,3},{68,4},{69,5},{70,6},{71,7},{72,8},{73... | collective-permute-start | bytes 393224 | tf_op jit(solution)/shard_map/ppermute | solution.py:139
  105.1 0.7 copy-start.6
  110.6 3.7 %collective-permute-start.11 = (bf16[2,2,2,2,2,54,128]{6,5,4,3,2,1,0:T(8,128)(2,1)S(1)}, bf16[2,2,2,2,2,54,128]{6,5,4,3,2,1,0:T(8,128)(2,1)S(1)}, u32[]{:S(2)}, u32[]{:S(2)}) collective-permute-start(bf16[2,2,2,2,2,54,128]{6,5,4,3,2,1,0:T(8,128)(2,1)S(1)} %fusion), channel_id=1, source_target_pairs={{0,1},{1,0},{2,3},{3,2},{4,5},{5,4},{6,7},{7,6},{8,9},{9,8},{10,11... | collective-permute-start | bytes 1327112 | tf_op jit(solution)/shard_map/ppermute | solution.py:21
  115.6 9.5 %collective-permute-start.12 = (bf16[2,2,2,2,54,128]{5,4,3,2,1,0:T(8,128)(2,1)S(1)}, bf16[2,2,2,2,54,128]{5,4,3,2,1,0:T(8,128)(2,1)S(1)}, u32[]{:S(2)}, u32[]{:S(2)}) collective-permute-start(bf16[2,2,2,2,54,128]{5,4,3,2,1,0:T(8,128)(2,1)S(1)} %fusion.19), channel_id=1, source_target_pairs={{0,32},{1,33},{2,34},{3,35},{4,36},{5,37},{6,38},{7,39},{8,40},{9,... | collective-permute-start | bytes 663560 | tf_op jit(solution)/shard_map/ppermute | solution.py:21
  117.9 17.0 %copy-start.3 = (bf16[2,4,8,8,128]{4,3,2,1,0:T(8,128)(2,1)S(1)}, bf16[2,4,8,8,128]{4,3,2,1,0:T(8,128)(2,1)}, u32[]{:S(2)}) copy-start(bf16[2,4,8,8,128]{4,3,2,1,0:T(8,128)(2,1)} %copy-done.2) | copy-start | bytes 393220
  117.9 17.0 %copy-start.5 = (bf16[2,4,8,8,128]{4,3,2,1,0:T(8,128)(2,1)S(1)}, bf16[2,4,8,8,128]{4,3,2,1,0:T(8,128)(2,1)}, u32[]{:S(2)}) copy-start(bf16[2,4,8,8,128]{4,3,2,1,0:T(8,128)(2,1)} %copy-done.4) | copy-start | bytes 393220
  117.9 17.0 %copy-start.7 = (bf16[2,4,8,8,128]{4,3,2,1,0:T(8,128)(2,1)S(1)}, bf16[2,4,8,8,128]{4,3,2,1,0:T(8,128)(2,1)}, u32[]{:S(2)}) copy-start(bf16[2,4,8,8,128]{4,3,2,1,0:T(8,128)(2,1)} %copy-done.6) | copy-start | bytes 393220
  125.9 23.6 %all-to-all-start.1 = ((bf16[16,54,128]{2,1,0:T(8,128)(2,1)}), bf16[16,54,128]{2,1,0:T(8,128)(2,1)S(1)}, u32[]{:S(2)}, u32[]{:S(2)}) async-start(bf16[16,54,128]{2,1,0:T(8,128)(2,1)} %bitcast.22), calls=%async_computation.1 | async-start | bytes 458752 | tf_op jit(solution)/shard_map/all_to_all | solution.py:55
  135.0 0.7 collective-permute-start.10

commit v11 on v7

--- a/solution.py
+++ b/solution.py
@@ -52,6 +52,27 @@
         received = exchanged(sent.astype(jnp.bfloat16), axis, 1 << bit)
         held = kept + received.astype(jnp.float32)
     held = held.reshape((-1,) + chunks.shape[1:]).astype(jnp.bfloat16)
+    received = lax.all_to_all(held, ring_axis, 0, 0, tiled=True)
+    return jnp.sum(received.astype(jnp.float32), axis=0, keepdims=True)
+
+
+def reduce_in_blocks(rows_all, axis, ring_axis, chunk_rows):
+    index = lax.axis_index(axis)
+    ring = lax.axis_size(ring_axis)
+    block = 4 * chunk_rows
+    held = rows_all.reshape(2, ring // 2, block, rows_all.shape[-1])
+    pieces = [held[:, :, k * chunk_rows : (k + 1) * chunk_rows] for k in range(4)]
+    upper = (index & 1) == 1
+    kept = jnp.stack([jnp.where(upper, pieces[1], pieces[0]), jnp.where(upper, pieces[3], pieces[2])], 2)
+    sent = jnp.stack([jnp.where(upper, pieces[0], pieces[1]), jnp.where(upper, pieces[2], pieces[3])], 2)
+    received = exchanged(sent.astype(jnp.bfloat16), axis, 1)
+    held = (kept + received.astype(jnp.float32)).reshape(2, ring, chunk_rows, rows_all.shape[-1])
+    top = bit_count(lax.axis_size(axis)) - 1
+    mine = (index >> top) & 1
+    kept = lax.dynamic_index_in_dim(held, mine, 0, keepdims=False)
+    sent = lax.dynamic_index_in_dim(held, 1 - mine, 0, keepdims=False)
+    received = exchanged(sent.astype(jnp.bfloat16), axis, 1 << top)
+    held = (kept + received.astype(jnp.float32)).astype(jnp.bfloat16)
     received = lax.all_to_all(held, ring_axis, 0, 0, tiled=True)
     return jnp.sum(received.astype(jnp.float32), axis=0, keepdims=True)
 
@@ -126,8 +147,8 @@
 
     scale_factor = 1.0 / math.sqrt(dp_count * micro_count * cell_count)
     grad_term = conv_kernel_grad(fields, slope_held) * scale_factor
-    grad_term = grad_term.reshape(dp_count, -1, channels)
-    reduced = reduce_by_halves(grad_term, DP, [0, bits - 1], "z")
+    grad_term = grad_term.reshape(-1, channels)
+    reduced = reduce_in_blocks(grad_term, DP, "z", grad_term.shape[0] // dp_count)
     return (grads_held[None], reduced)
 
 

time: 150 us -> 148 us (0.987)
  matrix products: 22.4 us -> 19.9 us
where the time goes in v11:
time: 148 us; the launch traced here: 147 us
  waiting for transfers between devices  81.3 us (55%)
  starting transfers between devices  36.9 us (25%)
  matrix products  19.9 us (13%)
  local copies, waits for them, and re-layouts  6.65 us (4%)
    ppermute x7, waiting for transfers between devices, local(): incoming = lax.ppermute(down_grad, 'segment', [(sender, sender - 1)])  37.4 us
    all_to_all x1, starting transfers between devices, gather_by_halves(): lax.all_to_all(jnp.broadcast_to(block, (ring,) + block.shape), ring_axis,...  15.2 us
    ppermute x4, waiting for transfers between devices, exchanged(): return lax.ppermute(array, axis, [(i, i ^ mask) for i in range(length)])  15.1 us
    all_to_all x1, waiting for transfers between devices, gather_by_halves(): lax.all_to_all(jnp.broadcast_to(block, (ring,) + block.shape), ring_axis,...  15 us
    conv_general_dilated x8, matrix products, conv_transposed(): lax.conv_general_dilated(slope, flipped, (1, 1, 1), [(1, 1)] * 3, dimensi...  14.6 us
    all_to_all x1, waiting for transfers between devices, reduce_in_blocks(): received = lax.all_to_all(held, ring_axis, 0, 0, tiled=True)  13.8 us
    ppermute x4, starting transfers between devices, exchanged(): return lax.ppermute(array, axis, [(i, i ^ mask) for i in range(length)])  9.9 us
    all_to_all x1, starting transfers between devices, reduce_in_blocks(): received = lax.all_to_all(held, ring_axis, 0, 0, tiled=True)  6.3 us
  transfers between devices with their start and end apart: 13, of which 7 were waited for; matrix products, arithmetic and copies ran while one was open for 4% of the time, Pallas kernels for 0%

profile of v11, /device:TPU:32, one launch (start us, length us, event | category | flops | bytes accessed | tf_op | source)
XLA Modules:
  0.0 147.1 jit_solution(7707468772939328974)
XLA Ops:
  0.6 1.4 broadcast_in_dim.11
  2.1 15.2 %all-to-all-start = ((bf16[16,54,128]{2,1,0:T(8,128)(2,1)}), bf16[16,54,128]{2,1,0:T(8,128)(2,1)S(1)}, u32[]{:S(2)}, u32[]{:S(2)}) async-start(bf16[16,54,128]{2,1,0:T(8,128)(2,1)} %broadcast_in_dim.11), calls=%async_computation | async-start | bytes 458752 | tf_op jit(solution)/shard_map/all_to_all | solution.py:31
  19.2 15.0 %all-to-all-done = bf16[16,54,128]{2,1,0:T(8,128)(2,1)S(1)} async-done(((bf16[16,54,128]{2,1,0:T(8,128)(2,1)}), bf16[16,54,128]{2,1,0:T(8,128)(2,1)S(1)}, u32[]{:S(2)}, u32[]{:S(2)}) %all-to-all-start) | async-done | bytes 221216 | tf_op jit(solution)/shard_map/all_to_all | solution.py:31
  34.2 3.5 %collective-permute-start = (bf16[16,54,128]{2,1,0:T(8,128)(2,1)S(1)}, bf16[16,54,128]{2,1,0:T(8,128)(2,1)S(1)}, u32[]{:S(2)}, u32[]{:S(2)}) collective-permute-start(bf16[16,54,128]{2,1,0:T(8,128)(2,1)S(1)} %all-to-all-done), channel_id=1, source_target_pairs={{0,32},{1,33},{2,34},{3,35},{4,36},{5,37},{6,38},{7,39},{8,40},{9,... | collective-permute-start | bytes 663560 | tf_op jit(solution)/shard_map/ppermute | solution.py:21
  37.8 5.2 %collective-permute-done = bf16[16,54,128]{2,1,0:T(8,128)(2,1)S(1)} collective-permute-done((bf16[16,54,128]{2,1,0:T(8,128)(2,1)S(1)}, bf16[16,54,128]{2,1,0:T(8,128)(2,1)S(1)}, u32[]{:S(2)}, u32[]{:S(2)}) %collective-permute-start) | collective-permute-done | bytes 221216 | tf_op jit(solution)/shard_map/ppermute | solution.py:21
  43.0 1.9 %collective-permute-start.1 = (bf16[2,16,54,128]{3,2,1,0:T(8,128)(2,1)S(1)}, bf16[2,16,54,128]{3,2,1,0:T(8,128)(2,1)S(1)}, u32[]{:S(2)}, u32[]{:S(2)}) collective-permute-start(bf16[2,16,54,128]{3,2,1,0:T(8,128)(2,1)S(1)} %pad_maximum_fusion), channel_id=1, source_target_pairs={{0,1},{1,0},{2,3},{3,2},{4,5},{5,4},{6,7},{7,6},{8,9},{9,8},{10,11... | collective-permute-start | bytes 1327112 | tf_op jit(solution)/shard_map/ppermute | solution.py:21
  45.0 1.7 %collective-permute-done.1 = bf16[2,16,54,128]{3,2,1,0:T(8,128)(2,1)S(1)} collective-permute-done((bf16[2,16,54,128]{3,2,1,0:T(8,128)(2,1)S(1)}, bf16[2,16,54,128]{3,2,1,0:T(8,128)(2,1)S(1)}, u32[]{:S(2)}, u32[]{:S(2)}) %collective-permute-start.1) | collective-permute-done | bytes 442400 | tf_op jit(solution)/shard_map/ppermute | solution.py:21
  47.7 1.8 %add_multiply_fusion = f32[2,4,8,8,128]{4,0,3,2,1:T(2,128)S(1)} fusion(bf16[3,3,3,128,128]{4,3,2,1,0:T(8,128)(2,1)S(1)} %reshape_reshape.6, f32[2,8,128]{2,0,1:T(2,128)S(1)} %get-tuple-element.23, f32[2,4,8,128]{3,0,2,1:T(2,128)S(1)} %broadcast_add_fusion, bf16[2,4,8,8,128]{4,3,2,1,0:T(8,128)(2,1)S(1)} %bitcast.61), kind=kOutput, calls=%fused_computation.50 | convolution fusion | flops 317784064 | bytes 1318912 | tf_op jit(solution)/shard_map/conv_general_dilated | solution.py:81
  49.5 1.7 %fusion = bf16[2,4,8,8,128]{4,0,3,2,1:T(2,128)(2,1)S(1)} fusion(bf16[3,3,3,128,128]{4,3,2,1,0:T(8,128)(2,1)S(1)} %reshape_reshape.6, pred[]{:T(512)S(6)} %eq.37, f32[2,4,8,8,128]{4,0,3,2,1:T(2,128)S(1)} %add_multiply_fusion, bf16[2,4,8,8,128]{4,3,2,1,0:T(8,128)(2,1)S(1)} %copy-done.1), kind=kOutput, calls=%fused_computation.10 | convolution fusion | flops 317718528 | bytes 1409025 | tf_op jit(solution)/shard_map/conv_general_dilated | solution.py:90
  51.9 1.8 %fusion.1 = bf16[2,4,8,8,128]{4,0,3,2,1:T(2,128)(2,1)S(1)} fusion(bf16[3,3,3,128,128]{4,3,2,1,0:T(8,128)(2,1)S(1)} %reshape_reshape.6, f32[2,4,8,8,128]{4,0,3,2,1:T(2,128)S(1)} %add_multiply_fusion, bf16[2,4,8,8,128]{4,0,3,2,1:T(2,128)(2,1)S(1)} %collective-permute-done.2, pred[]{:T(512)S(6)} %eq.37, bf16[2,4,8,8,128]{4,3,2,1,0:T(8,128)(2,1)S(1)} %copy-done.1), kind=kOutput, calls=%fused_computation.11 | convolution fusion | flops 317718528 | bytes 1540097 | tf_op jit(solution)/shard_map/conv_general_dilated | solution.py:90
  54.4 1.8 %fusion.2 = bf16[2,4,8,8,128]{4,0,3,2,1:T(2,128)(2,1)S(1)} fusion(bf16[3,3,3,128,128]{4,3,2,1,0:T(8,128)(2,1)S(1)} %reshape_reshape.6, f32[2,4,8,8,128]{4,0,3,2,1:T(2,128)S(1)} %add_multiply_fusion, bf16[2,4,8,8,128]{4,0,3,2,1:T(2,128)(2,1)S(1)} %collective-permute-done.3, pred[]{:T(512)S(6)} %eq.37, bf16[2,4,8,8,128]{4,3,2,1,0:T(8,128)(2,1)S(1)} %copy-done.1), kind=kOutput, calls=%fused_computation.12 | convolution fusion | flops 317718528 | bytes 1540097 | tf_op jit(solution)/shard_map/conv_general_dilated | solution.py:90
  56.8 1.8 %fusion.3 = bf16[2,4,8,8,128]{4,0,3,2,1:T(2,128)(2,1)S(1)} fusion(bf16[3,3,3,128,128]{4,3,2,1,0:T(8,128)(2,1)S(1)} %reshape_reshape.6, f32[2,4,8,8,128]{4,0,3,2,1:T(2,128)S(1)} %add_multiply_fusion, bf16[2,4,8,8,128]{4,0,3,2,1:T(2,128)(2,1)S(1)} %collective-permute-done.4, pred[]{:T(512)S(6)} %eq.37, bf16[2,4,8,8,128]{4,3,2,1,0:T(8,128)(2,1)S(1)} %copy-done.1), kind=kOutput, calls=%fused_computation.13 | convolution fusion | flops 317718528 | bytes 1540097 | tf_op jit(solution)/shard_map/conv_general_dilated | solution.py:90
  59.5 1.8 %fusion.4 = bf16[2,4,8,8,128]{4,0,3,2,1:T(2,128)(2,1)S(1)} fusion(bf16[3,3,3,128,128]{4,3,2,1,0:T(8,128)(2,1)S(1)} %reshape_reshape.6, f32[2,4,8,8,128]{4,0,3,2,1:T(2,128)S(1)} %add_multiply_fusion, bf16[2,4,8,8,128]{4,0,3,2,1:T(2,128)(2,1)S(1)} %collective-permute-done.5, pred[]{:T(512)S(6)} %eq.37, bf16[2,4,8,8,128]{4,3,2,1,0:T(8,128)(2,1)S(1)} %copy-done.1), kind=kOutput, calls=%fused_computation.14 | convolution fusion | flops 317718528 | bytes 1540097 | tf_op jit(solution)/shard_map/conv_general_dilated | solution.py:90
  61.9 1.8 %fusion.5 = bf16[2,4,8,8,128]{4,0,3,2,1:T(2,128)(2,1)S(1)} fusion(bf16[3,3,3,128,128]{4,3,2,1,0:T(8,128)(2,1)S(1)} %reshape_reshape.6, f32[2,4,8,8,128]{4,0,3,2,1:T(2,128)S(1)} %add_multiply_fusion, bf16[2,4,8,8,128]{4,0,3,2,1:T(2,128)(2,1)S(1)} %collective-permute-done.6, pred[]{:T(512)S(6)} %eq.37, bf16[2,4,8,8,128]{4,3,2,1,0:T(8,128)(2,1)S(1)} %copy-done.1), kind=kOutput, calls=%fused_computation.15 | convolution fusion | flops 317718528 | bytes 1540097 | tf_op jit(solution)/shard_map/conv_general_dilated | solution.py:90
  64.4 1.8 %fusion.6 = bf16[2,4,8,8,128]{4,0,3,2,1:T(2,128)(2,1)S(1)} fusion(bf16[3,3,3,128,128]{4,3,2,1,0:T(8,128)(2,1)S(1)} %reshape_reshape.6, f32[2,4,8,8,128]{4,0,3,2,1:T(2,128)S(1)} %add_multiply_fusion, bf16[2,4,8,8,128]{4,0,3,2,1:T(2,128)(2,1)S(1)} %collective-permute-done.7, pred[]{:T(512)S(6)} %eq.37, bf16[2,4,8,8,128]{4,3,2,1,0:T(8,128)(2,1)S(1)} %copy-done.1), kind=kOutput, calls=%fused_computation.16 | convolution fusion | flops 317718528 | bytes 1540097 | tf_op jit(solution)/shard_map/conv_general_dilated | solution.py:90
  67.5 37.4 %collective-permute-done.8 = bf16[2,4,8,8,128]{4,0,3,2,1:T(2,128)(2,1)S(1)} collective-permute-done((bf16[2,4,8,8,128]{4,0,3,2,1:T(2,128)(2,1)S(1)}, bf16[2,4,8,8,128]{4,0,3,2,1:T(2,128)(2,1)S(1)}, u32[]{:S(2)}, u32[]{:S(2)}) %collective-permute-start.8) | collective-permute-done | bytes 131104 | tf_op jit(solution)/shard_map/ppermute | solution.py:146
  104.9 3.5 %convolution_multiply_fusion = f32[3,3,3,128,128]{4,3,2,1,0:T(8,128)S(1)} fusion(pred[]{:T(512)S(6)} %eq.36, pred[]{:T(512)S(6)} %eq.40, pred[]{:T(512)S(6)} %eq.41, pred[]{:T(512)S(6)} %eq.42, pred[]{:T(512)S(6)} %eq.43, pred[]{:T(512)S(6)} %eq.44, pred[]{:T(512)S(6)} %eq.45, pred[]{:T(512)S(6)} %eq.37, bf16[2,4,8,8,128]{4,3,2,1,0:T(8,128)(2,1)S(1)} %bitcast.62, ...), kind=kOutput, calls=%fused_computation | convolution fusion | flops 320258048 | bytes 3211272 | tf_op jit(solution)/shard_map/conv_general_dilated | solution.py:98
  108.9 1.9 %collective-permute-start.9 = (bf16[2,8,2,54,128]{4,1,3,2,0:T(8,128)(2,1)S(1)}, bf16[2,8,2,54,128]{4,1,3,2,0:T(8,128)(2,1)S(1)}, u32[]{:S(2)}, u32[]{:S(2)}) collective-permute-start(bf16[2,8,2,54,128]{4,1,3,2,0:T(8,128)(2,1)S(1)} %pad_maximum_fusion.1), channel_id=1, source_target_pairs={{0,1},{1,0},{2,3},{3,2},{4,5},{5,4},{6,7},{7,6},{8,9},{9,8},{10,11... | collective-permute-start | bytes 1327112 | tf_op jit(solution)/shard_map/ppermute | solution.py:21
  111.1 1.4 collective-permute-done.9
  113.2 2.6 %collective-permute-start.10 = (bf16[16,54,128]{2,0,1:T(8,128)(2,1)S(1)}, bf16[16,54,128]{2,0,1:T(8,128)(2,1)S(1)}, u32[]{:S(2)}, u32[]{:S(2)}) collective-permute-start(bf16[16,54,128]{2,0,1:T(8,128)(2,1)S(1)} %fusion.21), channel_id=1, source_target_pairs={{0,32},{1,33},{2,34},{3,35},{4,36},{5,37},{6,38},{7,39},{8,40},{9,... | collective-permute-start | bytes 663560 | tf_op jit(solution)/shard_map/ppermute | solution.py:21
  115.8 6.8 %collective-permute-done.10 = bf16[16,54,128]{2,0,1:T(8,128)(2,1)S(1)} collective-permute-done((bf16[16,54,128]{2,0,1:T(8,128)(2,1)S(1)}, bf16[16,54,128]{2,0,1:T(8,128)(2,1)S(1)}, u32[]{:S(2)}, u32[]{:S(2)}) %collective-permute-start.10) | collective-permute-done | bytes 221216 | tf_op jit(solution)/shard_map/ppermute | solution.py:21
  123.4 6.3 %all-to-all-start.1 = ((bf16[16,54,128]{2,1,0:T(8,128)(2,1)}), bf16[16,54,128]{2,1,0:T(8,128)(2,1)S(1)}, u32[]{:S(2)}, u32[]{:S(2)}) async-start(bf16[16,54,128]{2,1,0:T(8,128)(2,1)} %copy.90), calls=%async_computation.1 | async-start | bytes 458752 | tf_op jit(solution)/shard_map/all_to_all | solution.py:76
  129.7 2.3 %fusion.9 = bf16[1,2,4,8,8,128]{5,1,4,3,2,0:T(2,128)(2,1)S(1)} fusion(bf16[3,3,3,128,128]{4,3,2,1,0:T(8,128)(2,1)S(1)} %reshape_reshape.6, pred[]{:T(512)S(6)} %eq.36, bf16[2,4,8,8,128]{4,0,3,2,1:T(2,128)(2,1)S(1)} %fusion.6, pred[]{:T(512)S(6)} %eq.40, bf16[2,4,8,8,128]{4,0,3,2,1:T(2,128)(2,1)S(1)} %fusion.5, pred[]{:T(512)S(6)} %eq.41, ...), kind=kOutput, calls=%fused_computation.19 | convolution fusion | flops 318242816 | bytes 2457608 | tf_op jit(solution)/shard_map/conv_general_dilated | solution.py:90
  132.7 13.8 %all-to-all-done.1 = bf16[16,54,128]{2,1,0:T(8,128)(2,1)S(1)} async-done(((bf16[16,54,128]{2,1,0:T(8,128)(2,1)}), bf16[16,54,128]{2,1,0:T(8,128)(2,1)S(1)}, u32[]{:S(2)}, u32[]{:S(2)}) %all-to-all-start.1) | async-done | bytes 221216 | tf_op jit(solution)/shard_map/all_to_all | solution.py:76
  (52 shorter events, 12.0 us)
Async XLA Ops:
  2.1 32.1 %all-to-all-start = ((bf16[16,54,128]{2,1,0:T(8,128)(2,1)}), bf16[16,54,128]{2,1,0:T(8,128)(2,1)S(1)}, u32[]{:S(2)}, u32[]{:S(2)}) async-start(bf16[16,54,128]{2,1,0:T(8,128)(2,1)} %broadcast_in_dim.11), calls=%async_computation | async-start | bytes 458752 | tf_op jit(solution)/shard_map/all_to_all | solution.py:31
  34.2 8.7 %collective-permute-start = (bf16[16,54,128]{2,1,0:T(8,128)(2,1)S(1)}, bf16[16,54,128]{2,1,0:T(8,128)(2,1)S(1)}, u32[]{:S(2)}, u32[]{:S(2)}) collective-permute-start(bf16[16,54,128]{2,1,0:T(8,128)(2,1)S(1)} %all-to-all-done), channel_id=1, source_target_pairs={{0,32},{1,33},{2,34},{3,35},{4,36},{5,37},{6,38},{7,39},{8,40},{9,... | collective-permute-start | bytes 663560 | tf_op jit(solution)/shard_map/ppermute | solution.py:21
  43.0 3.7 %collective-permute-start.1 = (bf16[2,16,54,128]{3,2,1,0:T(8,128)(2,1)S(1)}, bf16[2,16,54,128]{3,2,1,0:T(8,128)(2,1)S(1)}, u32[]{:S(2)}, u32[]{:S(2)}) collective-permute-start(bf16[2,16,54,128]{3,2,1,0:T(8,128)(2,1)S(1)} %pad_maximum_fusion), channel_id=1, source_target_pairs={{0,1},{1,0},{2,3},{3,2},{4,5},{5,4},{6,7},{7,6},{8,9},{9,8},{10,11... | collective-permute-start | bytes 1327112 | tf_op jit(solution)/shard_map/ppermute | solution.py:21
  46.8 0.9 copy-start
  47.7 1.8 %copy-start.1 = (bf16[2,4,8,8,128]{4,3,2,1,0:T(8,128)(2,1)S(1)}, bf16[2,4,8,8,128]{4,3,2,1,0:T(8,128)(2,1)}, u32[]{:S(2)}) copy-start(bf16[2,4,8,8,128]{4,3,2,1,0:T(8,128)(2,1)} %param.9) | copy-start | bytes 393220
  49.5 55.4 %copy-start.2 = (f32[2,4,8,8,128]{4,0,3,2,1:T(2,128)}, f32[2,4,8,8,128]{4,0,3,2,1:T(2,128)S(1)}, u32[]{:S(2)}) copy-start(f32[2,4,8,8,128]{4,0,3,2,1:T(2,128)S(1)} %add_multiply_fusion) | copy-start | bytes 786436
  51.2 0.7 collective-permute-start.2
  53.7 0.7 collective-permute-start.3
  56.1 0.7 collective-permute-start.4
  58.6 0.9 collective-permute-start.5
  61.2 0.7 collective-permute-start.6
  63.7 0.7 collective-permute-start.7
  66.2 38.7 %collective-permute-start.8 = (bf16[2,4,8,8,128]{4,0,3,2,1:T(2,128)(2,1)S(1)}, bf16[2,4,8,8,128]{4,0,3,2,1:T(2,128)(2,1)S(1)}, u32[]{:S(2)}, u32[]{:S(2)}) collective-permute-start(bf16[2,4,8,8,128]{4,0,3,2,1:T(2,128)(2,1)S(1)} %fusion.6), channel_id=1, source_target_pairs={{64,0},{65,1},{66,2},{67,3},{68,4},{69,5},{70,6},{71,7},{72,8},{73... | collective-permute-start | bytes 393224 | tf_op jit(solution)/shard_map/ppermute | solution.py:146
  108.9 3.7 %collective-permute-start.9 = (bf16[2,8,2,54,128]{4,1,3,2,0:T(8,128)(2,1)S(1)}, bf16[2,8,2,54,128]{4,1,3,2,0:T(8,128)(2,1)S(1)}, u32[]{:S(2)}, u32[]{:S(2)}) collective-permute-start(bf16[2,8,2,54,128]{4,1,3,2,0:T(8,128)(2,1)S(1)} %pad_maximum_fusion.1), channel_id=1, source_target_pairs={{0,1},{1,0},{2,3},{3,2},{4,5},{5,4},{6,7},{7,6},{8,9},{9,8},{10,11... | collective-permute-start | bytes 1327112 | tf_op jit(solution)/shard_map/ppermute | solution.py:21
  113.2 9.4 %collective-permute-start.10 = (bf16[16,54,128]{2,0,1:T(8,128)(2,1)S(1)}, bf16[16,54,128]{2,0,1:T(8,128)(2,1)S(1)}, u32[]{:S(2)}, u32[]{:S(2)}) collective-permute-start(bf16[16,54,128]{2,0,1:T(8,128)(2,1)S(1)} %fusion.21), channel_id=1, source_target_pairs={{0,32},{1,33},{2,34},{3,35},{4,36},{5,37},{6,38},{7,39},{8,40},{9,... | collective-permute-start | bytes 663560 | tf_op jit(solution)/shard_map/ppermute | solution.py:21
  122.6 7.1 %copy-start.3 = (f32[2,4,8,8,128]{4,0,3,2,1:T(2,128)S(1)}, f32[2,4,8,8,128]{4,0,3,2,1:T(2,128)}, u32[]{:S(2)}) copy-start(f32[2,4,8,8,128]{4,0,3,2,1:T(2,128)} %copy-done.2) | copy-start | bytes 786436
  123.4 23.1 %all-to-all-start.1 = ((bf16[16,54,128]{2,1,0:T(8,128)(2,1)}), bf16[16,54,128]{2,1,0:T(8,128)(2,1)S(1)}, u32[]{:S(2)}, u32[]{:S(2)}) async-start(bf16[16,54,128]{2,1,0:T(8,128)(2,1)} %copy.90), calls=%async_computation.1 | async-start | bytes 458752 | tf_op jit(solution)/shard_map/all_to_all | solution.py:76

commit v12 on v11

--- a/solution.py
+++ b/solution.py
@@ -131,19 +131,25 @@
     silu_slope = sigmoid_h * (1.0 + pre_act * (1.0 - sigmoid_h))
 
     is_top = segment_index == segments - 1
-    incoming = jnp.zeros(top_grad.shape, jnp.bfloat16)
-    grads_held = jnp.zeros(top_grad.shape, jnp.bfloat16)
-    slope_held = jnp.zeros(top_grad.shape, jnp.bfloat16)
+    micro_shape = top_grad.shape[1:]
+    incoming = [jnp.zeros(micro_shape, jnp.bfloat16) for _ in range(micro_count)]
+    grads_held = [jnp.zeros(micro_shape, jnp.bfloat16) for _ in range(micro_count)]
+    slopes_held = [jnp.zeros(micro_shape, jnp.bfloat16) for _ in range(micro_count)]
     for tick in range(segments):
-        cotangent = jnp.where(is_top, top_grad, incoming).astype(jnp.float32)
-        slope = (cotangent * silu_slope).astype(jnp.bfloat16)
-        down_grad = (cotangent + conv_transposed(slope, kernel)).astype(jnp.bfloat16)
         mine = segment_index == segments - 1 - tick
-        grads_held = jnp.where(mine, down_grad, grads_held)
-        slope_held = jnp.where(mine, slope, slope_held)
-        if tick + 1 < segments:
-            sender = segments - 1 - tick
-            incoming = lax.ppermute(down_grad, "segment", [(sender, sender - 1)])
+        arriving = []
+        for micro in range(micro_count):
+            cotangent = jnp.where(is_top, top_grad[micro], incoming[micro]).astype(jnp.float32)
+            slope = (cotangent * silu_slope[micro]).astype(jnp.bfloat16)
+            down_grad = (cotangent + conv_transposed(slope[None], kernel)[0]).astype(jnp.bfloat16)
+            grads_held[micro] = jnp.where(mine, down_grad, grads_held[micro])
+            slopes_held[micro] = jnp.where(mine, slope, slopes_held[micro])
+            if tick + 1 < segments:
+                sender = segments - 1 - tick
+                arriving.append(lax.ppermute(down_grad, "segment", [(sender, sender - 1)]))
+        incoming = arriving
+    grads_held = jnp.stack(grads_held)
+    slope_held = jnp.stack(slopes_held)
 
     scale_factor = 1.0 / math.sqrt(dp_count * micro_count * cell_count)
     grad_term = conv_kernel_grad(fields, slope_held) * scale_factor

time: 148 us -> 165 us (1.11)
  matrix products: 19.9 us -> 25.4 us
  starting transfers between devices: 36.9 us -> 42.4 us
  waiting for transfers between devices: 81.3 us -> 86.3 us
  other arithmetic: 1.32 us -> 3.29 us
    conv_general_dilated x8 -> x16, matrix products: 14.6 us -> 21.7 us  [conv_transposed(): lax.conv_general_dilated(slope, flipped, (1, 1, 1), [(1, 1)] * 3, dimensi...]
    ppermute x7 -> x14, starting transfers between devices: 5.49 us -> 11 us  [local(): arriving.append(lax.ppermute(down_grad, 'segment', [(sender, sender - 1)]))]
    ppermute x7 -> x14, waiting for transfers between devices: 37.4 us -> 41.4 us  [local(): arriving.append(lax.ppermute(down_grad, 'segment', [(sender, sender - 1)]))]
  transfers between devices with their start and end apart: 13 -> 20, of which waited for: 7 -> 8; matrix products, arithmetic and copies ran while one was open for 4% -> 4% of each run, Pallas kernels for 0% -> 0%
where the time goes in v12:
time: 165 us; the launch traced here: 164 us
  waiting for transfers between devices  86.3 us (52%)
  starting transfers between devices  42.4 us (26%)
  matrix products  25.4 us (15%)
  local copies, waits for them, and re-layouts  5.69 us (3%)
  other arithmetic  3.29 us (2%)
    ppermute x14, waiting for transfers between devices, local(): arriving.append(lax.ppermute(down_grad, 'segment', [(sender, sender - 1)]))  41.4 us
    conv_general_dilated x16, matrix products, conv_transposed(): lax.conv_general_dilated(slope, flipped, (1, 1, 1), [(1, 1)] * 3, dimensi...  21.7 us
    all_to_all x1, waiting for transfers between devices, gather_by_halves(): lax.all_to_all(jnp.broadcast_to(block, (ring,) + block.shape), ring_axis,...  15.2 us
    all_to_all x1, starting transfers between devices, gather_by_halves(): lax.all_to_all(jnp.broadcast_to(block, (ring,) + block.shape), ring_axis,...  15.2 us
    ppermute x4, waiting for transfers between devices, exchanged(): return lax.ppermute(array, axis, [(i, i ^ mask) for i in range(length)])  15.1 us
    all_to_all x1, waiting for transfers between devices, reduce_in_blocks(): received = lax.all_to_all(held, ring_axis, 0, 0, tiled=True)  14.6 us
    ppermute x14, starting transfers between devices, local(): arriving.append(lax.ppermute(down_grad, 'segment', [(sender, sender - 1)]))  11 us
    ppermute x4, starting transfers between devices, exchanged(): return lax.ppermute(array, axis, [(i, i ^ mask) for i in range(length)])  9.91 us
  transfers between devices with their start and end apart: 20, of which 8 were waited for; matrix products, arithmetic and copies ran while one was open for 4% of the time, Pallas kernels for 0%

profile of v12, /device:TPU:32, one launch (start us, length us, event | category | flops | bytes accessed | tf_op | source)
XLA Modules:
  0.0 164.5 jit_solution(14239884920244979707)
XLA Ops:
  0.6 1.4 broadcast_in_dim.55
  2.1 15.2 %all-to-all-start = ((bf16[16,54,128]{2,1,0:T(8,128)(2,1)}), bf16[16,54,128]{2,1,0:T(8,128)(2,1)S(1)}, u32[]{:S(2)}, u32[]{:S(2)}) async-start(bf16[16,54,128]{2,1,0:T(8,128)(2,1)} %broadcast_in_dim.55), calls=%async_computation | async-start | bytes 458752 | tf_op jit(solution)/shard_map/all_to_all | solution.py:31
  19.0 15.2 %all-to-all-done = bf16[16,54,128]{2,1,0:T(8,128)(2,1)S(1)} async-done(((bf16[16,54,128]{2,1,0:T(8,128)(2,1)}), bf16[16,54,128]{2,1,0:T(8,128)(2,1)S(1)}, u32[]{:S(2)}, u32[]{:S(2)}) %all-to-all-start) | async-done | bytes 221216 | tf_op jit(solution)/shard_map/all_to_all | solution.py:31
  34.2 3.5 %collective-permute-start = (bf16[16,54,128]{2,1,0:T(8,128)(2,1)S(1)}, bf16[16,54,128]{2,1,0:T(8,128)(2,1)S(1)}, u32[]{:S(2)}, u32[]{:S(2)}) collective-permute-start(bf16[16,54,128]{2,1,0:T(8,128)(2,1)S(1)} %all-to-all-done), channel_id=1, source_target_pairs={{0,32},{1,33},{2,34},{3,35},{4,36},{5,37},{6,38},{7,39},{8,40},{9,... | collective-permute-start | bytes 663560 | tf_op jit(solution)/shard_map/ppermute | solution.py:21
  37.7 5.2 %collective-permute-done = bf16[16,54,128]{2,1,0:T(8,128)(2,1)S(1)} collective-permute-done((bf16[16,54,128]{2,1,0:T(8,128)(2,1)S(1)}, bf16[16,54,128]{2,1,0:T(8,128)(2,1)S(1)}, u32[]{:S(2)}, u32[]{:S(2)}) %collective-permute-start) | collective-permute-done | bytes 221216 | tf_op jit(solution)/shard_map/ppermute | solution.py:21
  43.0 1.9 %collective-permute-start.1 = (bf16[2,16,54,128]{3,2,1,0:T(8,128)(2,1)S(1)}, bf16[2,16,54,128]{3,2,1,0:T(8,128)(2,1)S(1)}, u32[]{:S(2)}, u32[]{:S(2)}) collective-permute-start(bf16[2,16,54,128]{3,2,1,0:T(8,128)(2,1)S(1)} %pad_maximum_fusion), channel_id=1, source_target_pairs={{0,1},{1,0},{2,3},{3,2},{4,5},{5,4},{6,7},{7,6},{8,9},{9,8},{10,11... | collective-permute-start | bytes 1327112 | tf_op jit(solution)/shard_map/ppermute | solution.py:21
  45.0 1.7 %collective-permute-done.1 = bf16[2,16,54,128]{3,2,1,0:T(8,128)(2,1)S(1)} collective-permute-done((bf16[2,16,54,128]{3,2,1,0:T(8,128)(2,1)S(1)}, bf16[2,16,54,128]{3,2,1,0:T(8,128)(2,1)S(1)}, u32[]{:S(2)}, u32[]{:S(2)}) %collective-permute-start.1) | collective-permute-done | bytes 442400 | tf_op jit(solution)/shard_map/ppermute | solution.py:21
  47.7 1.5 fusion.70
  51.4 1.4 fusion.65
  57.8 1.4 fusion.59
  59.9 1.4 fusion.57
  67.0 29.9 %collective-permute-done.8 = bf16[4,8,8,128]{3,2,1,0:T(8,128)(2,1)S(1)} collective-permute-done((bf16[4,8,8,128]{3,2,1,0:T(8,128)(2,1)S(1)}, bf16[4,8,8,128]{3,2,1,0:T(8,128)(2,1)S(1)}, u32[]{:S(2)}, u32[]{:S(2)}) %collective-permute-start.8) | collective-permute-done | bytes 65568 | tf_op jit(solution)/shard_map/ppermute | solution.py:149
  99.0 1.4 fusion.47
  101.1 1.4 fusion.45
  107.7 1.4 fusion.53
  112.0 11.4 %collective-permute-done.15 = bf16[4,8,8,128]{3,2,1,0:T(8,128)(2,1)S(1)} collective-permute-done((bf16[4,8,8,128]{3,2,1,0:T(8,128)(2,1)S(1)}, bf16[4,8,8,128]{3,2,1,0:T(8,128)(2,1)S(1)}, u32[]{:S(2)}, u32[]{:S(2)}) %collective-permute-start.15) | collective-permute-done | bytes 65568 | tf_op jit(solution)/shard_map/ppermute | solution.py:149
  123.6 2.3 %convolution_multiply_fusion = f32[3,3,3,128,128]{4,3,2,1,0:T(8,128)S(1)} fusion(bf16[2,4,8,8,128]{4,3,2,1,0:T(8,128)(2,1)S(1)} %pad_maximum_fusion.2, bf16[2,4,8,8,128]{4,3,2,1,0:T(8,128)(2,1)S(1)} %bitcast.369), kind=kOutput, calls=%fused_computation | convolution fusion | flops 317636608 | bytes 2031616 | tf_op jit(solution)/shard_map/conv_general_dilated | solution.py:98
  126.3 1.9 %collective-permute-start.16 = (bf16[2,8,2,54,128]{4,1,3,2,0:T(8,128)(2,1)S(1)}, bf16[2,8,2,54,128]{4,1,3,2,0:T(8,128)(2,1)S(1)}, u32[]{:S(2)}, u32[]{:S(2)}) collective-permute-start(bf16[2,8,2,54,128]{4,1,3,2,0:T(8,128)(2,1)S(1)} %pad_maximum_fusion.1), channel_id=1, source_target_pairs={{0,1},{1,0},{2,3},{3,2},{4,5},{5,4},{6,7},{7,6},{8,9},{9,8},{10,11... | collective-permute-start | bytes 1327112 | tf_op jit(solution)/shard_map/ppermute | solution.py:21
  128.5 1.4 collective-permute-done.16
  130.6 2.6 %collective-permute-start.17 = (bf16[16,54,128]{2,0,1:T(8,128)(2,1)S(1)}, bf16[16,54,128]{2,0,1:T(8,128)(2,1)S(1)}, u32[]{:S(2)}, u32[]{:S(2)}) collective-permute-start(bf16[16,54,128]{2,0,1:T(8,128)(2,1)S(1)} %fusion.3), channel_id=1, source_target_pairs={{0,32},{1,33},{2,34},{3,35},{4,36},{5,37},{6,38},{7,39},{8,40},{9,... | collective-permute-start | bytes 663560 | tf_op jit(solution)/shard_map/ppermute | solution.py:21
  133.2 6.7 %collective-permute-done.17 = bf16[16,54,128]{2,0,1:T(8,128)(2,1)S(1)} collective-permute-done((bf16[16,54,128]{2,0,1:T(8,128)(2,1)S(1)}, bf16[16,54,128]{2,0,1:T(8,128)(2,1)S(1)}, u32[]{:S(2)}, u32[]{:S(2)}) %collective-permute-start.17) | collective-permute-done | bytes 221216 | tf_op jit(solution)/shard_map/ppermute | solution.py:21
  140.8 6.3 %all-to-all-start.1 = ((bf16[16,54,128]{2,1,0:T(8,128)(2,1)}), bf16[16,54,128]{2,1,0:T(8,128)(2,1)S(1)}, u32[]{:S(2)}, u32[]{:S(2)}) async-start(bf16[16,54,128]{2,1,0:T(8,128)(2,1)} %copy.161), calls=%async_computation.1 | async-start | bytes 458752 | tf_op jit(solution)/shard_map/all_to_all | solution.py:76
  147.1 1.4 fusion.37
  149.2 14.6 %all-to-all-done.1 = bf16[16,54,128]{2,1,0:T(8,128)(2,1)S(1)} async-done(((bf16[16,54,128]{2,1,0:T(8,128)(2,1)}), bf16[16,54,128]{2,1,0:T(8,128)(2,1)S(1)}, u32[]{:S(2)}, u32[]{:S(2)}) %all-to-all-start.1) | async-done | bytes 221216 | tf_op jit(solution)/shard_map/all_to_all | solution.py:76
  (100 shorter events, 30.7 us)
Async XLA Ops:
  2.1 32.1 %all-to-all-start = ((bf16[16,54,128]{2,1,0:T(8,128)(2,1)}), bf16[16,54,128]{2,1,0:T(8,128)(2,1)S(1)}, u32[]{:S(2)}, u32[]{:S(2)}) async-start(bf16[16,54,128]{2,1,0:T(8,128)(2,1)} %broadcast_in_dim.55), calls=%async_computation | async-start | bytes 458752 | tf_op jit(solution)/shard_map/all_to_all | solution.py:31
  34.2 8.7 %collective-permute-start = (bf16[16,54,128]{2,1,0:T(8,128)(2,1)S(1)}, bf16[16,54,128]{2,1,0:T(8,128)(2,1)S(1)}, u32[]{:S(2)}, u32[]{:S(2)}) collective-permute-start(bf16[16,54,128]{2,1,0:T(8,128)(2,1)S(1)} %all-to-all-done), channel_id=1, source_target_pairs={{0,32},{1,33},{2,34},{3,35},{4,36},{5,37},{6,38},{7,39},{8,40},{9,... | collective-permute-start | bytes 663560 | tf_op jit(solution)/shard_map/ppermute | solution.py:21
  43.0 3.7 %collective-permute-start.1 = (bf16[2,16,54,128]{3,2,1,0:T(8,128)(2,1)S(1)}, bf16[2,16,54,128]{3,2,1,0:T(8,128)(2,1)S(1)}, u32[]{:S(2)}, u32[]{:S(2)}) collective-permute-start(bf16[2,16,54,128]{3,2,1,0:T(8,128)(2,1)S(1)} %pad_maximum_fusion), channel_id=1, source_target_pairs={{0,1},{1,0},{2,3},{3,2},{4,5},{5,4},{6,7},{7,6},{8,9},{9,8},{10,11... | collective-permute-start | bytes 1327112 | tf_op jit(solution)/shard_map/ppermute | solution.py:21
  46.8 0.9 copy-start.1
  47.1 2.1 %copy-start = (bf16[2,4,8,8,128]{4,3,2,1,0:T(8,128)(2,1)S(1)}, bf16[2,4,8,8,128]{4,3,2,1,0:T(8,128)(2,1)}, u32[]{:S(2)}) copy-start(bf16[2,4,8,8,128]{4,3,2,1,0:T(8,128)(2,1)} %param.9) | copy-start | bytes 393220
  50.7 0.7 collective-permute-start.2
  52.8 0.7 collective-permute-start.3
  55.0 0.7 collective-permute-start.4
  57.1 0.7 collective-permute-start.5
  59.2 0.7 collective-permute-start.6
  61.3 2.2 %collective-permute-start.7 = (bf16[4,8,8,128]{3,2,1,0:T(8,128)(2,1)S(1)}, bf16[4,8,8,128]{3,2,1,0:T(8,128)(2,1)S(1)}, u32[]{:S(2)}, u32[]{:S(2)}) collective-permute-start(bf16[4,8,8,128]{3,2,1,0:T(8,128)(2,1)S(1)} %fusion.15), channel_id=1, source_target_pairs={{128,64},{129,65},{130,66},{131,67},{132,68},{133,69},{134,70},{13... | collective-permute-start | bytes 196616 | tf_op jit(solution)/shard_map/ppermute | solution.py:149
  65.0 31.9 %collective-permute-start.8 = (bf16[4,8,8,128]{3,2,1,0:T(8,128)(2,1)S(1)}, bf16[4,8,8,128]{3,2,1,0:T(8,128)(2,1)S(1)}, u32[]{:S(2)}, u32[]{:S(2)}) collective-permute-start(bf16[4,8,8,128]{3,2,1,0:T(8,128)(2,1)S(1)} %get-tuple-element.14), channel_id=1, source_target_pairs={{64,0},{65,1},{66,2},{67,3},{68,4},{69,5},{70,6},{71,7},{72,8},{73... | collective-permute-start | bytes 196616 | tf_op jit(solution)/shard_map/ppermute | solution.py:149
  66.3 30.6 %collective-permute-start.9 = (bf16[4,8,8,128]{3,2,1,0:T(8,128)(2,1)S(1)}, bf16[4,8,8,128]{3,2,1,0:T(8,128)(2,1)S(1)}, u32[]{:S(2)}, u32[]{:S(2)}) collective-permute-start(bf16[4,8,8,128]{3,2,1,0:T(8,128)(2,1)S(1)} %get-tuple-element.15), channel_id=1, source_target_pairs={{448,384},{449,385},{450,386},{451,387},{452,388},{453,389},{454,3... | collective-permute-start | bytes 196616 | tf_op jit(solution)/shard_map/ppermute | solution.py:149
  98.3 0.7 collective-permute-start.10
  100.4 0.7 collective-permute-start.11
  102.5 0.7 collective-permute-start.12
  104.7 0.7 collective-permute-start.13
  106.8 2.3 %collective-permute-start.14 = (bf16[4,8,8,128]{3,2,1,0:T(8,128)(2,1)S(1)}, bf16[4,8,8,128]{3,2,1,0:T(8,128)(2,1)S(1)}, u32[]{:S(2)}, u32[]{:S(2)}) collective-permute-start(bf16[4,8,8,128]{3,2,1,0:T(8,128)(2,1)S(1)} %fusion.31), channel_id=1, source_target_pairs={{128,64},{129,65},{130,66},{131,67},{132,68},{133,69},{134,70},{13... | collective-permute-start | bytes 196616 | tf_op jit(solution)/shard_map/ppermute | solution.py:149
  110.5 12.9 %collective-permute-start.15 = (bf16[4,8,8,128]{3,2,1,0:T(8,128)(2,1)S(1)}, bf16[4,8,8,128]{3,2,1,0:T(8,128)(2,1)S(1)}, u32[]{:S(2)}, u32[]{:S(2)}) collective-permute-start(bf16[4,8,8,128]{3,2,1,0:T(8,128)(2,1)S(1)} %fusion.33), channel_id=1, source_target_pairs={{64,0},{65,1},{66,2},{67,3},{68,4},{69,5},{70,6},{71,7},{72,8},{73... | collective-permute-start | bytes 196616 | tf_op jit(solution)/shard_map/ppermute | solution.py:149
  126.3 3.7 %collective-permute-start.16 = (bf16[2,8,2,54,128]{4,1,3,2,0:T(8,128)(2,1)S(1)}, bf16[2,8,2,54,128]{4,1,3,2,0:T(8,128)(2,1)S(1)}, u32[]{:S(2)}, u32[]{:S(2)}) collective-permute-start(bf16[2,8,2,54,128]{4,1,3,2,0:T(8,128)(2,1)S(1)} %pad_maximum_fusion.1), channel_id=1, source_target_pairs={{0,1},{1,0},{2,3},{3,2},{4,5},{5,4},{6,7},{7,6},{8,9},{9,8},{10,11... | collective-permute-start | bytes 1327112 | tf_op jit(solution)/shard_map/ppermute | solution.py:21
  130.6 9.4 %collective-permute-start.17 = (bf16[16,54,128]{2,0,1:T(8,128)(2,1)S(1)}, bf16[16,54,128]{2,0,1:T(8,128)(2,1)S(1)}, u32[]{:S(2)}, u32[]{:S(2)}) collective-permute-start(bf16[16,54,128]{2,0,1:T(8,128)(2,1)S(1)} %fusion.3), channel_id=1, source_target_pairs={{0,32},{1,33},{2,34},{3,35},{4,36},{5,37},{6,38},{7,39},{8,40},{9,... | collective-permute-start | bytes 663560 | tf_op jit(solution)/shard_map/ppermute | solution.py:21
  140.8 23.1 %all-to-all-start.1 = ((bf16[16,54,128]{2,1,0:T(8,128)(2,1)}), bf16[16,54,128]{2,1,0:T(8,128)(2,1)S(1)}, u32[]{:S(2)}, u32[]{:S(2)}) async-start(bf16[16,54,128]{2,1,0:T(8,128)(2,1)} %copy.161), calls=%async_computation.1 | async-start | bytes 458752 | tf_op jit(solution)/shard_map/all_to_all | solution.py:76
